TPU v7x, 128 devices: a whole 4x4x4 slice. The times are simulated.
128 devices in a mesh: row: 8 (over x, core), col: 16 (over y, z).
Axes of the slice: x: 4, y: 4, z: 4, core: 2. Of those that a mesh axis runs over, the one named last changes fastest.
Arguments:
- front: float32 [8, 8, 4, 16, 256, 256], P(None, 'row', None, 'col'), as said below
- tile_live: int32 [60], replicated, may hold values 0 or 1
- row_target: int32 [60], replicated, may hold values from 0 to 63, as said below
- col_target: int32 [60], replicated, may hold values from 0 to 63, as said below
Outputs:
- panel_factor: float32 [8, 8, 256, 1024], P(None, 'row')
- parent_update: float32 [8, 8, 4, 16, 256, 256], P(None, 'row', None, 'col')
Inputs may be any that keep to these rules, and one draw needn't show every extreme that they name: `front`: the leading 4 * 256 rows and columns, upper triangle taken from the lower, form a symmetric positive definite matrix whose eigenvalues are 0.1 or more. `row_target`: Distinct. The update tile rows m with m + 4 congruent to r mod 8 go at most 1 to positions of any one residue mod 8, and exactly 1 for some r and residue. `col_target`: Distinct, and col_target[m] mod 16 equals (m + 4) mod 16.
All inputs are finite; a program needn't handle non-finite values.
Results may differ from a plain program's by a relative error of at most 0.000098.
Values sent between devices are 32-bit elements; how exact they have to be, the bound alone decides.
No kernel may reach another device: no remote copies, remote signals or barrier semaphores. Data moves between devices by JAX's collectives and lax.ppermute only.
A program may use at most 192 MiB of HBM per device.

v0:
```python
import jax
import jax.numpy as jnp
from jax import lax
from jax.sharding import PartitionSpec as P

NT = 64
PANEL_TILES = 2
PANELS = 2
LEAD = 4


PRECISE = lax.Precision.HIGHEST


def broadcast(block, axis, owner):
    block = jnp.where(lax.axis_index(axis) == owner, block, jnp.zeros_like(block))
    return lax.psum(block, axis)


def symmetric_lower(block_now):
    return jnp.tril(block_now) + jnp.tril(block_now, -1).T


def valid_gain(valid_flags, ndims):
    return valid_flags.astype(jnp.float32).reshape((-1,) + (1,) * (ndims - 1))


def route_rows(block_now, send_local, send_valid, recv_source, recv_valid, grid_rows):
    outgoing = jnp.take(block_now, send_local, axis=0) * valid_gain(send_valid, block_now.ndim)
    outgoing = outgoing.reshape((grid_rows, -1) + block_now.shape[1:])
    incoming = lax.all_to_all(outgoing, "row", split_axis=0, concat_axis=0, tiled=True)
    incoming = incoming.reshape((-1,) + block_now.shape[1:])
    return jnp.take(incoming, recv_source, axis=0) * valid_gain(recv_valid, block_now.ndim)


def local(front, tile_live, row_target, col_target):
    grid_rows = lax.axis_size("row")
    grid_cols = lax.axis_size("col")
    my_row = lax.axis_index("row")
    my_col = lax.axis_index("col")
    rows_dev = front.shape[0]
    cols_dev = front.shape[2]
    tile_size = front.shape[4]
    per_dest = rows_dev // grid_rows
    current = front[:, 0, :, 0]
    global_rows = jnp.arange(rows_dev, dtype=jnp.int32) * grid_rows + my_row
    global_cols = jnp.arange(cols_dev, dtype=jnp.int32) * grid_cols + my_col
    update_count = tile_live.shape[0]
    trail_pick = jnp.clip(global_rows - LEAD, 0, update_count - 1)
    row_live = jnp.where(global_rows >= LEAD, jnp.take(tile_live, trail_pick), 1)
    row_gain = row_live.astype(jnp.float32)[:, None, None]
    update_index = jnp.arange(update_count, dtype=jnp.int32)
    source_row = (update_index + LEAD) % grid_rows
    target_row = row_target % grid_rows
    target_slot = row_target // grid_rows
    earlier = (
        (source_row[:, None] == source_row[None, :])
        & (target_row[:, None] == target_row[None, :])
        & (update_index[None, :] < update_index[:, None])
    )
    arrival = jnp.sum(earlier.astype(jnp.int32), axis=1)
    send_slots = jnp.arange(grid_rows * per_dest, dtype=jnp.int32)
    send_match = (
        (source_row[None, :] == my_row)
        & (target_row[None, :] == send_slots[:, None] // per_dest)
        & (arrival[None, :] == send_slots[:, None] % per_dest)
    ).astype(jnp.int32)
    send_local = jnp.sum(send_match * ((update_index + LEAD) // grid_rows)[None, :], axis=1)
    send_valid = jnp.sum(send_match, axis=1) > 0
    out_slots = jnp.arange(rows_dev, dtype=jnp.int32)
    recv_match = (
        (target_row[None, :] == my_row) & (target_slot[None, :] == out_slots[:, None])
    ).astype(jnp.int32)
    recv_source = jnp.sum(recv_match * (source_row * per_dest + arrival)[None, :], axis=1)
    recv_valid = jnp.sum(recv_match, axis=1) > 0
    source_col = (update_index + LEAD) % grid_cols
    out_cols = jnp.arange(cols_dev, dtype=jnp.int32)
    col_match = (
        (source_col[None, :] == my_col) & ((col_target // grid_cols)[None, :] == out_cols[:, None])
    ).astype(jnp.int32)
    col_local = jnp.sum(col_match * ((update_index + LEAD) // grid_cols)[None, :], axis=1)
    col_valid = jnp.sum(col_match, axis=1) > 0
    col_gain = col_valid.astype(jnp.float32)
    groups = [(step * PANEL_TILES, PANEL_TILES) for step in range(PANELS)]
    column_limit = NT
    factors = []
    col_factors = []
    for start_tile, panel_width in groups:
        columns = []
        for tile_col in range(start_tile, start_tile + panel_width):
            piece = current[:, tile_col // grid_cols]
            columns.append(broadcast(piece, "col", tile_col % grid_cols))
        panel_block = jnp.concatenate(columns, axis=2) * row_gain
        diag_parts = []
        for tile_row in range(start_tile, start_tile + panel_width):
            owns_row = my_row == tile_row % grid_rows
            diag_parts.append(jnp.where(owns_row, panel_block[tile_row // grid_rows], 0.0))
        diag_block = lax.psum(jnp.concatenate(diag_parts, axis=0), "row")
        diag_factor = jnp.linalg.cholesky(symmetric_lower(diag_block))
        panel_flat = panel_block.reshape(rows_dev * tile_size, panel_width * tile_size)
        solved = jax.scipy.linalg.solve_triangular(diag_factor, panel_flat.T, lower=True).T
        solved = solved.reshape(rows_dev, tile_size, panel_width * tile_size)
        diag_tiles = diag_factor.reshape(panel_width, tile_size, panel_width * tile_size)
        diag_rows = jnp.take(
            diag_tiles, jnp.clip(global_rows - start_tile, 0, panel_width - 1), axis=0
        )
        below = (global_rows >= start_tile + panel_width)[:, None, None]
        inside = (global_rows >= start_tile)[:, None, None]
        factor = jnp.where(below, solved, jnp.where(inside, diag_rows, 0.0))
        factors.append(factor)
        chosen_rows = (
            jnp.arange(cols_dev, dtype=jnp.int32) * (grid_cols // grid_rows) + my_col // grid_rows
        )
        chosen = jnp.take(factor, chosen_rows, axis=0)
        col_factor = broadcast(chosen, "row", my_col % grid_rows)
        col_factors.append(col_factor)
        col_ok = (global_cols >= start_tile + panel_width) & (global_cols < column_limit)
        col_use = col_factor * col_ok.astype(jnp.float32)[:, None, None]
        any_col = jnp.any(col_ok)
        updated = []
        for row_slot in range(rows_dev):
            active = (
                (row_live[row_slot] > 0)
                & (global_rows[row_slot] >= start_tile + panel_width)
                & any_col
            )
            row_factor = factor[row_slot]
            updated.append(
                lax.cond(
                    active,
                    lambda block_now, row_factor=row_factor, col_use=col_use: block_now
                    - jnp.einsum("ik,bjk->bij", row_factor, col_use, precision=PRECISE),
                    lambda block_now: block_now,
                    current[row_slot],
                )
            )
        current = jnp.stack(updated)
    all_factor = jnp.concatenate(factors, axis=2)
    permuted = jnp.take(current, col_local, axis=1) * col_gain[None, :, None, None]
    parent = route_rows(permuted, send_local, send_valid, recv_source, recv_valid, grid_rows)
    return (all_factor[:, None], parent[:, None, :, None])


def solution(mesh):
    in_specs = (P(None, "row", None, "col", None, None), P(), P(), P())
    out_specs = (P(None, "row", None, None), P(None, "row", None, "col", None, None))
    return jax.shard_map(local, mesh=mesh, in_specs=in_specs, out_specs=out_specs, check_vma=False)
```

profile of v0, /device:TPU:1, one launch (start us, length us, event | category | flops | bytes accessed | tf_op | source)
XLA Modules:
  0.0 1103.7 jit_solution(5710114558274784918)
XLA Ops:
  14.8 105.6 %all-reduce.20.cloned.1.call-done = (f32[8,256,256]{2,1,0:T(8,128)}, f32[8,256,256]{2,1,0:T(8,128)}) async-done(((f32[8,256,256]{2,1,0:T(8,128)}, f32[8,256,256]{2,1,0:T(8,128)}), (f32[8,256,256]{2,1,0:T(8,128)}, f32[8,256,256]{2,1,0:T(8,128)})) %all-reduce.20.cloned.1.call-update) | async-done | bytes 4194320 | tf_op jit(solution)/shard_map/psum | solution.py:17
  127.6 4.4 fusion.58
  132.0 51.5 %all-reduce.10.cloned.1.call-done = f32[512,512]{1,0:T(8,128)} async-done(((f32[512,512]{1,0:T(8,128)}), f32[512,512]{1,0:T(8,128)}) %all-reduce.10.cloned.1.call-update) | async-done | bytes 1048592 | tf_op jit(solution)/shard_map/psum | solution.py:98
  187.1 11.7 %cholesky.286 = f32[128,128]{1,0:T(8,128)S(1)} custom-call(f32[128,128]{1,0:T(8,128)S(1)} %cholesky.426), custom_call_target="Cholesky" | custom-call | tf_op jit(solution)/shard_map/jit(cholesky)/cholesky | solution.py:99
  198.9 9.8 custom-call.27
  209.4 11.7 %cholesky.305 = f32[128,128]{1,0:T(8,128)S(1)} custom-call(f32[128,128]{1,0:T(8,128)S(1)} %cholesky.430), custom_call_target="Cholesky" | custom-call | tf_op jit(solution)/shard_map/jit(cholesky)/cholesky | solution.py:99
  222.5 10.1 custom-call.28
  233.3 11.7 %cholesky.326 = f32[128,128]{1,0:T(8,128)S(1)} custom-call(f32[128,128]{1,0:T(8,128)S(1)} %cholesky.435), custom_call_target="Cholesky" | custom-call | tf_op jit(solution)/shard_map/jit(cholesky)/cholesky | solution.py:99
  245.7 9.8 custom-call.29
  256.1 11.9 %cholesky.343 = f32[128,128]{1,0:T(8,128)S(1)} custom-call(f32[128,128]{1,0:T(8,128)S(1)} %convolution_subtract_fusion.9), custom_call_target="Cholesky" | custom-call | tf_op jit(solution)/shard_map/jit(cholesky)/cholesky | solution.py:99
  271.5 8.5 while.4
  280.0 39.3 %custom-call.30 = f32[4,128,128]{1,2,0:T(8,128)S(1)} custom-call(f32[4,128,128]{2,1,0:T(8,128)S(1)} %get-tuple-element.317), custom_call_target="InvertDiagBlocksLowerTriangular" | custom-call | tf_op jit(solution)/shard_map/jit(_solve_triangular)/triangular_solve | solution.py:101
  333.0 5.7 copy.206
  341.6 6.6 fusion.61
  352.8 6.3 fusion.158
  393.2 24.8 %all-reduce.12.cloned.1.call-done = f32[4,256,512]{2,1,0:T(8,128)} async-done(((f32[4,256,512]{2,1,0:T(8,128)}), f32[4,256,512]{2,1,0:T(8,128)}) %all-reduce.12.cloned.1.call-update) | async-done | bytes 2097168 | tf_op jit(solution)/shard_map/psum | solution.py:17
  431.5 4.3 conditional.21
  454.5 4.2 conditional.17
  472.0 106.3 %all-reduce.18.cloned.1.call-done = (f32[8,256,256]{2,1,0:T(8,128)}, f32[8,256,256]{2,1,0:T(8,128)}) async-done(((f32[8,256,256]{2,1,0:T(8,128)}, f32[8,256,256]{2,1,0:T(8,128)}), (f32[8,256,256]{2,1,0:T(8,128)}, f32[8,256,256]{2,1,0:T(8,128)})) %all-reduce.18.cloned.1.call-update) | async-done | bytes 4194320 | tf_op jit(solution)/shard_map/psum | solution.py:17
  585.9 4.4 fusion.59
  590.3 51.1 %all-reduce.14.cloned.1.call-done = f32[512,512]{1,0:T(8,128)} async-done(((f32[512,512]{1,0:T(8,128)}), f32[512,512]{1,0:T(8,128)}) %all-reduce.14.cloned.1.call-update) | async-done | bytes 1048592 | tf_op jit(solution)/shard_map/psum | solution.py:98
  647.2 11.7 %cholesky.358 = f32[128,128]{1,0:T(8,128)S(1)} custom-call(f32[128,128]{1,0:T(8,128)S(1)} %cholesky.439), custom_call_target="Cholesky" | custom-call | tf_op jit(solution)/shard_map/jit(cholesky)/cholesky | solution.py:99
  659.1 9.8 custom-call.31
  671.4 11.7 %cholesky.377 = f32[128,128]{1,0:T(8,128)S(1)} custom-call(f32[128,128]{1,0:T(8,128)S(1)} %cholesky.443), custom_call_target="Cholesky" | custom-call | tf_op jit(solution)/shard_map/jit(cholesky)/cholesky | solution.py:99
  684.5 10.0 custom-call.32
  696.1 11.7 %cholesky.398 = f32[128,128]{1,0:T(8,128)S(1)} custom-call(f32[128,128]{1,0:T(8,128)S(1)} %cholesky.448), custom_call_target="Cholesky" | custom-call | tf_op jit(solution)/shard_map/jit(cholesky)/cholesky | solution.py:99
  708.5 9.8 custom-call.33
  719.7 12.1 %cholesky.415 = f32[128,128]{1,0:T(8,128)S(1)} custom-call(f32[128,128]{1,0:T(8,128)S(1)} %convolution_subtract_fusion.8), custom_call_target="Cholesky" | custom-call | tf_op jit(solution)/shard_map/jit(cholesky)/cholesky | solution.py:99
  736.2 11.6 %while.5 = (s32[]{:T(128)}, f32[512,512]{1,0:T(8,128)}, s32[4,2]{0,1:T(2,128)S(1)}, f32[4,128,128]{2,1,0:T(8,128)S(1)}, s32[]{:T(128)}) while((s32[]{:T(128)}, f32[512,512]{1,0:T(8,128)}, s32[4,2]{0,1:T(2,128)S(1)}, f32[4,128,128]{2,1,0:T(8,128)S(1)}, s32[]{:T(128)}) %tuple.389), condition=%wide.while_cond.clone, body=%wide.while_body.clone.sunk | while | flops 2 | bytes 131181 | solution.py:101
  747.8 39.3 %custom-call.34 = f32[4,128,128]{1,2,0:T(8,128)S(1)} custom-call(f32[4,128,128]{2,1,0:T(8,128)S(1)} %get-tuple-element.318), custom_call_target="InvertDiagBlocksLowerTriangular" | custom-call | tf_op jit(solution)/shard_map/jit(_solve_triangular)/triangular_solve | solution.py:101
  802.7 5.5 copy.207
  811.0 6.5 fusion.60
  832.3 55.1 %all-reduce.16.cloned.1.call-done = f32[4,256,512]{2,1,0:T(8,128)} async-done(((f32[4,256,512]{2,1,0:T(8,128)}), f32[4,256,512]{2,1,0:T(8,128)}) %all-reduce.16.cloned.1.call-update) | async-done | bytes 2097168 | tf_op jit(solution)/shard_map/psum | solution.py:17
  894.2 6.4 conditional.31
  901.8 6.7 conditional.30
  908.6 6.6 conditional.29
  916.4 6.7 conditional.28
  923.1 6.5 conditional.27
  933.3 5.7 conditional.25
  947.8 7.9 gather_fusion.1
  955.7 4.2 multiply_bitcast_fusion
  963.9 7.9 gather_fusion.6
  971.8 7.8 fusion.57
  979.6 7.4 all-to-all-start
  987.2 8.3 maximum_bitcast_fusion
  995.5 85.2 %all-to-all-done = f32[8,1,4,256,256]{4,3,2,1,0:T(8,128)} async-done(((f32[8,1,4,256,256]{4,3,2,1,0:T(8,128)}), f32[8,1,4,256,256]{4,3,2,1,0:T(8,128)}, u32[]{:S(2)}, u32[]{:S(2)}) %all-to-all-start) | async-done | bytes 8388640 | tf_op jit(solution)/shard_map/all_to_all | solution.py:31
  1080.7 7.9 gather_fusion.7
  1088.6 7.9 fusion.56
  (275 shorter events, 267.8 us)
Async XLA Ops:
  7.2 6.6 copy-start
  7.2 113.2 %all-reduce.20.cloned.1.call-start = ((), (), s32[]{:S(2)}) async-start(), calls=%async_computation.6 | async-start | bytes 8388608 | tf_op jit(solution)/shard_map/psum | solution.py:17
  11.2 3.4 copy-start.21
  13.6 169.9 %all-reduce.10.cloned.1.call-start = ((), (), s32[]{:S(2)}) async-start(), calls=%async_computation.1 | async-start | bytes 2097152 | tf_op jit(solution)/shard_map/psum | solution.py:98
  122.7 295.3 %all-reduce.12.cloned.1.call-start = ((), (), s32[]{:S(2)}) async-start(), calls=%async_computation.2 | async-start | bytes 4194304 | tf_op jit(solution)/shard_map/psum | solution.py:17
  319.3 5.8 copy-start.6
  352.7 225.6 %all-reduce.18.cloned.1.call-start = ((), (), s32[]{:S(2)}) async-start(), calls=%async_computation.5 | async-start | bytes 8388608 | tf_op jit(solution)/shard_map/psum | solution.py:17
  461.2 5.5 copy-start.12
  461.2 5.6 copy-start.11
  463.9 3.0 copy-start.10
  465.3 1.7 copy-start.9
  466.7 1.3 copy-start.8
  466.8 1.5 copy-start.7
  468.4 3.2 copy-start.20
  471.0 170.4 %all-reduce.14.cloned.1.call-start = ((), (), s32[]{:S(2)}) async-start(), calls=%async_computation.3 | async-start | bytes 2097152 | tf_op jit(solution)/shard_map/psum | solution.py:98
  580.6 306.7 %all-reduce.16.cloned.1.call-start = ((), (), s32[]{:S(2)}) async-start(), calls=%async_computation.4 | async-start | bytes 4194304 | tf_op jit(solution)/shard_map/psum | solution.py:17
  641.4 2.8 copy-start.18
  646.2 1.0 copy-start.19
  787.2 5.8 copy-start.5
  900.6 1.2 copy-start.4
  915.2 1.2 copy-start.3
  929.6 1.2 copy-start.2
  939.0 3.6 copy-start.17
  939.0 4.6 copy-start.16
  939.0 5.7 copy-start.15
  940.1 5.7 copy-start.14
  942.6 4.2 copy-start.13
  979.6 101.1 %all-to-all-start = ((f32[8,1,4,256,256]{4,3,2,1,0:T(8,128)}), f32[8,1,4,256,256]{4,3,2,1,0:T(8,128)}, u32[]{:S(2)}, u32[]{:S(2)}) async-start(f32[8,1,4,256,256]{4,3,2,1,0:T(8,128)} %fusion.57), calls=%async_computation | async-start | bytes 16777216 | tf_op jit(solution)/shard_map/all_to_all | solution.py:31
  1088.6 7.9 copy-start.1
Sparse Core Ops, SparseCore 0:
  13.7 106.5 all-reduce.19
  122.8 60.5 all-reduce.9
  352.8 65.1 all-reduce.11
  471.1 107.1 all-reduce.17
  580.8 60.5 all-reduce.13
  822.3 65.0 all-reduce.15
where the time goes:
time: 1120 us; the launch traced here: 1100 us
  waiting for transfers between devices  480 us (43%)
  other arithmetic  318 us (28%)
  local copies, waits for them, and re-layouts  172 us (15%)
  matrix products  79.7 us (7%)
  between operations  45.8 us (4%)
    psum x4, waiting for transfers between devices, broadcast(): return lax.psum(block, axis)  292 us
    another operation x30, other arithmetic, local(): diag_factor = jnp.linalg.cholesky(symmetric_lower(diag_block))  159 us
    psum x2, waiting for transfers between devices, local(): diag_block = lax.psum(jnp.concatenate(diag_parts, axis=0), 'row')  103 us
    all_to_all x1, waiting for transfers between devices, route_rows(): lax.all_to_all(outgoing, 'row', split_axis=0, concat_axis=0, tiled=True)  85.2 us
    another operation x5, other arithmetic, local(): jax.scipy.linalg.solve_triangular(diag_factor, panel_flat.T, lower=True)  80.1 us
    dot_general x12, matrix products, local(): jnp.einsum('ik,bjk->bij', row_factor, col_use, precision=PRECISE)  48.2 us
    unnamed x69, local copies, waits for them, and re-layouts  39.9 us
    another operation x14, matrix products, local(): jax.scipy.linalg.solve_triangular(diag_factor, panel_flat.T, lower=True)  24.1 us
  transfers between devices with their start and end apart: 7, of which 7 were waited for; matrix products, arithmetic and copies ran while one was open for 5% of the time, Pallas kernels for 0%

commit v1 on v0

v1 whole, which is shorter than its diff:
```python
import jax
import jax.numpy as jnp
from jax import lax
from jax.sharding import PartitionSpec as P

LEAD = 4
PRECISE = lax.Precision.HIGHEST


def valid_gain(valid_flags, ndims):
    return valid_flags.astype(jnp.float32).reshape((-1,) + (1,) * (ndims - 1))


def route_rows(block_now, send_local, send_valid, recv_source, recv_valid, grid_rows):
    outgoing = jnp.take(block_now, send_local, axis=0) * valid_gain(send_valid, block_now.ndim)
    outgoing = outgoing.reshape((grid_rows, -1) + block_now.shape[1:])
    incoming = lax.all_to_all(outgoing, "row", split_axis=0, concat_axis=0, tiled=True)
    incoming = incoming.reshape((-1,) + block_now.shape[1:])
    return jnp.take(incoming, recv_source, axis=0) * valid_gain(recv_valid, block_now.ndim)


def local(front, tile_live, row_target, col_target):
    grid_rows = lax.axis_size("row")
    grid_cols = lax.axis_size("col")
    my_row = lax.axis_index("row")
    my_col = lax.axis_index("col")
    rows_dev = front.shape[0]
    cols_dev = front.shape[2]
    tile = front.shape[4]
    lead_w = LEAD * tile
    per_dest = rows_dev // grid_rows
    current = front[:, 0, :, 0]
    update_count = tile_live.shape[0]

    update_index = jnp.arange(update_count, dtype=jnp.int32)
    source_row = (update_index + LEAD) % grid_rows
    target_row = row_target % grid_rows
    target_slot = row_target // grid_rows
    earlier = (
        (source_row[:, None] == source_row[None, :])
        & (target_row[:, None] == target_row[None, :])
        & (update_index[None, :] < update_index[:, None])
    )
    arrival = jnp.sum(earlier.astype(jnp.int32), axis=1)
    send_slots = jnp.arange(grid_rows * per_dest, dtype=jnp.int32)
    send_match = (
        (source_row[None, :] == my_row)
        & (target_row[None, :] == send_slots[:, None] // per_dest)
        & (arrival[None, :] == send_slots[:, None] % per_dest)
    ).astype(jnp.int32)
    send_local = jnp.sum(send_match * ((update_index + LEAD) // grid_rows)[None, :], axis=1)
    send_valid = jnp.sum(send_match, axis=1) > 0
    out_slots = jnp.arange(rows_dev, dtype=jnp.int32)
    recv_match = (
        (target_row[None, :] == my_row) & (target_slot[None, :] == out_slots[:, None])
    ).astype(jnp.int32)
    recv_source = jnp.sum(recv_match * (source_row * per_dest + arrival)[None, :], axis=1)
    recv_valid = jnp.sum(recv_match, axis=1) > 0
    source_col = (update_index + LEAD) % grid_cols
    out_cols = jnp.arange(cols_dev, dtype=jnp.int32)
    col_match = (
        (source_col[None, :] == my_col) & ((col_target // grid_cols)[None, :] == out_cols[:, None])
    ).astype(jnp.int32)
    col_local = jnp.sum(col_match * ((update_index + LEAD) // grid_cols)[None, :], axis=1)
    col_valid = jnp.sum(col_match, axis=1) > 0
    col_gain = col_valid.astype(jnp.float32)

    lead_tile = current[0, 0]
    row_tiles = lax.all_gather(lead_tile, "col")[:LEAD]
    lead_tiles = lax.all_gather(row_tiles, "row")[:LEAD]
    lead_block = lead_tiles.transpose(0, 2, 1, 3).reshape(lead_w, lead_w)
    sym = jnp.tril(lead_block) + jnp.tril(lead_block, -1).T
    chol = jnp.linalg.cholesky(sym)

    chunks = rows_dev * 2
    half = tile // 2
    panel_col = current[:, 0].reshape(chunks, half, tile)
    gathered = lax.all_to_all(panel_col, "col", split_axis=0, concat_axis=0, tiled=True)
    panel_rows = gathered[:LEAD].transpose(1, 0, 2).reshape(half, lead_w)
    my_tile_row = (my_col // 2) * grid_rows + my_row
    live = jnp.where(
        my_tile_row >= LEAD,
        jnp.take(tile_live, jnp.clip(my_tile_row - LEAD, 0, update_count - 1)),
        1,
    ).astype(jnp.float32)
    solved = jax.scipy.linalg.solve_triangular(chol, (panel_rows * live).T, lower=True).T
    start = jnp.clip(my_tile_row * tile + (my_col % 2) * half, 0, lead_w - half)
    chol_rows = lax.dynamic_slice(chol, (start, 0), (half, lead_w))
    piece = jnp.where(my_tile_row < LEAD, chol_rows, solved)
    factor_rows = lax.all_gather(piece, "col").reshape(rows_dev, tile, lead_w)

    src_row = my_col % grid_rows
    pick = jnp.arange(cols_dev, dtype=jnp.int32) * (grid_cols // grid_rows) + my_col // grid_rows
    col_src = jnp.take(factor_rows, pick, axis=0).reshape(grid_rows, -1, lead_w)
    rel = (my_row - src_row) % grid_rows
    mine = jnp.where(rel == 0, col_src[0], 0.0)
    for shift in range(1, grid_rows):
        perm = []
        for c in range(grid_cols):
            s = c % grid_rows
            perm.append((s * grid_cols + c, ((s + shift) % grid_rows) * grid_cols + c))
        mine = mine + lax.ppermute(col_src[shift], ("row", "col"), perm)
    spread = lax.all_gather(mine, "row")
    order = (src_row + jnp.arange(grid_rows, dtype=jnp.int32)) % grid_rows
    col_factor = jnp.take(spread, order, axis=0).reshape(cols_dev, tile, lead_w)

    prod = jnp.einsum("aik,bjk->abij", factor_rows, col_factor, precision=PRECISE)
    schur = current - prod

    permuted = jnp.take(schur, col_local, axis=1) * col_gain[None, :, None, None]
    parent = route_rows(permuted, send_local, send_valid, recv_source, recv_valid, grid_rows)
    return (factor_rows[:, None], parent[:, None, :, None])


def solution(mesh):
    in_specs = (P(None, "row", None, "col", None, None), P(), P(), P())
    out_specs = (P(None, "row", None, None), P(None, "row", None, "col", None, None))
    return jax.shard_map(local, mesh=mesh, in_specs=in_specs, out_specs=out_specs, check_vma=False)
```

time: 1120 us -> 850 us (0.76)
  waiting for transfers between devices: 480 us -> 310 us
  local copies, waits for them, and re-layouts: 172 us -> 120 us
  between operations: 45.8 us -> 20.6 us
  matrix products: 79.7 us -> 65.5 us
  starting transfers between devices: 7.62 us -> 20.1 us
  other arithmetic: 318 us -> 306 us
    psum x6 -> x0, waiting for transfers between devices: 394 us -> none  [the longest x4 292 us: broadcast(): return lax.psum(block, axis)]
    all_gather x0 -> x4, waiting for transfers between devices: none -> 191 us  [the longest x1 70.2 us: local(): factor_rows = lax.all_gather(piece, 'col').reshape(rows_dev, tile, lead_w)]
    cond x16 -> x0, local copies, waits for them, and re-layouts: 38.7 us -> none
    all_to_all x0 -> x1, waiting for transfers between devices: none -> 25.6 us  [local(): lax.all_to_all(panel_col, 'col', split_axis=0, concat_axis=0, tiled=True)]
    another operation x35 -> x33, other arithmetic: 239 us -> 258 us  [the longest x30 172 us: local(): chol = jnp.linalg.cholesky(sym)]
    dot_general x12 -> x1, matrix products: 48.2 us -> 30.9 us  [local(): jnp.einsum('aik,bjk->abij', factor_rows, col_factor, precision=PRECISE)]
    select_n x15 -> x7, other arithmetic: 25.4 us -> 9.66 us  [the longest x2 2.7 us: local(): col_src = jnp.take(factor_rows, pick, axis=0).reshape(grid_rows, -1, lead_w)]
    transpose x4 -> x0, other arithmetic: 13.7 us -> none  [the longest x2 8.76 us: local(): solved = jax.scipy.linalg.solve_triangular(diag_factor, panel_flat.T, low...]
  transfers between devices with their start and end apart: 7 -> 13, of which waited for: 7 -> 6; matrix products, arithmetic and copies ran while one was open for 5% -> 1% of each run, Pallas kernels for 0% -> 0%
where the time goes in v1:
time: 850 us; the launch traced here: 843 us
  waiting for transfers between devices  310 us (36%)
  other arithmetic  306 us (36%)
  local copies, waits for them, and re-layouts  120 us (14%)
  matrix products  65.5 us (8%)
  between operations  20.6 us (2%)
  starting transfers between devices  20.1 us (2%)
    another operation x30, other arithmetic, local(): chol = jnp.linalg.cholesky(sym)  172 us
    all_to_all x1, waiting for transfers between devices, route_rows(): lax.all_to_all(outgoing, 'row', split_axis=0, concat_axis=0, tiled=True)  93.5 us
    another operation x3, other arithmetic, local(): jax.scipy.linalg.solve_triangular(chol, (panel_rows * live).T, lower=True)  85.6 us
    all_gather x1, waiting for transfers between devices, local(): factor_rows = lax.all_gather(piece, 'col').reshape(rows_dev, tile, lead_w)  70.2 us
    all_gather x1, waiting for transfers between devices, local(): row_tiles = lax.all_gather(lead_tile, 'col')[:LEAD]  54.7 us
    all_gather x1, waiting for transfers between devices, local(): spread = lax.all_gather(mine, 'row')  52.5 us
    unnamed x25, local copies, waits for them, and re-layouts  34 us
    dot_general x1, matrix products, local(): jnp.einsum('aik,bjk->abij', factor_rows, col_factor, precision=PRECISE)  30.9 us
  transfers between devices with their start and end apart: 13, of which 6 were waited for; matrix products, arithmetic and copies ran while one was open for 1% of the time, Pallas kernels for 0%

profile of v1, /device:TPU:1, one launch (start us, length us, event | category | flops | bytes accessed | tf_op | source)
XLA Modules:
  0.0 842.8 jit_solution(6044269375804220116)
XLA Ops:
  7.2 8.7 %copy.54 = f32[8,1,4,1,256,256]{4,5,0,2,3,1:T(8,128)} copy(f32[8,1,4,1,256,256]{5,4,3,2,1,0:T(8,128)} %param.6) | data formatting | bytes 16777216 | tf_op args[0]
  17.8 54.7 %all-gather.10.cloned.1.call-done = f32[16,1,256,256]{3,2,1,0:T(8,128)} async-done(((f32[1,1,256,256]{3,2,1,0:T(8,128)}), f32[16,1,256,256]{3,2,1,0:T(8,128)}) %all-gather.10.cloned.1.call-update) | async-done | bytes 4194320 | tf_op jit(solution)/shard_map/all_gather | solution.py:69
  78.5 5.0 all-to-all-start
  84.9 25.6 %all-to-all-done = f32[16,128,256]{2,1,0:T(8,128)S(1)} async-done(((f32[16,128,256]{2,1,0:T(8,128)}), f32[16,128,256]{2,1,0:T(8,128)S(1)}, u32[]{:S(2)}, u32[]{:S(2)}) %all-to-all-start) | async-done | bytes 2097184 | tf_op jit(solution)/shard_map/all_to_all | solution.py:78
  110.8 13.9 %all-gather.16.cloned.1.call-done = f32[32,1,256,256]{3,2,1,0:T(8,128)} async-done(((f32[4,1,256,256]{3,2,1,0:T(8,128)}), f32[32,1,256,256]{3,2,1,0:T(8,128)}) %all-gather.16.cloned.1.call-update) | async-done | bytes 8388624 | tf_op jit(solution)/shard_map/all_gather | solution.py:70
  127.0 2.7 copy.56
  132.6 2.5 fusion.4
  135.1 5.3 copy.57
  140.5 6.0 bitcast_add_fusion.1
  146.4 5.8 copy.58
  152.3 4.4 fusion.2
  158.6 11.7 %cholesky.222 = f32[128,128]{1,0:T(8,128)S(1)} custom-call(f32[128,128]{1,0:T(8,128)S(1)} %cholesky.577), custom_call_target="Cholesky" | custom-call | tf_op jit(solution)/shard_map/jit(cholesky)/cholesky | solution.py:73
  170.4 9.8 %custom-call.63 = f32[1,128,128]{1,2,0:T(8,128)S(1)} custom-call(f32[1,128,128]{2,1,0:T(8,128)S(1)} %get-tuple-element.95), custom_call_target="InvertDiagBlocksLowerTriangular" | custom-call | tf_op jit(solution)/shard_map/jit(cholesky)/cholesky | solution.py:73
  180.2 2.5 cholesky.254
  186.6 11.9 %cholesky.243 = f32[128,128]{1,0:T(8,128)S(1)} custom-call(f32[128,128]{1,0:T(8,128)S(1)} %cholesky.581), custom_call_target="Cholesky" | custom-call | tf_op jit(solution)/shard_map/jit(cholesky)/cholesky | solution.py:73
  199.1 9.8 %custom-call.64 = f32[1,128,128]{1,2,0:T(8,128)S(1)} custom-call(f32[1,128,128]{2,1,0:T(8,128)S(1)} %get-tuple-element.92), custom_call_target="InvertDiagBlocksLowerTriangular" | custom-call | tf_op jit(solution)/shard_map/jit(cholesky)/cholesky | solution.py:73
  212.3 11.7 %cholesky.466 = f32[128,128]{1,0:T(8,128)S(1)} custom-call(f32[128,128]{1,0:T(8,128)S(1)} %cholesky.586), custom_call_target="Cholesky" | custom-call | tf_op jit(solution)/shard_map/jit(cholesky)/cholesky | solution.py:73
  225.3 9.8 %custom-call.65 = f32[1,128,128]{1,2,0:T(8,128)S(1)} custom-call(f32[1,128,128]{2,1,0:T(8,128)S(1)} %get-tuple-element.89), custom_call_target="InvertDiagBlocksLowerTriangular" | custom-call | tf_op jit(solution)/shard_map/jit(cholesky)/cholesky | solution.py:73
  238.6 11.9 %cholesky.485 = f32[128,128]{1,0:T(8,128)S(1)} custom-call(f32[128,128]{1,0:T(8,128)S(1)} %cholesky.591), custom_call_target="Cholesky" | custom-call | tf_op jit(solution)/shard_map/jit(cholesky)/cholesky | solution.py:73
  251.8 9.8 %custom-call.66 = f32[1,128,128]{1,2,0:T(8,128)S(1)} custom-call(f32[1,128,128]{2,1,0:T(8,128)S(1)} %get-tuple-element.86), custom_call_target="InvertDiagBlocksLowerTriangular" | custom-call | tf_op jit(solution)/shard_map/jit(cholesky)/cholesky | solution.py:73
  265.0 11.7 %cholesky.504 = f32[128,128]{1,0:T(8,128)S(1)} custom-call(f32[128,128]{1,0:T(8,128)S(1)} %cholesky.596), custom_call_target="Cholesky" | custom-call | tf_op jit(solution)/shard_map/jit(cholesky)/cholesky | solution.py:73
  278.1 10.2 %custom-call.67 = f32[1,128,128]{1,2,0:T(8,128)S(1)} custom-call(f32[1,128,128]{2,1,0:T(8,128)S(1)} %get-tuple-element.83), custom_call_target="InvertDiagBlocksLowerTriangular" | custom-call | tf_op jit(solution)/shard_map/jit(cholesky)/cholesky | solution.py:73
  291.7 11.7 %cholesky.524 = f32[128,128]{1,0:T(8,128)S(1)} custom-call(f32[128,128]{1,0:T(8,128)S(1)} %cholesky.601), custom_call_target="Cholesky" | custom-call | tf_op jit(solution)/shard_map/jit(cholesky)/cholesky | solution.py:73
  304.7 9.8 %custom-call.68 = f32[1,128,128]{1,2,0:T(8,128)S(1)} custom-call(f32[1,128,128]{2,1,0:T(8,128)S(1)} %get-tuple-element.80), custom_call_target="InvertDiagBlocksLowerTriangular" | custom-call | tf_op jit(solution)/shard_map/jit(cholesky)/cholesky | solution.py:73
  317.5 11.9 %cholesky.544 = f32[128,128]{1,0:T(8,128)S(1)} custom-call(f32[128,128]{1,0:T(8,128)S(1)} %cholesky.606), custom_call_target="Cholesky" | custom-call | tf_op jit(solution)/shard_map/jit(cholesky)/cholesky | solution.py:73
  330.6 9.8 %custom-call.69 = f32[1,128,128]{1,2,0:T(8,128)S(1)} custom-call(f32[1,128,128]{2,1,0:T(8,128)S(1)} %get-tuple-element.77), custom_call_target="InvertDiagBlocksLowerTriangular" | custom-call | tf_op jit(solution)/shard_map/jit(cholesky)/cholesky | solution.py:73
  343.1 11.7 %cholesky.562 = f32[128,128]{1,0:T(8,128)S(1)} custom-call(f32[128,128]{1,0:T(8,128)S(1)} %convolution_subtract_fusion.11), custom_call_target="Cholesky" | custom-call | tf_op jit(solution)/shard_map/jit(cholesky)/cholesky | solution.py:73
  361.7 6.8 fusion.3
  368.5 22.8 %while.2 = (s32[]{:T(128)}, f32[1024,1024]{1,0:T(8,128)}, s32[8,2]{0,1:T(2,128)S(1)}, f32[8,128,128]{2,1,0:T(8,128)S(1)}, s32[]{:T(128)}) while((s32[]{:T(128)}, f32[1024,1024]{1,0:T(8,128)}, s32[8,2]{0,1:T(2,128)S(1)}, f32[8,128,128]{2,1,0:T(8,128)S(1)}, s32[]{:T(128)}) %tuple.83), condition=%wide.while_cond, body=%wide.while_body.sunk | while | flops 2 | bytes 131181 | solution.py:86
  391.3 78.8 %custom-call.70 = f32[8,128,128]{1,2,0:T(8,128)S(1)} custom-call(f32[8,128,128]{2,1,0:T(8,128)S(1)} %get-tuple-element.10), custom_call_target="InvertDiagBlocksLowerTriangular" | custom-call | tf_op jit(solution)/shard_map/jit(_solve_triangular)/triangular_solve | solution.py:86
  485.1 70.2 %all-gather.12.cloned.1.call-done = f32[2048,1024]{1,0:T(8,128)} async-done(((f32[128,1024]{1,0:T(8,128)}), f32[2048,1024]{1,0:T(8,128)}) %all-gather.12.cloned.1.call-update) | async-done | bytes 8388624 | tf_op jit(solution)/shard_map/all_gather | solution.py:90
  555.3 6.2 gather_fusion
  561.5 2.7 broadcast_select_fusion.1
  577.0 3.2 fusion.17
  580.8 52.5 %all-gather.14.cloned.1.call-done = f32[1024,1024]{1,0:T(8,128)} async-done(((f32[128,1024]{1,0:T(8,128)}), f32[1024,1024]{1,0:T(8,128)}) %all-gather.14.cloned.1.call-update) | async-done | bytes 4194320 | tf_op jit(solution)/shard_map/all_gather | solution.py:103
  633.3 5.0 gather_fusion.1
  638.4 2.5 broadcast_select_fusion
  640.9 30.9 %bitcast_subtract_fusion = f32[8,4,256,256]{2,3,0,1:T(8,128)} fusion(f32[4,256,1024,1]{2,1,3,0:T(8,128)S(1)} %bitcast.195, f32[8,256,1024,1]{2,1,0,3:T(8,128)} %bitcast.187, f32[8,1,4,1,256,256]{4,5,0,2,3,1:T(8,128)} %copy.54), kind=kOutput, calls=%fused_computation.7 | convolution fusion | flops 25771900928 | bytes 29360128 | tf_op jit(solution)/shard_map/aik,bjk->abij/dot_general | solution.py:107
  671.8 7.9 gather_fusion.2
  679.6 7.9 multiply_bitcast_fusion
  687.5 7.9 gather_fusion.3
  695.4 7.8 fusion.1
  703.3 5.5 all-to-all-start.1
  709.0 93.5 %all-to-all-done.1 = f32[8,1,4,256,256]{3,4,2,1,0:T(8,128)} async-done(((f32[8,1,4,256,256]{3,4,2,1,0:T(8,128)}), f32[8,1,4,256,256]{3,4,2,1,0:T(8,128)}, u32[]{:S(2)}, u32[]{:S(2)}) %all-to-all-start.1) | async-done | bytes 8388640 | tf_op jit(solution)/shard_map/all_to_all | solution.py:17
  802.5 7.9 gather_fusion.4
  810.3 7.8 fusion
  818.2 9.1 %copy.71 = f32[8,1,4,1,256,256]{5,4,3,2,1,0:T(8,128)} copy(f32[8,1,4,1,256,256]{4,5,2,0,3,1:T(8,128)} %fusion) | data formatting | bytes 16777216
  827.3 8.4 %copy.119 = f32[8,1,256,1024]{3,2,1,0:T(8,128)} copy(f32[8,1,256,1024]{3,2,1,0:T(8,128)} %bitcast.188) | data formatting | bytes 16777216
  (173 shorter events, 99.0 us)
Async XLA Ops:
  7.2 65.3 %all-gather.10.cloned.1.call-start = ((), (), s32[]{:S(2)}) async-start(), calls=%async_computation.2 | async-start | bytes 4456448 | tf_op jit(solution)/shard_map/all_gather | solution.py:69
  17.7 107.0 %all-gather.16.cloned.1.call-start = ((), (), s32[]{:S(2)}) async-start(), calls=%async_computation.5 | async-start | bytes 9437184 | tf_op jit(solution)/shard_map/all_gather | solution.py:70
  76.7 6.9 copy-start.5
  78.5 32.1 %all-to-all-start = ((f32[16,128,256]{2,1,0:T(8,128)}), f32[16,128,256]{2,1,0:T(8,128)S(1)}, u32[]{:S(2)}, u32[]{:S(2)}) async-start(f32[16,128,256]{2,1,0:T(8,128)} %bitcast.20), calls=%async_computation | async-start | bytes 4194304 | tf_op jit(solution)/shard_map/all_to_all | solution.py:78
  83.5 471.8 %all-gather.12.cloned.1.call-start = ((), (), s32[]{:S(2)}) async-start(), calls=%async_computation.3 | async-start | bytes 8912896 | tf_op jit(solution)/shard_map/all_gather | solution.py:90
  124.8 2.2 slice-start
  130.7 2.0 copy-start
  156.7 1.9 copy-start.2
  474.8 9.9 %copy-start.6 = (s32[60]{0:T(128)S(1)}, s32[60]{0:T(128)}, u32[]{:S(2)}) copy-start(s32[60]{0:T(128)} %param.9) | copy-start | bytes 724
  484.7 148.7 %all-gather.14.cloned.1.call-start = ((), (), s32[]{:S(2)}) async-start(), calls=%async_computation.4 | async-start | bytes 4718592 | tf_op jit(solution)/shard_map/all_gather | solution.py:103
  564.2 2.0 copy-start.1
  566.7 13.7 %copy-start.4 = (s32[60]{0:T(128)S(1)}, s32[60]{0:T(128)}, u32[]{:S(2)}) copy-start(s32[60]{0:T(128)} %param.8) | copy-start | bytes 724
  566.7 6.4 collective-permute-start
  568.0 6.6 collective-permute-start.1
  568.7 8.2 collective-permute-start.2
  570.2 6.8 collective-permute-start.3
  571.7 5.3 collective-permute-start.4
  573.1 3.9 collective-permute-start.5
  574.6 0.8 copy-start.3
  575.5 1.5 collective-permute-start.6
  703.3 99.2 %all-to-all-start.1 = ((f32[8,1,4,256,256]{3,4,2,1,0:T(8,128)}), f32[8,1,4,256,256]{3,4,2,1,0:T(8,128)}, u32[]{:S(2)}, u32[]{:S(2)}) async-start(f32[8,1,4,256,256]{3,4,2,1,0:T(8,128)} %fusion.1), calls=%async_computation.1 | async-start | bytes 16777216 | tf_op jit(solution)/shard_map/all_to_all | solution.py:17
Sparse Core Ops, SparseCore 0:
  17.9 54.5 all-gather.9
  75.0 49.7 all-gather.15
  484.8 70.5 all-gather.11
  580.4 52.9 all-gather.13

commit v2 on v1

--- a/solution.py
+++ b/solution.py
@@ -70,7 +70,6 @@
     lead_tiles = lax.all_gather(row_tiles, "row")[:LEAD]
     lead_block = lead_tiles.transpose(0, 2, 1, 3).reshape(lead_w, lead_w)
     sym = jnp.tril(lead_block) + jnp.tril(lead_block, -1).T
-    chol = jnp.linalg.cholesky(sym)
 
     chunks = rows_dev * 2
     half = tile // 2
@@ -83,7 +82,18 @@
         jnp.take(tile_live, jnp.clip(my_tile_row - LEAD, 0, update_count - 1)),
         1,
     ).astype(jnp.float32)
-    solved = jax.scipy.linalg.solve_triangular(chol, (panel_rows * live).T, lower=True).T
+    masked = panel_rows * live
+    bound = 1.0 + 10.0 * jnp.sum(masked * masked)
+    aug = jnp.concatenate(
+        [
+            jnp.concatenate([sym, masked.T], axis=1),
+            jnp.concatenate([masked, jnp.where(jnp.eye(half, dtype=jnp.bool_), bound, 0.0)], axis=1),
+        ],
+        axis=0,
+    )
+    aug_factor = jnp.linalg.cholesky(aug)
+    chol = aug_factor[:lead_w, :lead_w]
+    solved = aug_factor[lead_w:, :lead_w]
     start = jnp.clip(my_tile_row * tile + (my_col % 2) * half, 0, lead_w - half)
     chol_rows = lax.dynamic_slice(chol, (start, 0), (half, lead_w))
     piece = jnp.where(my_tile_row < LEAD, chol_rows, solved)

time: 850 us -> 769 us (0.905)
  other arithmetic: 306 us -> 243 us
  local copies, waits for them, and re-layouts: 120 us -> 108 us
    another operation x33 -> x34, other arithmetic: 258 us -> 191 us  [local(): aug_factor = jnp.linalg.cholesky(aug)]
    another operation x40 -> x34, local copies, waits for them, and re-layouts: 25.9 us -> 9.51 us  [local(): aug_factor = jnp.linalg.cholesky(aug)]
    another operation x29 -> x16, matrix products: 34.6 us -> 28.1 us  [local(): aug_factor = jnp.linalg.cholesky(aug)]
    unnamed x25 -> x20, local copies, waits for them, and re-layouts: 34 us -> 36.4 us
where the time goes in v2:
time: 769 us; the launch traced here: 761 us
  waiting for transfers between devices  309 us (40%)
  other arithmetic  243 us (32%)
  local copies, waits for them, and re-layouts  108 us (14%)
  matrix products  59 us (8%)
  between operations  22 us (3%)
  starting transfers between devices  20.1 us (3%)
    another operation x34, other arithmetic, local(): aug_factor = jnp.linalg.cholesky(aug)  191 us
    all_to_all x1, waiting for transfers between devices, route_rows(): lax.all_to_all(outgoing, 'row', split_axis=0, concat_axis=0, tiled=True)  93.5 us
    all_gather x1, waiting for transfers between devices, local(): factor_rows = lax.all_gather(piece, 'col').reshape(rows_dev, tile, lead_w)  70.2 us
    all_gather x1, waiting for transfers between devices, local(): row_tiles = lax.all_gather(lead_tile, 'col')[:LEAD]  54.7 us
    all_gather x1, waiting for transfers between devices, local(): spread = lax.all_gather(mine, 'row')  52.5 us
    unnamed x20, local copies, waits for them, and re-layouts  36.4 us
    dot_general x1, matrix products, local(): jnp.einsum('aik,bjk->abij', factor_rows, col_factor, precision=PRECISE)  30.9 us
    another operation x16, matrix products, local(): aug_factor = jnp.linalg.cholesky(aug)  28.1 us
  transfers between devices with their start and end apart: 13, of which 6 were waited for; matrix products, arithmetic and copies ran while one was open for 1% of the time, Pallas kernels for 0%

profile of v2, /device:TPU:1, one launch (start us, length us, event | category | flops | bytes accessed | tf_op | source)
XLA Modules:
  0.0 761.2 jit_solution(14935917948489428547)
XLA Ops:
  7.2 8.7 %copy.108 = f32[8,1,4,1,256,256]{4,5,0,2,3,1:T(8,128)} copy(f32[8,1,4,1,256,256]{5,4,3,2,1,0:T(8,128)} %param.6) | data formatting | bytes 16777216 | tf_op args[0]
  17.8 54.7 %all-gather.10.cloned.1.call-done = f32[16,1,256,256]{3,2,1,0:T(8,128)} async-done(((f32[1,1,256,256]{3,2,1,0:T(8,128)}), f32[16,1,256,256]{3,2,1,0:T(8,128)}) %all-gather.10.cloned.1.call-update) | async-done | bytes 4194320 | tf_op jit(solution)/shard_map/all_gather | solution.py:69
  78.5 5.0 all-to-all-start
  85.0 25.6 %all-to-all-done = f32[16,128,256]{2,1,0:T(8,128)S(1)} async-done(((f32[16,128,256]{2,1,0:T(8,128)}), f32[16,128,256]{2,1,0:T(8,128)S(1)}, u32[]{:S(2)}, u32[]{:S(2)}) %all-to-all-start) | async-done | bytes 2097184 | tf_op jit(solution)/shard_map/all_to_all | solution.py:77
  112.4 12.4 %all-gather.16.cloned.1.call-done = f32[32,1,256,256]{3,2,1,0:T(8,128)} async-done(((f32[4,1,256,256]{3,2,1,0:T(8,128)}), f32[32,1,256,256]{3,2,1,0:T(8,128)}) %all-gather.16.cloned.1.call-update) | async-done | bytes 8388624 | tf_op jit(solution)/shard_map/all_gather | solution.py:70
  127.0 2.7 copy.110
  135.1 5.3 copy.111
  140.5 3.9 bitcast_add_fusion.1
  146.4 2.8 maximum_maximum_fusion
  149.2 6.9 copy.115
  156.1 5.4 fusion.2
  163.9 11.7 %cholesky.253 = f32[128,128]{1,0:T(8,128)S(1)} custom-call(f32[128,128]{1,0:T(8,128)S(1)} %cholesky.661), custom_call_target="Cholesky" | custom-call | tf_op jit(solution)/shard_map/jit(cholesky)/cholesky | solution.py:94
  175.7 2.7 cholesky.282
  178.6 9.8 %custom-call.67 = f32[1,128,128]{1,2,0:T(8,128)S(1)} custom-call(f32[1,128,128]{2,1,0:T(8,128)S(1)} %copy.118), custom_call_target="InvertDiagBlocksLowerTriangular" | custom-call | tf_op jit(solution)/shard_map/jit(cholesky)/cholesky | solution.py:94
  192.5 11.7 %cholesky.275 = f32[128,128]{1,0:T(8,128)S(1)} custom-call(f32[128,128]{1,0:T(8,128)S(1)} %cholesky.665), custom_call_target="Cholesky" | custom-call | tf_op jit(solution)/shard_map/jit(cholesky)/cholesky | solution.py:94
  205.2 10.0 %custom-call.68 = f32[1,128,128]{1,2,0:T(8,128)S(1)} custom-call(f32[1,128,128]{2,1,0:T(8,128)S(1)} %copy.121), custom_call_target="InvertDiagBlocksLowerTriangular" | custom-call | tf_op jit(solution)/shard_map/jit(cholesky)/cholesky | solution.py:94
  218.7 11.7 %cholesky.528 = f32[128,128]{1,0:T(8,128)S(1)} custom-call(f32[128,128]{1,0:T(8,128)S(1)} %cholesky.670), custom_call_target="Cholesky" | custom-call | tf_op jit(solution)/shard_map/jit(cholesky)/cholesky | solution.py:94
  231.4 9.8 %custom-call.69 = f32[1,128,128]{1,2,0:T(8,128)S(1)} custom-call(f32[1,128,128]{2,1,0:T(8,128)S(1)} %copy.124), custom_call_target="InvertDiagBlocksLowerTriangular" | custom-call | tf_op jit(solution)/shard_map/jit(cholesky)/cholesky | solution.py:94
  245.0 11.9 %cholesky.547 = f32[128,128]{1,0:T(8,128)S(1)} custom-call(f32[128,128]{1,0:T(8,128)S(1)} %cholesky.675), custom_call_target="Cholesky" | custom-call | tf_op jit(solution)/shard_map/jit(cholesky)/cholesky | solution.py:94
  257.9 9.8 %custom-call.70 = f32[1,128,128]{1,2,0:T(8,128)S(1)} custom-call(f32[1,128,128]{2,1,0:T(8,128)S(1)} %copy.127), custom_call_target="InvertDiagBlocksLowerTriangular" | custom-call | tf_op jit(solution)/shard_map/jit(cholesky)/cholesky | solution.py:94
  268.8 2.7 fusion.8
  271.5 11.7 %cholesky.566 = f32[128,128]{1,0:T(8,128)S(1)} custom-call(f32[128,128]{1,0:T(8,128)S(1)} %cholesky.680), custom_call_target="Cholesky" | custom-call | tf_op jit(solution)/shard_map/jit(cholesky)/cholesky | solution.py:94
  284.2 10.2 %custom-call.71 = f32[1,128,128]{1,2,0:T(8,128)S(1)} custom-call(f32[1,128,128]{2,1,0:T(8,128)S(1)} %copy.130), custom_call_target="InvertDiagBlocksLowerTriangular" | custom-call | tf_op jit(solution)/shard_map/jit(cholesky)/cholesky | solution.py:94
  298.1 11.7 %cholesky.586 = f32[128,128]{1,0:T(8,128)S(1)} custom-call(f32[128,128]{1,0:T(8,128)S(1)} %cholesky.685), custom_call_target="Cholesky" | custom-call | tf_op jit(solution)/shard_map/jit(cholesky)/cholesky | solution.py:94
  310.8 9.8 %custom-call.72 = f32[1,128,128]{1,2,0:T(8,128)S(1)} custom-call(f32[1,128,128]{2,1,0:T(8,128)S(1)} %copy.133), custom_call_target="InvertDiagBlocksLowerTriangular" | custom-call | tf_op jit(solution)/shard_map/jit(cholesky)/cholesky | solution.py:94
  324.1 11.9 %cholesky.606 = f32[128,128]{1,0:T(8,128)S(1)} custom-call(f32[128,128]{1,0:T(8,128)S(1)} %cholesky.690), custom_call_target="Cholesky" | custom-call | tf_op jit(solution)/shard_map/jit(cholesky)/cholesky | solution.py:94
  336.9 9.8 %custom-call.73 = f32[1,128,128]{1,2,0:T(8,128)S(1)} custom-call(f32[1,128,128]{2,1,0:T(8,128)S(1)} %copy.136), custom_call_target="InvertDiagBlocksLowerTriangular" | custom-call | tf_op jit(solution)/shard_map/jit(cholesky)/cholesky | solution.py:94
  349.9 11.7 %cholesky.626 = f32[128,128]{1,0:T(8,128)S(1)} custom-call(f32[128,128]{1,0:T(8,128)S(1)} %cholesky.695), custom_call_target="Cholesky" | custom-call | tf_op jit(solution)/shard_map/jit(cholesky)/cholesky | solution.py:94
  362.6 9.8 %custom-call.74 = f32[1,128,128]{1,2,0:T(8,128)S(1)} custom-call(f32[1,128,128]{2,1,0:T(8,128)S(1)} %copy.139), custom_call_target="InvertDiagBlocksLowerTriangular" | custom-call | tf_op jit(solution)/shard_map/jit(cholesky)/cholesky | solution.py:94
  375.0 11.9 %cholesky.644 = f32[128,128]{1,0:T(8,128)S(1)} custom-call(f32[128,128]{1,0:T(8,128)S(1)} %convolution_subtract_fusion.4), custom_call_target="Cholesky" | custom-call | tf_op jit(solution)/shard_map/jit(cholesky)/cholesky | solution.py:94
  398.7 2.9 select_select_fusion
  403.5 70.2 %all-gather.12.cloned.1.call-done = f32[2048,1024]{1,0:T(8,128)} async-done(((f32[128,1024]{1,0:T(8,128)}), f32[2048,1024]{1,0:T(8,128)}) %all-gather.12.cloned.1.call-update) | async-done | bytes 8388624 | tf_op jit(solution)/shard_map/all_gather | solution.py:100
  473.8 6.2 gather_fusion
  480.0 2.7 broadcast_select_fusion.1
  495.4 3.2 fusion.29
  499.3 52.5 %all-gather.14.cloned.1.call-done = f32[1024,1024]{1,0:T(8,128)} async-done(((f32[128,1024]{1,0:T(8,128)}), f32[1024,1024]{1,0:T(8,128)}) %all-gather.14.cloned.1.call-update) | async-done | bytes 4194320 | tf_op jit(solution)/shard_map/all_gather | solution.py:113
  551.8 5.0 gather_fusion.1
  559.3 30.9 %bitcast_subtract_fusion = f32[8,4,256,256]{2,3,0,1:T(8,128)} fusion(f32[4,256,1024,1]{2,1,3,0:T(8,128)S(1)} %bitcast.142, f32[8,256,1024,1]{2,1,0,3:T(8,128)} %bitcast.131, f32[8,1,4,1,256,256]{4,5,0,2,3,1:T(8,128)} %copy.108), kind=kOutput, calls=%fused_computation.5 | convolution fusion | flops 25771900928 | bytes 29360128 | tf_op jit(solution)/shard_map/aik,bjk->abij/dot_general | solution.py:117
  590.2 7.9 %gather_fusion.2 = f32[4,8,256,256]{2,3,1,0:T(8,128)} fusion(f32[8,4,256,256]{2,3,0,1:T(8,128)} %bitcast_subtract_fusion, s32[1024]{0:T(1024)S(1)} %pad_clamp_fusion.2), kind=kCustom, calls=%fused_computation.4 | custom fusion | bytes 16777232 | tf_op jit(solution)/shard_map/jit(_take)/gather | solution.py:120
  598.0 7.9 %multiply_bitcast_fusion = f32[8,4,256,256]{2,3,0,1:T(8,128)} fusion(f32[4,8,256,256]{2,3,1,0:T(8,128)} %gather_fusion.2, f32[4]{0:T(128)S(1)} %get-tuple-element.61, pred[4]{0:T(512)(128)(4,1)S(1)} %compare_and_fusion.4), kind=kLoop, calls=%fused_computation.10 | loop fusion | flops 4194304 | bytes 16777236 | tf_op jit(solution)/shard_map/mul | solution.py:120
  606.0 7.9 %gather_fusion.3 = f32[8,4,256,256]{2,3,1,0:T(8,128)} fusion(f32[8,4,256,256]{2,3,0,1:T(8,128)} %multiply_bitcast_fusion, s32[1024]{0:T(1024)S(1)} %pad_clamp_fusion.1), kind=kCustom, calls=%fused_computation.clone | custom fusion | bytes 16777248 | tf_op jit(solution)/shard_map/jit(_take)/gather | solution.py:15
  613.8 7.8 %fusion.1 = f32[8,1,4,256,256]{3,4,2,1,0:T(8,128)} fusion(f32[8,4,256,256]{2,3,1,0:T(8,128)} %gather_fusion.3, f32[8]{0:T(128)S(1)} %get-tuple-element.60, pred[8]{0:T(512)(128)(4,1)S(1)} %get-tuple-element.59), kind=kLoop, calls=%fused_computation.9 | loop fusion | flops 4194304 | bytes 16777256 | tf_op jit(solution)/shard_map/reshape | solution.py:16
  621.7 5.5 all-to-all-start.1
  627.4 93.5 %all-to-all-done.1 = f32[8,1,4,256,256]{3,4,2,1,0:T(8,128)} async-done(((f32[8,1,4,256,256]{3,4,2,1,0:T(8,128)}), f32[8,1,4,256,256]{3,4,2,1,0:T(8,128)}, u32[]{:S(2)}, u32[]{:S(2)}) %all-to-all-start.1) | async-done | bytes 8388640 | tf_op jit(solution)/shard_map/all_to_all | solution.py:17
  720.9 7.9 %gather_fusion.4 = f32[8,4,256,256]{2,3,1,0:T(8,128)} fusion(f32[8,4,256,256]{2,3,1,0:T(8,128)} %bitcast.52, s32[1024]{0:T(1024)S(1)} %pad_clamp_fusion), kind=kCustom, calls=%fused_computation.1.clone | custom fusion | bytes 16777248 | tf_op jit(solution)/shard_map/jit(_take)/gather | solution.py:19
  728.8 7.8 %fusion = f32[8,1,4,1,256,256]{4,5,2,0,3,1:T(8,128)} fusion(f32[8,4,256,256]{2,3,1,0:T(8,128)} %gather_fusion.4, f32[8]{0:T(128)S(1)} %get-tuple-element.58, pred[8]{0:T(512)(128)(4,1)S(1)} %get-tuple-element.57), kind=kLoop, calls=%fused_computation.7 | loop fusion | flops 4194304 | bytes 16777256 | tf_op jit(solution)/shard_map/broadcast_in_dim | solution.py:122
  736.6 9.1 %copy.143 = f32[8,1,4,1,256,256]{5,4,3,2,1,0:T(8,128)} copy(f32[8,1,4,1,256,256]{4,5,2,0,3,1:T(8,128)} %fusion) | data formatting | bytes 16777216
  745.7 8.4 %copy.163 = f32[8,1,256,1024]{3,2,1,0:T(8,128)} copy(f32[8,1,256,1024]{3,2,1,0:T(8,128)} %bitcast.132) | data formatting | bytes 16777216
  (154 shorter events, 78.1 us)
Async XLA Ops:
  7.2 65.3 %all-gather.10.cloned.1.call-start = ((), (), s32[]{:S(2)}) async-start(), calls=%async_computation.2 | async-start | bytes 4456448 | tf_op jit(solution)/shard_map/all_gather | solution.py:69
  17.7 107.0 %all-gather.16.cloned.1.call-start = ((), (), s32[]{:S(2)}) async-start(), calls=%async_computation.5 | async-start | bytes 9437184 | tf_op jit(solution)/shard_map/all_gather | solution.py:70
  74.8 8.8 %copy-start.6 = (s32[60]{0:T(128)S(1)}, s32[60]{0:T(128)}, u32[]{:S(2)}) copy-start(s32[60]{0:T(128)} %param.7) | copy-start | bytes 724
  78.5 32.1 %all-to-all-start = ((f32[16,128,256]{2,1,0:T(8,128)}), f32[16,128,256]{2,1,0:T(8,128)S(1)}, u32[]{:S(2)}, u32[]{:S(2)}) async-start(f32[16,128,256]{2,1,0:T(8,128)} %bitcast.4), calls=%async_computation | async-start | bytes 4194304 | tf_op jit(solution)/shard_map/all_to_all | solution.py:77
  83.5 390.3 %all-gather.12.cloned.1.call-start = ((), (), s32[]{:S(2)}) async-start(), calls=%async_computation.3 | async-start | bytes 8912896 | tf_op jit(solution)/shard_map/all_gather | solution.py:100
  124.8 2.2 slice-start
  130.7 2.0 copy-start
  144.4 2.0 copy-start.1
  161.6 2.3 copy-start.3
  401.6 1.6 copy-start.7
  403.1 148.7 %all-gather.14.cloned.1.call-start = ((), (), s32[]{:S(2)}) async-start(), calls=%async_computation.4 | async-start | bytes 4718592 | tf_op jit(solution)/shard_map/all_gather | solution.py:113
  482.7 2.0 copy-start.2
  484.7 14.2 %copy-start.5 = (s32[60]{0:T(128)S(1)}, s32[60]{0:T(128)}, u32[]{:S(2)}) copy-start(s32[60]{0:T(128)} %param.8) | copy-start | bytes 724
  485.1 6.4 collective-permute-start
  486.4 6.6 collective-permute-start.1
  487.1 8.2 %collective-permute-start.2 = (f32[128,1024]{1,0:T(8,128)S(1)}, f32[128,1024]{1,0:T(8,128)}, u32[]{:S(2)}, u32[]{:S(2)}) collective-permute-start(f32[128,1024]{1,0:T(8,128)S(1)} %get-tuple-element.35), channel_id=1, source_target_pairs={{0,48},{17,65},{34,82},{51,99},{68,116},{85,5},{102,22},{119,39},{... | collective-permute-start | bytes 1572872 | tf_op jit(solution)/shard_map/ppermute | solution.py:112
  488.6 6.8 collective-permute-start.3
  490.1 5.3 collective-permute-start.4
  491.5 3.9 collective-permute-start.5
  493.1 0.8 copy-start.4
  493.9 1.5 collective-permute-start.6
  621.7 99.2 %all-to-all-start.1 = ((f32[8,1,4,256,256]{3,4,2,1,0:T(8,128)}), f32[8,1,4,256,256]{3,4,2,1,0:T(8,128)}, u32[]{:S(2)}, u32[]{:S(2)}) async-start(f32[8,1,4,256,256]{3,4,2,1,0:T(8,128)} %fusion.1), calls=%async_computation.1 | async-start | bytes 16777216 | tf_op jit(solution)/shard_map/all_to_all | solution.py:17
Sparse Core Ops, SparseCore 0:
  17.9 54.5 all-gather.9
  75.0 49.7 all-gather.15
  403.2 70.5 all-gather.11
  498.8 52.9 all-gather.13

commit v3 on v2

--- a/solution.py
+++ b/solution.py
@@ -100,25 +100,27 @@
     factor_rows = lax.all_gather(piece, "col").reshape(rows_dev, tile, lead_w)
 
     src_row = my_col % grid_rows
-    pick = jnp.arange(cols_dev, dtype=jnp.int32) * (grid_cols // grid_rows) + my_col // grid_rows
-    col_src = jnp.take(factor_rows, pick, axis=0).reshape(grid_rows, -1, lead_w)
-    rel = (my_row - src_row) % grid_rows
-    mine = jnp.where(rel == 0, col_src[0], 0.0)
-    for shift in range(1, grid_rows):
+    mine = None
+    for j in range(grid_rows):
         perm = []
         for c in range(grid_cols):
             s = c % grid_rows
-            perm.append((s * grid_cols + c, ((s + shift) % grid_rows) * grid_cols + c))
-        mine = mine + lax.ppermute(col_src[shift], ("row", "col"), perm)
+            source_col = 4 * (j // 2) + 2 * (c // grid_rows) + j % 2
+            perm.append((s * grid_cols + source_col, ((s + j) % grid_rows) * grid_cols + c))
+        moved = lax.ppermute(piece, ("row", "col"), perm)
+        mine = moved if mine is None else mine + moved
     spread = lax.all_gather(mine, "row")
     order = (src_row + jnp.arange(grid_rows, dtype=jnp.int32)) % grid_rows
-    col_factor = jnp.take(spread, order, axis=0).reshape(cols_dev, tile, lead_w)
+    col_factor = spread[order].reshape(cols_dev, tile, lead_w)
 
     prod = jnp.einsum("aik,bjk->abij", factor_rows, col_factor, precision=PRECISE)
-    schur = current - prod
+    schur = (current - prod).reshape((rows_dev * cols_dev,) + current.shape[2:])
 
-    permuted = jnp.take(schur, col_local, axis=1) * col_gain[None, :, None, None]
-    parent = route_rows(permuted, send_local, send_valid, recv_source, recv_valid, grid_rows)
+    flat_idx = send_local[:, None] * cols_dev + col_local[None, :]
+    keep = (send_valid[:, None] & col_valid[None, :])[:, :, None, None]
+    outgoing = jnp.where(keep, schur[flat_idx], 0.0)
+    incoming = lax.all_to_all(outgoing, "row", split_axis=0, concat_axis=0, tiled=True)
+    parent = jnp.where(recv_valid[:, None, None, None], incoming[recv_source], 0.0)
     return (factor_rows[:, None], parent[:, None, :, None])
 
 

time: 769 us -> 743 us (0.966)
  local copies, waits for them, and re-layouts: 108 us -> 90.4 us
  other arithmetic: 243 us -> 228 us
    gather x5 -> x3, local copies, waits for them, and re-layouts: 34.8 us -> 20.7 us  [the longest x1 7.86 us: local(): incoming[recv_source]]
    unnamed x20 -> x17, local copies, waits for them, and re-layouts: 36.4 us -> 24.4 us
    select_n x8 -> x5, other arithmetic: 5.28 us -> 16.1 us  [the longest x2 8.07 us: local(): outgoing = jnp.where(keep, schur[flat_idx], 0.0)]
    sub x0 -> x1, local copies, waits for them, and re-layouts: none -> 9.13 us  [local(): schur = (current - prod).reshape((rows_dev * cols_dev,) + current.shape[2:])]
    mul x1, other arithmetic: 7.93 us -> 0.01 us  [local(): flat_idx = send_local[:, None] * cols_dev + col_local[None, :]]
    broadcast_in_dim x1 -> x0, other arithmetic: 7.84 us -> none  [local(): return (factor_rows[:, None], parent[:, None, :, None])]
    reshape x1 -> x0, other arithmetic: 7.84 us -> none  [route_rows(): outgoing = outgoing.reshape((grid_rows, -1) + block_now.shape[1:])]
  transfers between devices with their start and end apart: 13 -> 14, of which waited for: 6 -> 8; matrix products, arithmetic and copies ran while one was open for 1% -> 2% of each run, Pallas kernels for 0% -> 0%
where the time goes in v3:
time: 743 us; the launch traced here: 735 us
  waiting for transfers between devices  316 us (43%)
  other arithmetic  228 us (31%)
  local copies, waits for them, and re-layouts  90.4 us (12%)
  matrix products  59.9 us (8%)
  between operations  21.7 us (3%)
  starting transfers between devices  19.6 us (3%)
    another operation x34, other arithmetic, local(): aug_factor = jnp.linalg.cholesky(aug)  191 us
    all_to_all x1, waiting for transfers between devices, local(): lax.all_to_all(outgoing, 'row', split_axis=0, concat_axis=0, tiled=True)  93.6 us
    all_gather x1, waiting for transfers between devices, local(): factor_rows = lax.all_gather(piece, 'col').reshape(rows_dev, tile, lead_w)  67.4 us
    all_gather x1, waiting for transfers between devices, local(): spread = lax.all_gather(mine, 'row')  55.5 us
    all_gather x1, waiting for transfers between devices, local(): row_tiles = lax.all_gather(lead_tile, 'col')[:LEAD]  54.7 us
    dot_general x1, matrix products, local(): jnp.einsum('aik,bjk->abij', factor_rows, col_factor, precision=PRECISE)  31.7 us
    another operation x16, matrix products, local(): aug_factor = jnp.linalg.cholesky(aug)  28.1 us
    all_to_all x1, waiting for transfers between devices, local(): lax.all_to_all(panel_col, 'col', split_axis=0, concat_axis=0, tiled=True)  25.6 us
  transfers between devices with their start and end apart: 14, of which 8 were waited for; matrix products, arithmetic and copies ran while one was open for 2% of the time, Pallas kernels for 0%

profile of v3, /device:TPU:1, one launch (start us, length us, event | category | flops | bytes accessed | tf_op | source)
XLA Modules:
  0.0 735.1 jit_solution(1929440740664225509)
XLA Ops:
  7.2 8.7 %copy.106 = f32[8,1,4,1,256,256]{4,5,0,2,3,1:T(8,128)} copy(f32[8,1,4,1,256,256]{5,4,3,2,1,0:T(8,128)} %param.4) | data formatting | bytes 16777216 | tf_op args[0]
  17.8 54.7 %all-gather.10.cloned.1.call-done = f32[16,1,256,256]{3,2,1,0:T(8,128)} async-done(((f32[1,1,256,256]{3,2,1,0:T(8,128)}), f32[16,1,256,256]{3,2,1,0:T(8,128)}) %all-gather.10.cloned.1.call-update) | async-done | bytes 4194320 | tf_op jit(solution)/shard_map/all_gather | solution.py:69
  78.5 5.0 all-to-all-start
  85.0 25.6 %all-to-all-done = f32[16,128,256]{2,1,0:T(8,128)S(1)} async-done(((f32[16,128,256]{2,1,0:T(8,128)}), f32[16,128,256]{2,1,0:T(8,128)S(1)}, u32[]{:S(2)}, u32[]{:S(2)}) %all-to-all-start) | async-done | bytes 2097184 | tf_op jit(solution)/shard_map/all_to_all | solution.py:77
  112.4 12.4 %all-gather.16.cloned.1.call-done = f32[32,1,256,256]{3,2,1,0:T(8,128)} async-done(((f32[4,1,256,256]{3,2,1,0:T(8,128)}), f32[32,1,256,256]{3,2,1,0:T(8,128)}) %all-gather.16.cloned.1.call-update) | async-done | bytes 8388624 | tf_op jit(solution)/shard_map/all_gather | solution.py:70
  127.0 2.7 copy.108
  135.1 5.3 copy.109
  140.5 3.9 bitcast_add_fusion.1
  146.4 2.8 maximum_maximum_fusion
  149.2 6.9 copy.113
  156.1 5.1 fusion
  163.5 11.7 %cholesky.253 = f32[128,128]{1,0:T(8,128)S(1)} custom-call(f32[128,128]{1,0:T(8,128)S(1)} %cholesky.661), custom_call_target="Cholesky" | custom-call | tf_op jit(solution)/shard_map/jit(cholesky)/cholesky | solution.py:94
  175.3 2.7 cholesky.282
  178.3 9.8 %custom-call.67 = f32[1,128,128]{1,2,0:T(8,128)S(1)} custom-call(f32[1,128,128]{2,1,0:T(8,128)S(1)} %copy.116), custom_call_target="InvertDiagBlocksLowerTriangular" | custom-call | tf_op jit(solution)/shard_map/jit(cholesky)/cholesky | solution.py:94
  192.1 11.7 %cholesky.275 = f32[128,128]{1,0:T(8,128)S(1)} custom-call(f32[128,128]{1,0:T(8,128)S(1)} %cholesky.665), custom_call_target="Cholesky" | custom-call | tf_op jit(solution)/shard_map/jit(cholesky)/cholesky | solution.py:94
  204.8 10.0 %custom-call.68 = f32[1,128,128]{1,2,0:T(8,128)S(1)} custom-call(f32[1,128,128]{2,1,0:T(8,128)S(1)} %copy.119), custom_call_target="InvertDiagBlocksLowerTriangular" | custom-call | tf_op jit(solution)/shard_map/jit(cholesky)/cholesky | solution.py:94
  218.4 11.7 %cholesky.528 = f32[128,128]{1,0:T(8,128)S(1)} custom-call(f32[128,128]{1,0:T(8,128)S(1)} %cholesky.670), custom_call_target="Cholesky" | custom-call | tf_op jit(solution)/shard_map/jit(cholesky)/cholesky | solution.py:94
  231.0 9.8 %custom-call.69 = f32[1,128,128]{1,2,0:T(8,128)S(1)} custom-call(f32[1,128,128]{2,1,0:T(8,128)S(1)} %copy.122), custom_call_target="InvertDiagBlocksLowerTriangular" | custom-call | tf_op jit(solution)/shard_map/jit(cholesky)/cholesky | solution.py:94
  242.1 2.6 convolution_subtract_fusion.2
  244.7 12.1 %cholesky.547 = f32[128,128]{1,0:T(8,128)S(1)} custom-call(f32[128,128]{1,0:T(8,128)S(1)} %cholesky.675), custom_call_target="Cholesky" | custom-call | tf_op jit(solution)/shard_map/jit(cholesky)/cholesky | solution.py:94
  257.7 9.8 %custom-call.70 = f32[1,128,128]{1,2,0:T(8,128)S(1)} custom-call(f32[1,128,128]{2,1,0:T(8,128)S(1)} %copy.125), custom_call_target="InvertDiagBlocksLowerTriangular" | custom-call | tf_op jit(solution)/shard_map/jit(cholesky)/cholesky | solution.py:94
  268.7 2.7 fusion.6
  271.4 11.7 %cholesky.566 = f32[128,128]{1,0:T(8,128)S(1)} custom-call(f32[128,128]{1,0:T(8,128)S(1)} %cholesky.680), custom_call_target="Cholesky" | custom-call | tf_op jit(solution)/shard_map/jit(cholesky)/cholesky | solution.py:94
  284.1 10.0 %custom-call.71 = f32[1,128,128]{1,2,0:T(8,128)S(1)} custom-call(f32[1,128,128]{2,1,0:T(8,128)S(1)} %copy.128), custom_call_target="InvertDiagBlocksLowerTriangular" | custom-call | tf_op jit(solution)/shard_map/jit(cholesky)/cholesky | solution.py:94
  295.1 2.6 fusion.12
  297.8 11.7 %cholesky.586 = f32[128,128]{1,0:T(8,128)S(1)} custom-call(f32[128,128]{1,0:T(8,128)S(1)} %cholesky.685), custom_call_target="Cholesky" | custom-call | tf_op jit(solution)/shard_map/jit(cholesky)/cholesky | solution.py:94
  310.4 9.8 %custom-call.72 = f32[1,128,128]{1,2,0:T(8,128)S(1)} custom-call(f32[1,128,128]{2,1,0:T(8,128)S(1)} %copy.131), custom_call_target="InvertDiagBlocksLowerTriangular" | custom-call | tf_op jit(solution)/shard_map/jit(cholesky)/cholesky | solution.py:94
  323.7 12.1 %cholesky.606 = f32[128,128]{1,0:T(8,128)S(1)} custom-call(f32[128,128]{1,0:T(8,128)S(1)} %cholesky.690), custom_call_target="Cholesky" | custom-call | tf_op jit(solution)/shard_map/jit(cholesky)/cholesky | solution.py:94
  336.8 9.8 %custom-call.73 = f32[1,128,128]{1,2,0:T(8,128)S(1)} custom-call(f32[1,128,128]{2,1,0:T(8,128)S(1)} %copy.134), custom_call_target="InvertDiagBlocksLowerTriangular" | custom-call | tf_op jit(solution)/shard_map/jit(cholesky)/cholesky | solution.py:94
  349.8 11.7 %cholesky.626 = f32[128,128]{1,0:T(8,128)S(1)} custom-call(f32[128,128]{1,0:T(8,128)S(1)} %cholesky.695), custom_call_target="Cholesky" | custom-call | tf_op jit(solution)/shard_map/jit(cholesky)/cholesky | solution.py:94
  362.5 9.8 %custom-call.74 = f32[1,128,128]{1,2,0:T(8,128)S(1)} custom-call(f32[1,128,128]{2,1,0:T(8,128)S(1)} %copy.137), custom_call_target="InvertDiagBlocksLowerTriangular" | custom-call | tf_op jit(solution)/shard_map/jit(cholesky)/cholesky | solution.py:94
  374.9 11.9 %cholesky.644 = f32[128,128]{1,0:T(8,128)S(1)} custom-call(f32[128,128]{1,0:T(8,128)S(1)} %convolution_subtract_fusion.4), custom_call_target="Cholesky" | custom-call | tf_op jit(solution)/shard_map/jit(cholesky)/cholesky | solution.py:94
  398.5 2.9 select_select_fusion
  402.1 3.2 collective-permute-start
  408.7 2.7 collective-permute-done
  412.1 3.7 collective-permute-done.1
  420.0 55.5 %all-gather.14.cloned.1.call-done = f32[1024,1024]{1,0:T(8,128)} async-done(((f32[128,1024]{1,0:T(8,128)}), f32[1024,1024]{1,0:T(8,128)}) %all-gather.14.cloned.1.call-update) | async-done | bytes 4194320 | tf_op jit(solution)/shard_map/all_gather | solution.py:112
  475.5 5.0 gather_fusion
  480.5 67.4 %all-gather.12.cloned.1.call-done = f32[2048,1024]{1,0:T(8,128)} async-done(((f32[128,1024]{1,0:T(8,128)}), f32[2048,1024]{1,0:T(8,128)}) %all-gather.12.cloned.1.call-update) | async-done | bytes 8388624 | tf_op jit(solution)/shard_map/all_gather | solution.py:100
  547.9 31.7 %bitcast_subtract_fusion = f32[8,4,256,256]{2,3,0,1:T(8,128)} fusion(f32[4,256,1024,1]{2,1,3,0:T(8,128)} %bitcast.106, f32[8,256,1024,1]{2,1,0,3:T(8,128)} %bitcast.100, f32[8,1,4,1,256,256]{4,5,0,2,3,1:T(8,128)} %copy.106), kind=kOutput, calls=%fused_computation.4 | convolution fusion | flops 25771900928 | bytes 29360128 | tf_op jit(solution)/shard_map/aik,bjk->abij/dot_general | solution.py:116
  579.6 9.1 %copy.139 = f32[8,4,256,256]{3,2,1,0:T(8,128)} copy(f32[8,4,256,256]{2,3,0,1:T(8,128)} %bitcast_subtract_fusion) | data formatting | bytes 16777216 | tf_op jit(solution)/shard_map/sub | solution.py:117
  588.7 7.9 %gather_fusion.1 = f32[32,256,256]{2,1,0:T(8,128)} fusion(f32[32,256,256]{2,1,0:T(8,128)} %bitcast.95, s32[1024]{0:T(1024)S(1)} %pad_clamp_fusion.1), kind=kCustom, calls=%fused_computation.1 | custom fusion | bytes 16777344 | tf_op jit(solution)/shard_map/gather | solution.py:121
  596.6 8.0 %broadcast_select_fusion = f32[8,4,256,256]{3,2,1,0:T(8,128)} fusion(f32[8,4,256,256]{3,2,1,0:T(8,128)} %bitcast.94, pred[8,4]{1,0:T(8,128)(4,1)S(1)} %broadcast_and_fusion), kind=kLoop, calls=%fused_computation.11 | loop fusion | flops 2097152 | bytes 16777248 | tf_op jit(solution)/shard_map/jit(_where)/select_n | solution.py:121
  604.6 5.7 all-to-all-start.1
  610.5 93.6 %all-to-all-done.1 = f32[8,4,256,256]{3,2,1,0:T(8,128)} async-done(((f32[8,4,256,256]{3,2,1,0:T(8,128)}), f32[8,4,256,256]{3,2,1,0:T(8,128)}, u32[]{:S(2)}, u32[]{:S(2)}) %all-to-all-start.1) | async-done | bytes 8388640 | tf_op jit(solution)/shard_map/all_to_all | solution.py:122
  704.1 7.9 %gather_fusion.2 = f32[8,4,256,256]{3,2,1,0:T(8,128)} fusion(f32[8,4,256,256]{3,2,1,0:T(8,128)} %all-to-all-done.1, s32[1024]{0:T(1024)S(1)} %pad_clamp_fusion), kind=kCustom, calls=%fused_computation.2 | custom fusion | bytes 16777248 | tf_op jit(solution)/shard_map/gather | solution.py:123
  711.9 8.0 %bitcast_select_fusion = f32[8,1,4,1,256,256]{5,4,3,2,1,0:T(8,128)} fusion(f32[8,4,256,256]{3,2,1,0:T(8,128)} %gather_fusion.2, pred[8]{0:T(512)(128)(4,1)S(1)} %broadcast_compare_fusion.2), kind=kLoop, calls=%fused_computation.3 | loop fusion | flops 2097152 | bytes 16777224 | tf_op jit(solution)/shard_map/jit(_where)/select_n | solution.py:123
  720.0 8.4 %copy.160 = f32[8,1,256,1024]{3,2,1,0:T(8,128)} copy(f32[8,1,256,1024]{3,2,1,0:T(8,128)} %bitcast.101) | data formatting | bytes 16777216
  (139 shorter events, 63.9 us)
Async XLA Ops:
  7.2 65.3 %all-gather.10.cloned.1.call-start = ((), (), s32[]{:S(2)}) async-start(), calls=%async_computation.2 | async-start | bytes 4456448 | tf_op jit(solution)/shard_map/all_gather | solution.py:69
  17.7 107.0 %all-gather.16.cloned.1.call-start = ((), (), s32[]{:S(2)}) async-start(), calls=%async_computation.5 | async-start | bytes 9437184 | tf_op jit(solution)/shard_map/all_gather | solution.py:70
  74.8 8.7 %copy-start.5 = (s32[60]{0:T(128)S(1)}, s32[60]{0:T(128)}, u32[]{:S(2)}) copy-start(s32[60]{0:T(128)} %param.5) | copy-start | bytes 724
  78.5 32.1 %all-to-all-start = ((f32[16,128,256]{2,1,0:T(8,128)}), f32[16,128,256]{2,1,0:T(8,128)S(1)}, u32[]{:S(2)}, u32[]{:S(2)}) async-start(f32[16,128,256]{2,1,0:T(8,128)} %bitcast.4), calls=%async_computation | async-start | bytes 4194304 | tf_op jit(solution)/shard_map/all_to_all | solution.py:77
  83.5 392.0 %all-gather.14.cloned.1.call-start = ((), (), s32[]{:S(2)}) async-start(), calls=%async_computation.4 | async-start | bytes 4718592 | tf_op jit(solution)/shard_map/all_gather | solution.py:112
  124.8 2.2 slice-start
  130.7 2.0 copy-start
  144.4 2.0 copy-start.1
  161.2 2.3 copy-start.2
  402.0 17.1 %copy-start.6 = (s32[60]{0:T(128)S(1)}, s32[60]{0:T(128)}, u32[]{:S(2)}) copy-start(s32[60]{0:T(128)} %param.7) | copy-start | bytes 724
  402.0 17.3 %copy-start.4 = (s32[60]{0:T(128)S(1)}, s32[60]{0:T(128)}, u32[]{:S(2)}) copy-start(s32[60]{0:T(128)} %param.6) | copy-start | bytes 724
  402.1 16.5 %copy-start.3 = (f32[128,1024]{1,0:T(8,128)}, f32[128,1024]{1,0:T(8,128)S(1)}, u32[]{:S(2)}) copy-start(f32[128,1024]{1,0:T(8,128)S(1)} %slice_select_fusion) | copy-start | bytes 1572868
  402.1 9.3 %collective-permute-start = (f32[128,1024]{1,0:T(8,128)S(1)}, f32[128,1024]{1,0:T(8,128)S(1)}, u32[]{:S(2)}, u32[]{:S(2)}) collective-permute-start(f32[128,1024]{1,0:T(8,128)S(1)} %slice_select_fusion), channel_id=1, source_target_pairs={{0,0},{16,17},{32,34},{48,51},{64,68},{80,85},{96,102},{112,119},{... | collective-permute-start | bytes 1572872 | tf_op jit(solution)/shard_map/ppermute | solution.py:110
  405.3 10.5 %collective-permute-start.1 = (f32[128,1024]{1,0:T(8,128)S(1)}, f32[128,1024]{1,0:T(8,128)S(1)}, u32[]{:S(2)}, u32[]{:S(2)}) collective-permute-start(f32[128,1024]{1,0:T(8,128)S(1)} %slice_select_fusion), channel_id=1, source_target_pairs={{1,16},{17,33},{33,50},{49,67},{65,84},{81,101},{97,118},{113,7},{... | collective-permute-start | bytes 1572872 | tf_op jit(solution)/shard_map/ppermute | solution.py:110
  406.6 9.9 %collective-permute-start.2 = (f32[128,1024]{1,0:T(8,128)S(1)}, f32[128,1024]{1,0:T(8,128)S(1)}, u32[]{:S(2)}, u32[]{:S(2)}) collective-permute-start(f32[128,1024]{1,0:T(8,128)S(1)} %slice_select_fusion), channel_id=1, source_target_pairs={{4,32},{20,49},{36,66},{52,83},{68,100},{84,117},{100,6},{116,23},... | collective-permute-start | bytes 1572872 | tf_op jit(solution)/shard_map/ppermute | solution.py:110
  407.3 9.9 %collective-permute-start.3 = (f32[128,1024]{1,0:T(8,128)S(1)}, f32[128,1024]{1,0:T(8,128)S(1)}, u32[]{:S(2)}, u32[]{:S(2)}) collective-permute-start(f32[128,1024]{1,0:T(8,128)S(1)} %slice_select_fusion), channel_id=1, source_target_pairs={{5,48},{21,65},{37,82},{53,99},{69,116},{85,5},{101,22},{117,39},{... | collective-permute-start | bytes 1572872 | tf_op jit(solution)/shard_map/ppermute | solution.py:110
  408.0 9.2 %collective-permute-start.4 = (f32[128,1024]{1,0:T(8,128)S(1)}, f32[128,1024]{1,0:T(8,128)S(1)}, u32[]{:S(2)}, u32[]{:S(2)}) collective-permute-start(f32[128,1024]{1,0:T(8,128)S(1)} %slice_select_fusion), channel_id=1, source_target_pairs={{8,64},{24,81},{40,98},{56,115},{72,4},{88,21},{104,38},{120,55},{... | collective-permute-start | bytes 1572872 | tf_op jit(solution)/shard_map/ppermute | solution.py:110
  411.4 5.9 collective-permute-start.5
  415.8 1.4 collective-permute-start.6
  416.5 0.7 collective-permute-start.7
  418.5 129.3 %all-gather.12.cloned.1.call-start = ((), (), s32[]{:S(2)}) async-start(), calls=%async_computation.3 | async-start | bytes 8912896 | tf_op jit(solution)/shard_map/all_gather | solution.py:100
  604.6 99.5 %all-to-all-start.1 = ((f32[8,4,256,256]{3,2,1,0:T(8,128)}), f32[8,4,256,256]{3,2,1,0:T(8,128)}, u32[]{:S(2)}, u32[]{:S(2)}) async-start(f32[8,4,256,256]{3,2,1,0:T(8,128)} %broadcast_select_fusion), calls=%async_computation.1 | async-start | bytes 16777216 | tf_op jit(solution)/shard_map/all_to_all | solution.py:122
Sparse Core Ops, SparseCore 0:
  17.9 54.5 all-gather.9
  75.0 49.7 all-gather.15
  418.6 56.8 all-gather.13
  477.5 70.3 all-gather.11

commit v4 on v3

--- a/solution.py
+++ b/solution.py
@@ -69,8 +69,6 @@
     row_tiles = lax.all_gather(lead_tile, "col")[:LEAD]
     lead_tiles = lax.all_gather(row_tiles, "row")[:LEAD]
     lead_block = lead_tiles.transpose(0, 2, 1, 3).reshape(lead_w, lead_w)
-    sym = jnp.tril(lead_block) + jnp.tril(lead_block, -1).T
-
     chunks = rows_dev * 2
     half = tile // 2
     panel_col = current[:, 0].reshape(chunks, half, tile)
@@ -86,12 +84,12 @@
     bound = 1.0 + 10.0 * jnp.sum(masked * masked)
     aug = jnp.concatenate(
         [
-            jnp.concatenate([sym, masked.T], axis=1),
+            jnp.concatenate([lead_block, jnp.zeros((lead_w, half), jnp.float32)], axis=1),
             jnp.concatenate([masked, jnp.where(jnp.eye(half, dtype=jnp.bool_), bound, 0.0)], axis=1),
         ],
         axis=0,
     )
-    aug_factor = jnp.linalg.cholesky(aug)
+    aug_factor = lax.linalg.cholesky(aug, symmetrize_input=False)
     chol = aug_factor[:lead_w, :lead_w]
     solved = aug_factor[lead_w:, :lead_w]
     start = jnp.clip(my_tile_row * tile + (my_col % 2) * half, 0, lead_w - half)
@@ -109,9 +107,18 @@
             perm.append((s * grid_cols + source_col, ((s + j) % grid_rows) * grid_cols + c))
         moved = lax.ppermute(piece, ("row", "col"), perm)
         mine = moved if mine is None else mine + moved
-    spread = lax.all_gather(mine, "row")
-    order = (src_row + jnp.arange(grid_rows, dtype=jnp.int32)) % grid_rows
-    col_factor = spread[order].reshape(cols_dev, tile, lead_w)
+    ring = [mine]
+    for step in range(1, grid_rows // 2):
+        perm = [(i, (i + 2 * step) % grid_rows) for i in range(grid_rows)]
+        ring.append(lax.ppermute(mine, "row", perm))
+    ring = jnp.stack(ring)
+    partner = lax.ppermute(ring, "row", [(i, i ^ 1) for i in range(grid_rows)])
+    combined = jnp.concatenate([ring, partner], axis=0)
+    chunk_ids = jnp.arange(grid_rows, dtype=jnp.int32)
+    own_d = (my_row - src_row - chunk_ids) % grid_rows
+    par_d = ((my_row ^ 1) - src_row - chunk_ids) % grid_rows
+    pos = jnp.where(own_d % 2 == 0, own_d // 2, grid_rows // 2 + par_d // 2)
+    col_factor = combined[pos].reshape(cols_dev, tile, lead_w)
 
     prod = jnp.einsum("aik,bjk->abij", factor_rows, col_factor, precision=PRECISE)
     schur = (current - prod).reshape((rows_dev * cols_dev,) + current.shape[2:])

time: 743 us -> 660 us (0.89)
  waiting for transfers between devices: 316 us -> 228 us
  starting transfers between devices: 19.6 us -> 46.4 us
  local copies, waits for them, and re-layouts: 90.4 us -> 76.3 us
  other arithmetic: 228 us -> 219 us
    all_gather x1, waiting for transfers between devices: 67.4 us -> 10.7 us  [local(): factor_rows = lax.all_gather(piece, 'col').reshape(rows_dev, tile, lead_w)]
    all_gather x1 -> x0, waiting for transfers between devices: 55.5 us -> none  [local(): spread = lax.all_gather(mine, 'row')]
    ppermute x0 -> x4, starting transfers between devices: none -> 26.8 us  [the longest x3 24.5 us: local(): ring.append(lax.ppermute(mine, 'row', perm))]
    ppermute x0 -> x4, waiting for transfers between devices: none -> 21.8 us  [the longest x3 21.8 us: local(): ring.append(lax.ppermute(mine, 'row', perm))]
    another operation x34 -> x35, other arithmetic: 191 us -> 195 us  [the longest x34 195 us: local(): aug_factor = lax.linalg.cholesky(aug, symmetrize_input=False)]
    unnamed x17 -> x20, local copies, waits for them, and re-layouts: 24.4 us -> 26 us
  transfers between devices with their start and end apart: 14 -> 17, of which waited for: 8 -> 10; matrix products, arithmetic and copies ran while one was open for 2% -> 3% of each run, Pallas kernels for 0% -> 0%
where the time goes in v4:
time: 660 us; the launch traced here: 649 us
  waiting for transfers between devices  228 us (35%)
  other arithmetic  219 us (33%)
  local copies, waits for them, and re-layouts  76.3 us (12%)
  matrix products  58.5 us (9%)
  starting transfers between devices  46.4 us (7%)
  between operations  21.6 us (3%)
    another operation x34, other arithmetic, local(): aug_factor = lax.linalg.cholesky(aug, symmetrize_input=False)  195 us
    all_to_all x1, waiting for transfers between devices, local(): lax.all_to_all(outgoing, 'row', split_axis=0, concat_axis=0, tiled=True)  93.6 us
    all_gather x1, waiting for transfers between devices, local(): row_tiles = lax.all_gather(lead_tile, 'col')[:LEAD]  54.7 us
    dot_general x1, matrix products, local(): jnp.einsum('aik,bjk->abij', factor_rows, col_factor, precision=PRECISE)  31.7 us
    another operation x16, matrix products, local(): aug_factor = lax.linalg.cholesky(aug, symmetrize_input=False)  26.8 us
    unnamed x20, local copies, waits for them, and re-layouts  26 us
    all_to_all x1, waiting for transfers between devices, local(): lax.all_to_all(panel_col, 'col', split_axis=0, concat_axis=0, tiled=True)  25.6 us
    ppermute x3, starting transfers between devices, local(): ring.append(lax.ppermute(mine, 'row', perm))  24.5 us
  transfers between devices with their start and end apart: 17, of which 10 were waited for; matrix products, arithmetic and copies ran while one was open for 3% of the time, Pallas kernels for 0%

profile of v4, /device:TPU:1, one launch (start us, length us, event | category | flops | bytes accessed | tf_op | source)
XLA Modules:
  0.0 649.0 jit_solution(5201733033821269030)
XLA Ops:
  7.2 8.7 %copy.22 = f32[8,1,4,1,256,256]{4,5,0,2,3,1:T(8,128)} copy(f32[8,1,4,1,256,256]{5,4,3,2,1,0:T(8,128)} %param.4) | data formatting | bytes 16777216 | tf_op args[0]
  17.8 54.7 %all-gather.8.cloned.1.call-done = f32[16,1,256,256]{3,2,1,0:T(8,128)} async-done(((f32[1,1,256,256]{3,2,1,0:T(8,128)}), f32[16,1,256,256]{3,2,1,0:T(8,128)}) %all-gather.8.cloned.1.call-update) | async-done | bytes 4194320 | tf_op jit(solution)/shard_map/all_gather | solution.py:69
  78.5 5.0 all-to-all-start
  85.0 25.6 %all-to-all-done = f32[16,128,256]{2,1,0:T(8,128)S(1)} async-done(((f32[16,128,256]{2,1,0:T(8,128)}), f32[16,128,256]{2,1,0:T(8,128)S(1)}, u32[]{:S(2)}, u32[]{:S(2)}) %all-to-all-start) | async-done | bytes 2097184 | tf_op jit(solution)/shard_map/all_to_all | solution.py:75
  112.0 12.7 %all-gather.12.cloned.1.call-done = f32[32,1,256,256]{3,2,1,0:T(8,128)} async-done(((f32[4,1,256,256]{3,2,1,0:T(8,128)}), f32[32,1,256,256]{3,2,1,0:T(8,128)}) %all-gather.12.cloned.1.call-update) | async-done | bytes 8388624 | tf_op jit(solution)/shard_map/all_gather | solution.py:70
  127.0 2.7 copy.24
  132.6 11.7 %cholesky.252 = f32[128,128]{1,0:T(8,128)S(1)} custom-call(f32[128,128]{1,0:T(8,128)S(1)} %cholesky.658), custom_call_target="Cholesky" | custom-call | tf_op jit(solution)/shard_map/cholesky | solution.py:92
  144.4 9.8 %custom-call.50 = f32[1,128,128]{1,2,0:T(8,128)S(1)} custom-call(f32[1,128,128]{2,1,0:T(8,128)S(1)} %get-tuple-element.57), custom_call_target="InvertDiagBlocksLowerTriangular" | custom-call | tf_op jit(solution)/shard_map/cholesky | solution.py:92
  154.2 3.0 cholesky.281
  162.2 11.7 %cholesky.274 = f32[128,128]{1,0:T(8,128)S(1)} custom-call(f32[128,128]{1,0:T(8,128)S(1)} %cholesky.662), custom_call_target="Cholesky" | custom-call | tf_op jit(solution)/shard_map/cholesky | solution.py:92
  174.6 9.8 %custom-call.51 = f32[1,128,128]{1,2,0:T(8,128)S(1)} custom-call(f32[1,128,128]{2,1,0:T(8,128)S(1)} %get-tuple-element.54), custom_call_target="InvertDiagBlocksLowerTriangular" | custom-call | tf_op jit(solution)/shard_map/cholesky | solution.py:92
  187.9 11.7 %cholesky.526 = f32[128,128]{1,0:T(8,128)S(1)} custom-call(f32[128,128]{1,0:T(8,128)S(1)} %cholesky.667), custom_call_target="Cholesky" | custom-call | tf_op jit(solution)/shard_map/cholesky | solution.py:92
  200.9 9.9 %custom-call.52 = f32[1,128,128]{1,2,0:T(8,128)S(1)} custom-call(f32[1,128,128]{2,1,0:T(8,128)S(1)} %get-tuple-element.51), custom_call_target="InvertDiagBlocksLowerTriangular" | custom-call | tf_op jit(solution)/shard_map/cholesky | solution.py:92
  212.1 2.6 convolution_subtract_fusion.2
  214.7 11.7 %cholesky.545 = f32[128,128]{1,0:T(8,128)S(1)} custom-call(f32[128,128]{1,0:T(8,128)S(1)} %cholesky.672), custom_call_target="Cholesky" | custom-call | tf_op jit(solution)/shard_map/cholesky | solution.py:92
  227.7 9.8 %custom-call.53 = f32[1,128,128]{1,2,0:T(8,128)S(1)} custom-call(f32[1,128,128]{2,1,0:T(8,128)S(1)} %get-tuple-element.48), custom_call_target="InvertDiagBlocksLowerTriangular" | custom-call | tf_op jit(solution)/shard_map/cholesky | solution.py:92
  238.7 2.7 fusion.4
  241.4 11.9 %cholesky.564 = f32[128,128]{1,0:T(8,128)S(1)} custom-call(f32[128,128]{1,0:T(8,128)S(1)} %cholesky.677), custom_call_target="Cholesky" | custom-call | tf_op jit(solution)/shard_map/cholesky | solution.py:92
  254.6 9.8 %custom-call.54 = f32[1,128,128]{1,2,0:T(8,128)S(1)} custom-call(f32[1,128,128]{2,1,0:T(8,128)S(1)} %get-tuple-element.45), custom_call_target="InvertDiagBlocksLowerTriangular" | custom-call | tf_op jit(solution)/shard_map/cholesky | solution.py:92
  265.4 2.6 fusion.10
  268.1 11.7 %cholesky.584 = f32[128,128]{1,0:T(8,128)S(1)} custom-call(f32[128,128]{1,0:T(8,128)S(1)} %cholesky.682), custom_call_target="Cholesky" | custom-call | tf_op jit(solution)/shard_map/cholesky | solution.py:92
  281.2 10.2 %custom-call.55 = f32[1,128,128]{1,2,0:T(8,128)S(1)} custom-call(f32[1,128,128]{2,1,0:T(8,128)S(1)} %get-tuple-element.42), custom_call_target="InvertDiagBlocksLowerTriangular" | custom-call | tf_op jit(solution)/shard_map/cholesky | solution.py:92
  292.4 2.5 fusion.13
  294.9 11.7 %cholesky.604 = f32[128,128]{1,0:T(8,128)S(1)} custom-call(f32[128,128]{1,0:T(8,128)S(1)} %cholesky.687), custom_call_target="Cholesky" | custom-call | tf_op jit(solution)/shard_map/cholesky | solution.py:92
  307.9 9.8 %custom-call.56 = f32[1,128,128]{1,2,0:T(8,128)S(1)} custom-call(f32[1,128,128]{2,1,0:T(8,128)S(1)} %get-tuple-element.39), custom_call_target="InvertDiagBlocksLowerTriangular" | custom-call | tf_op jit(solution)/shard_map/cholesky | solution.py:92
  320.8 11.8 %cholesky.624 = f32[128,128]{1,0:T(8,128)S(1)} custom-call(f32[128,128]{1,0:T(8,128)S(1)} %cholesky.692), custom_call_target="Cholesky" | custom-call | tf_op jit(solution)/shard_map/cholesky | solution.py:92
  334.0 9.8 %custom-call.57 = f32[1,128,128]{1,2,0:T(8,128)S(1)} custom-call(f32[1,128,128]{2,1,0:T(8,128)S(1)} %get-tuple-element.36), custom_call_target="InvertDiagBlocksLowerTriangular" | custom-call | tf_op jit(solution)/shard_map/cholesky | solution.py:92
  346.5 11.7 %cholesky.641 = f32[128,128]{1,0:T(8,128)S(1)} custom-call(f32[128,128]{1,0:T(8,128)S(1)} %convolution_subtract_fusion.4), custom_call_target="Cholesky" | custom-call | tf_op jit(solution)/shard_map/cholesky | solution.py:92
  365.7 2.9 select_select_fusion
  370.2 3.2 collective-permute-start
  376.8 2.9 collective-permute-done
  380.5 5.6 collective-permute-done.1
  388.9 6.7 %collective-permute-start.8 = (f32[128,1024]{1,0:T(8,128)S(1)}, f32[128,1024]{1,0:T(8,128)S(1)}, u32[]{:S(2)}, u32[]{:S(2)}) collective-permute-start(f32[128,1024]{1,0:T(8,128)S(1)} %get-tuple-element.30), channel_id=1, source_target_pairs={{0,32},{16,48},{32,64},{48,80},{64,96},{80,112},{96,0},{112,16},{1... | collective-permute-start | bytes 1572872 | tf_op jit(solution)/shard_map/ppermute | solution.py:113
  395.7 17.8 %collective-permute-start.9 = (f32[128,1024]{1,0:T(8,128)S(1)}, f32[128,1024]{1,0:T(8,128)S(1)}, u32[]{:S(2)}, u32[]{:S(2)}) collective-permute-start(f32[128,1024]{1,0:T(8,128)S(1)} %get-tuple-element.30), channel_id=1, source_target_pairs={{0,64},{16,80},{32,96},{48,112},{64,0},{80,16},{96,32},{112,48},{1... | collective-permute-start | bytes 1572872 | tf_op jit(solution)/shard_map/ppermute | solution.py:113
  413.6 9.3 %collective-permute-done.8 = f32[128,1024]{1,0:T(8,128)S(1)} collective-permute-done((f32[128,1024]{1,0:T(8,128)S(1)}, f32[128,1024]{1,0:T(8,128)S(1)}, u32[]{:S(2)}, u32[]{:S(2)}) %collective-permute-start.8) | collective-permute-done | bytes 524320 | tf_op jit(solution)/shard_map/ppermute | solution.py:113
  423.0 12.1 %collective-permute-done.9 = f32[128,1024]{1,0:T(8,128)S(1)} collective-permute-done((f32[128,1024]{1,0:T(8,128)S(1)}, f32[128,1024]{1,0:T(8,128)S(1)}, u32[]{:S(2)}, u32[]{:S(2)}) %collective-permute-start.9) | collective-permute-done | bytes 524320 | tf_op jit(solution)/shard_map/ppermute | solution.py:113
  442.6 3.2 constant_dynamic-update-slice_fusion
  445.9 5.0 gather_fusion
  450.8 10.7 %all-gather.10.cloned.1.call-done = f32[2048,1024]{1,0:T(8,128)} async-done(((f32[128,1024]{1,0:T(8,128)}), f32[2048,1024]{1,0:T(8,128)}) %all-gather.10.cloned.1.call-update) | async-done | bytes 8388624 | tf_op jit(solution)/shard_map/all_gather | solution.py:98
  461.5 31.7 %bitcast_subtract_fusion = f32[8,4,256,256]{2,3,0,1:T(8,128)} fusion(f32[4,256,1024,1]{2,1,3,0:T(8,128)} %bitcast.102, f32[8,256,1024,1]{2,1,0,3:T(8,128)} %bitcast.100, f32[8,1,4,1,256,256]{4,5,0,2,3,1:T(8,128)} %copy.22), kind=kOutput, calls=%fused_computation.4 | convolution fusion | flops 25771900928 | bytes 29360128 | tf_op jit(solution)/shard_map/aik,bjk->abij/dot_general | solution.py:123
  493.3 9.1 %copy.27 = f32[8,4,256,256]{3,2,1,0:T(8,128)} copy(f32[8,4,256,256]{2,3,0,1:T(8,128)} %bitcast_subtract_fusion) | data formatting | bytes 16777216 | tf_op jit(solution)/shard_map/sub | solution.py:124
  502.4 7.9 %gather_fusion.1 = f32[32,256,256]{2,1,0:T(8,128)} fusion(f32[32,256,256]{2,1,0:T(8,128)} %bitcast.93, s32[1024]{0:T(1024)S(1)} %pad_clamp_fusion.1), kind=kCustom, calls=%fused_computation.1 | custom fusion | bytes 16777344 | tf_op jit(solution)/shard_map/gather | solution.py:128
  510.3 8.0 %broadcast_select_fusion = f32[8,4,256,256]{3,2,1,0:T(8,128)} fusion(f32[8,4,256,256]{3,2,1,0:T(8,128)} %bitcast.92, pred[8,4]{1,0:T(8,128)(4,1)S(1)} %broadcast_and_fusion), kind=kLoop, calls=%fused_computation.9 | loop fusion | flops 2097152 | bytes 16777248 | tf_op jit(solution)/shard_map/jit(_where)/select_n | solution.py:128
  518.3 5.8 all-to-all-start.1
  524.2 93.6 %all-to-all-done.1 = f32[8,4,256,256]{3,2,1,0:T(8,128)} async-done(((f32[8,4,256,256]{3,2,1,0:T(8,128)}), f32[8,4,256,256]{3,2,1,0:T(8,128)}, u32[]{:S(2)}, u32[]{:S(2)}) %all-to-all-start.1) | async-done | bytes 8388640 | tf_op jit(solution)/shard_map/all_to_all | solution.py:129
  617.8 7.9 %gather_fusion.2 = f32[8,4,256,256]{3,2,1,0:T(8,128)} fusion(f32[8,4,256,256]{3,2,1,0:T(8,128)} %all-to-all-done.1, s32[1024]{0:T(1024)S(1)} %pad_clamp_fusion), kind=kCustom, calls=%fused_computation.2 | custom fusion | bytes 16777248 | tf_op jit(solution)/shard_map/gather | solution.py:130
  625.6 8.0 %bitcast_select_fusion = f32[8,1,4,1,256,256]{5,4,3,2,1,0:T(8,128)} fusion(f32[8,4,256,256]{3,2,1,0:T(8,128)} %gather_fusion.2, pred[8]{0:T(512)(128)(4,1)S(1)} %broadcast_compare_fusion.2), kind=kLoop, calls=%fused_computation.3 | loop fusion | flops 2097152 | bytes 16777224 | tf_op jit(solution)/shard_map/jit(_where)/select_n | solution.py:130
  633.7 8.4 %copy.53 = f32[8,1,256,1024]{3,2,1,0:T(8,128)} copy(f32[8,1,256,1024]{3,2,1,0:T(8,128)} %bitcast.101) | data formatting | bytes 16777216
  (117 shorter events, 60.0 us)
Async XLA Ops:
  7.2 65.3 %all-gather.8.cloned.1.call-start = ((), (), s32[]{:S(2)}) async-start(), calls=%async_computation.2 | async-start | bytes 4456448 | tf_op jit(solution)/shard_map/all_gather | solution.py:69
  17.7 107.0 %all-gather.12.cloned.1.call-start = ((), (), s32[]{:S(2)}) async-start(), calls=%async_computation.4 | async-start | bytes 9437184 | tf_op jit(solution)/shard_map/all_gather | solution.py:70
  74.8 8.7 %copy-start.5 = (s32[60]{0:T(128)S(1)}, s32[60]{0:T(128)}, u32[]{:S(2)}) copy-start(s32[60]{0:T(128)} %param.5) | copy-start | bytes 724
  78.5 32.1 %all-to-all-start = ((f32[16,128,256]{2,1,0:T(8,128)}), f32[16,128,256]{2,1,0:T(8,128)S(1)}, u32[]{:S(2)}, u32[]{:S(2)}) async-start(f32[16,128,256]{2,1,0:T(8,128)} %bitcast.3), calls=%async_computation | async-start | bytes 4194304 | tf_op jit(solution)/shard_map/all_to_all | solution.py:75
  83.5 378.0 %all-gather.10.cloned.1.call-start = ((), (), s32[]{:S(2)}) async-start(), calls=%async_computation.3 | async-start | bytes 8912896 | tf_op jit(solution)/shard_map/all_gather | solution.py:98
  124.8 2.2 slice-start
  130.7 1.9 copy-start
  154.2 4.1 copy-start.1
  158.7 2.5 copy-start.2
  368.6 18.8 %copy-start.4 = (s32[60]{0:T(128)S(1)}, s32[60]{0:T(128)}, u32[]{:S(2)}) copy-start(s32[60]{0:T(128)} %param.6) | copy-start | bytes 724
  368.6 18.9 %copy-start.6 = (s32[60]{0:T(128)S(1)}, s32[60]{0:T(128)}, u32[]{:S(2)}) copy-start(s32[60]{0:T(128)} %param.7) | copy-start | bytes 724
  370.2 9.6 %collective-permute-start = (f32[128,1024]{1,0:T(8,128)}, f32[128,1024]{1,0:T(8,128)S(1)}, u32[]{:S(2)}, u32[]{:S(2)}) collective-permute-start(f32[128,1024]{1,0:T(8,128)} %slice_select_fusion), channel_id=1, source_target_pairs={{0,0},{16,17},{32,34},{48,51},{64,68},{80,85},{96,102},{112,119},{... | collective-permute-start | bytes 1572872 | tf_op jit(solution)/shard_map/ppermute | solution.py:108
  373.4 12.7 %collective-permute-start.1 = (f32[128,1024]{1,0:T(8,128)}, f32[128,1024]{1,0:T(8,128)S(1)}, u32[]{:S(2)}, u32[]{:S(2)}) collective-permute-start(f32[128,1024]{1,0:T(8,128)} %slice_select_fusion), channel_id=1, source_target_pairs={{1,16},{17,33},{33,50},{49,67},{65,84},{81,101},{97,118},{113,7},{... | collective-permute-start | bytes 1572872 | tf_op jit(solution)/shard_map/ppermute | solution.py:108
  374.7 12.0 %collective-permute-start.2 = (f32[128,1024]{1,0:T(8,128)}, f32[128,1024]{1,0:T(8,128)S(1)}, u32[]{:S(2)}, u32[]{:S(2)}) collective-permute-start(f32[128,1024]{1,0:T(8,128)} %slice_select_fusion), channel_id=1, source_target_pairs={{4,32},{20,49},{36,66},{52,83},{68,100},{84,117},{100,6},{116,23},... | collective-permute-start | bytes 1572872 | tf_op jit(solution)/shard_map/ppermute | solution.py:108
  375.4 12.3 %collective-permute-start.3 = (f32[128,1024]{1,0:T(8,128)}, f32[128,1024]{1,0:T(8,128)S(1)}, u32[]{:S(2)}, u32[]{:S(2)}) collective-permute-start(f32[128,1024]{1,0:T(8,128)} %slice_select_fusion), channel_id=1, source_target_pairs={{5,48},{21,65},{37,82},{53,99},{69,116},{85,5},{101,22},{117,39},{... | collective-permute-start | bytes 1572872 | tf_op jit(solution)/shard_map/ppermute | solution.py:108
  376.1 11.6 %collective-permute-start.4 = (f32[128,1024]{1,0:T(8,128)}, f32[128,1024]{1,0:T(8,128)S(1)}, u32[]{:S(2)}, u32[]{:S(2)}) collective-permute-start(f32[128,1024]{1,0:T(8,128)} %slice_select_fusion), channel_id=1, source_target_pairs={{8,64},{24,81},{40,98},{56,115},{72,4},{88,21},{104,38},{120,55},{... | collective-permute-start | bytes 1572872 | tf_op jit(solution)/shard_map/ppermute | solution.py:108
  379.8 7.9 %collective-permute-start.5 = (f32[128,1024]{1,0:T(8,128)}, f32[128,1024]{1,0:T(8,128)S(1)}, u32[]{:S(2)}, u32[]{:S(2)}) collective-permute-start(f32[128,1024]{1,0:T(8,128)} %slice_select_fusion), channel_id=1, source_target_pairs={{9,80},{25,97},{41,114},{57,3},{73,20},{89,37},{105,54},{121,71},{... | collective-permute-start | bytes 1572872 | tf_op jit(solution)/shard_map/ppermute | solution.py:108
  386.1 1.7 collective-permute-start.6
  386.8 1.0 collective-permute-start.7
  388.9 34.0 %collective-permute-start.8 = (f32[128,1024]{1,0:T(8,128)S(1)}, f32[128,1024]{1,0:T(8,128)S(1)}, u32[]{:S(2)}, u32[]{:S(2)}) collective-permute-start(f32[128,1024]{1,0:T(8,128)S(1)} %get-tuple-element.30), channel_id=1, source_target_pairs={{0,32},{16,48},{32,64},{48,80},{64,96},{80,112},{96,0},{112,16},{1... | collective-permute-start | bytes 1572872 | tf_op jit(solution)/shard_map/ppermute | solution.py:113
  395.7 39.4 %collective-permute-start.9 = (f32[128,1024]{1,0:T(8,128)S(1)}, f32[128,1024]{1,0:T(8,128)S(1)}, u32[]{:S(2)}, u32[]{:S(2)}) collective-permute-start(f32[128,1024]{1,0:T(8,128)S(1)} %get-tuple-element.30), channel_id=1, source_target_pairs={{0,64},{16,80},{32,96},{48,112},{64,0},{80,16},{96,32},{112,48},{1... | collective-permute-start | bytes 1572872 | tf_op jit(solution)/shard_map/ppermute | solution.py:113
  413.5 22.0 %collective-permute-start.10 = (f32[128,1024]{1,0:T(8,128)S(1)}, f32[128,1024]{1,0:T(8,128)S(1)}, u32[]{:S(2)}, u32[]{:S(2)}) collective-permute-start(f32[128,1024]{1,0:T(8,128)S(1)} %get-tuple-element.30), channel_id=1, source_target_pairs={{0,96},{16,112},{32,0},{48,16},{64,32},{80,48},{96,64},{112,80},{1... | collective-permute-start | bytes 1572872 | tf_op jit(solution)/shard_map/ppermute | solution.py:113
  435.5 0.8 copy-start.3
  436.3 6.3 collective-permute-start.11
  518.3 99.5 %all-to-all-start.1 = ((f32[8,4,256,256]{3,2,1,0:T(8,128)}), f32[8,4,256,256]{3,2,1,0:T(8,128)}, u32[]{:S(2)}, u32[]{:S(2)}) async-start(f32[8,4,256,256]{3,2,1,0:T(8,128)} %broadcast_select_fusion), calls=%async_computation.1 | async-start | bytes 16777216 | tf_op jit(solution)/shard_map/all_to_all | solution.py:129
Sparse Core Ops, SparseCore 0:
  17.9 54.5 all-gather.7
  75.0 49.7 all-gather.11
  370.3 91.1 all-gather.9

commit v5 on v4

--- a/solution.py
+++ b/solution.py
@@ -17,6 +17,20 @@
     incoming = lax.all_to_all(outgoing, "row", split_axis=0, concat_axis=0, tiled=True)
     incoming = incoming.reshape((-1,) + block_now.shape[1:])
     return jnp.take(incoming, recv_source, axis=0) * valid_gain(recv_valid, block_now.ndim)
+
+
+def spread_from_first_four(x, axis, size):
+    idx = lax.axis_index(axis)
+    held = jnp.where(idx < LEAD, x, 0.0)
+    for q in range(1, size // LEAD):
+        held = held + lax.ppermute(x, axis, [(j, j + LEAD * q) for j in range(LEAD)])
+    parts = [held]
+    for k in range(1, LEAD):
+        perm = [(i, LEAD * (i // LEAD) + (i % LEAD + k) % LEAD) for i in range(size)]
+        parts.append(lax.ppermute(held, axis, perm))
+    parts = jnp.stack(parts)
+    order = (idx % LEAD - jnp.arange(LEAD, dtype=jnp.int32)) % LEAD
+    return parts[order]
 
 
 def local(front, tile_live, row_target, col_target):
@@ -66,9 +80,9 @@
     col_gain = col_valid.astype(jnp.float32)
 
     lead_tile = current[0, 0]
-    row_tiles = lax.all_gather(lead_tile, "col")[:LEAD]
-    lead_tiles = lax.all_gather(row_tiles, "row")[:LEAD]
-    lead_block = lead_tiles.transpose(0, 2, 1, 3).reshape(lead_w, lead_w)
+    col_tiles = spread_from_first_four(lead_tile, "row", grid_rows)
+    lead_tiles = spread_from_first_four(col_tiles, "col", grid_cols)
+    lead_block = lead_tiles.transpose(1, 2, 0, 3).reshape(lead_w, lead_w)
     chunks = rows_dev * 2
     half = tile // 2
     panel_col = current[:, 0].reshape(chunks, half, tile)

time: 660 us -> 695 us (1.053)
  starting transfers between devices: 46.4 us -> 68 us
  other arithmetic: 219 us -> 229 us
    ppermute x0 -> x10, waiting for transfers between devices: none -> 76.8 us  [the longest x6 41.9 us: spread_from_first_four(): parts.append(lax.ppermute(held, axis, perm))]
    all_gather x2 -> x0, waiting for transfers between devices: 67.4 us -> none  [the longest x1 54.7 us: local(): row_tiles = lax.all_gather(lead_tile, 'col')[:LEAD]]
    ppermute x0 -> x10, starting transfers between devices: none -> 23.3 us  [the longest x4 15.2 us: spread_from_first_four(): lax.ppermute(x, axis, [(j, j + LEAD * q) for j in range(LEAD)])]
    all_to_all x1, waiting for transfers between devices: 25.6 us -> 13.5 us  [local(): lax.all_to_all(panel_col, 'col', split_axis=0, concat_axis=0, tiled=True)]
    slice x6 -> x0, local copies, waits for them, and re-layouts: 9.07 us -> none  [the longest x3 4.89 us: local(): lead_tiles = lax.all_gather(row_tiles, 'row')[:LEAD]]
    all_gather x1, waiting for transfers between devices: 10.7 us -> 17.7 us  [local(): factor_rows = lax.all_gather(piece, 'col').reshape(rows_dev, tile, lead_w)]
    unnamed x20 -> x18, local copies, waits for them, and re-layouts: 26 us -> 27.2 us
  transfers between devices with their start and end apart: 17 -> 25, of which waited for: 10 -> 15; matrix products, arithmetic and copies ran while one was open for 3% -> 3% of each run, Pallas kernels for 0% -> 0%
where the time goes in v5:
time: 695 us; the launch traced here: 689 us
  waiting for transfers between devices  231 us (33%)
  other arithmetic  229 us (33%)
  local copies, waits for them, and re-layouts  80.2 us (12%)
  starting transfers between devices  68 us (10%)
  matrix products  58.7 us (8%)
  between operations  21.9 us (3%)
    another operation x34, other arithmetic, local(): aug_factor = lax.linalg.cholesky(aug, symmetrize_input=False)  195 us
    all_to_all x1, waiting for transfers between devices, local(): lax.all_to_all(outgoing, 'row', split_axis=0, concat_axis=0, tiled=True)  93.6 us
    ppermute x6, waiting for transfers between devices, spread_from_first_four(): parts.append(lax.ppermute(held, axis, perm))  41.9 us
    ppermute x4, waiting for transfers between devices, spread_from_first_four(): lax.ppermute(x, axis, [(j, j + LEAD * q) for j in range(LEAD)])  34.9 us
    dot_general x1, matrix products, local(): jnp.einsum('aik,bjk->abij', factor_rows, col_factor, precision=PRECISE)  32 us
    unnamed x18, local copies, waits for them, and re-layouts  27.2 us
    another operation x16, matrix products, local(): aug_factor = lax.linalg.cholesky(aug, symmetrize_input=False)  26.7 us
    ppermute x3, starting transfers between devices, local(): ring.append(lax.ppermute(mine, 'row', perm))  25.7 us
  transfers between devices with their start and end apart: 25, of which 15 were waited for; matrix products, arithmetic and copies ran while one was open for 3% of the time, Pallas kernels for 0%

profile of v5, /device:TPU:1, one launch (start us, length us, event | category | flops | bytes accessed | tf_op | source)
XLA Modules:
  0.0 688.7 jit_solution(10515350984584599936)
XLA Ops:
  7.2 8.7 %copy.15 = f32[8,1,4,1,256,256]{4,5,0,2,3,1:T(8,128)} copy(f32[8,1,4,1,256,256]{5,4,3,2,1,0:T(8,128)} %param.4) | data formatting | bytes 16777216 | tf_op args[0]
  16.8 5.5 collective-permute-start
  22.3 4.9 collective-permute-done
  31.2 4.3 collective-permute-done.1
  35.5 7.2 %collective-permute-done.2 = f32[256,256]{0,1:T(8,128)S(1)} collective-permute-done((f32[256,256]{0,1:T(8,128)S(1)}, f32[256,256]{0,1:T(8,128)S(1)}, u32[]{:S(2)}, u32[]{:S(2)}) %collective-permute-start.2) | collective-permute-done | bytes 262176 | tf_op jit(solution)/shard_map/ppermute | solution.py:30
  44.1 4.2 collective-permute-start.4
  57.5 5.3 all-to-all-start
  62.8 7.4 %collective-permute-done.4 = f32[4,256,256]{1,2,0:T(8,128)} collective-permute-done((f32[4,256,256]{1,2,0:T(8,128)S(1)}, f32[4,256,256]{1,2,0:T(8,128)}, u32[]{:S(2)}, u32[]{:S(2)}) %collective-permute-start.4) | collective-permute-done | bytes 1048608 | tf_op jit(solution)/shard_map/ppermute | solution.py:26
  70.3 22.5 %collective-permute-done.5 = f32[4,256,256]{1,2,0:T(8,128)} collective-permute-done((f32[4,256,256]{1,2,0:T(8,128)S(1)}, f32[4,256,256]{1,2,0:T(8,128)}, u32[]{:S(2)}, u32[]{:S(2)}) %collective-permute-start.5) | collective-permute-done | bytes 1048608 | tf_op jit(solution)/shard_map/ppermute | solution.py:26
  94.9 3.8 collective-permute-start.9
  101.3 13.5 %all-to-all-done = f32[16,128,256]{2,1,0:T(8,128)} async-done(((f32[16,128,256]{2,1,0:T(8,128)}), f32[16,128,256]{2,1,0:T(8,128)}, u32[]{:S(2)}, u32[]{:S(2)}) %all-to-all-start) | async-done | bytes 2097184 | tf_op jit(solution)/shard_map/all_to_all | solution.py:89
  117.3 26.3 %collective-permute-done.9 = f32[4,256,256]{1,2,0:T(8,128)S(1)} collective-permute-done((f32[4,256,256]{1,2,0:T(8,128)S(1)}, f32[4,256,256]{1,2,0:T(8,128)S(1)}, u32[]{:S(2)}, u32[]{:S(2)}) %collective-permute-start.9) | collective-permute-done | bytes 1048608 | tf_op jit(solution)/shard_map/ppermute | solution.py:30
  147.1 4.0 pad_maximum_fusion
  151.0 4.9 gather_fusion.1
  156.0 5.7 copy.16
  166.8 11.7 %cholesky.252 = f32[128,128]{1,0:T(8,128)S(1)} custom-call(f32[128,128]{1,0:T(8,128)S(1)} %cholesky.658), custom_call_target="Cholesky" | custom-call | tf_op jit(solution)/shard_map/cholesky | solution.py:106
  181.2 9.8 %custom-call.50 = f32[1,128,128]{1,2,0:T(8,128)S(1)} custom-call(f32[1,128,128]{2,1,0:T(8,128)S(1)} %get-tuple-element.55), custom_call_target="InvertDiagBlocksLowerTriangular" | custom-call | tf_op jit(solution)/shard_map/cholesky | solution.py:106
  196.8 11.9 %cholesky.274 = f32[128,128]{1,0:T(8,128)S(1)} custom-call(f32[128,128]{1,0:T(8,128)S(1)} %cholesky.662), custom_call_target="Cholesky" | custom-call | tf_op jit(solution)/shard_map/cholesky | solution.py:106
  209.3 9.8 %custom-call.51 = f32[1,128,128]{1,2,0:T(8,128)S(1)} custom-call(f32[1,128,128]{2,1,0:T(8,128)S(1)} %get-tuple-element.52), custom_call_target="InvertDiagBlocksLowerTriangular" | custom-call | tf_op jit(solution)/shard_map/cholesky | solution.py:106
  222.7 11.7 %cholesky.526 = f32[128,128]{1,0:T(8,128)S(1)} custom-call(f32[128,128]{1,0:T(8,128)S(1)} %cholesky.667), custom_call_target="Cholesky" | custom-call | tf_op jit(solution)/shard_map/cholesky | solution.py:106
  235.7 9.8 %custom-call.52 = f32[1,128,128]{1,2,0:T(8,128)S(1)} custom-call(f32[1,128,128]{2,1,0:T(8,128)S(1)} %get-tuple-element.49), custom_call_target="InvertDiagBlocksLowerTriangular" | custom-call | tf_op jit(solution)/shard_map/cholesky | solution.py:106
  249.3 11.9 %cholesky.545 = f32[128,128]{1,0:T(8,128)S(1)} custom-call(f32[128,128]{1,0:T(8,128)S(1)} %cholesky.672), custom_call_target="Cholesky" | custom-call | tf_op jit(solution)/shard_map/cholesky | solution.py:106
  262.5 9.8 %custom-call.53 = f32[1,128,128]{1,2,0:T(8,128)S(1)} custom-call(f32[1,128,128]{2,1,0:T(8,128)S(1)} %get-tuple-element.46), custom_call_target="InvertDiagBlocksLowerTriangular" | custom-call | tf_op jit(solution)/shard_map/cholesky | solution.py:106
  276.2 11.7 %cholesky.564 = f32[128,128]{1,0:T(8,128)S(1)} custom-call(f32[128,128]{1,0:T(8,128)S(1)} %cholesky.677), custom_call_target="Cholesky" | custom-call | tf_op jit(solution)/shard_map/cholesky | solution.py:106
  289.2 10.2 %custom-call.54 = f32[1,128,128]{1,2,0:T(8,128)S(1)} custom-call(f32[1,128,128]{2,1,0:T(8,128)S(1)} %get-tuple-element.43), custom_call_target="InvertDiagBlocksLowerTriangular" | custom-call | tf_op jit(solution)/shard_map/cholesky | solution.py:106
  303.1 11.7 %cholesky.584 = f32[128,128]{1,0:T(8,128)S(1)} custom-call(f32[128,128]{1,0:T(8,128)S(1)} %cholesky.682), custom_call_target="Cholesky" | custom-call | tf_op jit(solution)/shard_map/cholesky | solution.py:106
  316.2 9.8 %custom-call.55 = f32[1,128,128]{1,2,0:T(8,128)S(1)} custom-call(f32[1,128,128]{2,1,0:T(8,128)S(1)} %get-tuple-element.40), custom_call_target="InvertDiagBlocksLowerTriangular" | custom-call | tf_op jit(solution)/shard_map/cholesky | solution.py:106
  329.5 11.9 %cholesky.604 = f32[128,128]{1,0:T(8,128)S(1)} custom-call(f32[128,128]{1,0:T(8,128)S(1)} %cholesky.687), custom_call_target="Cholesky" | custom-call | tf_op jit(solution)/shard_map/cholesky | solution.py:106
  342.6 9.8 %custom-call.56 = f32[1,128,128]{1,2,0:T(8,128)S(1)} custom-call(f32[1,128,128]{2,1,0:T(8,128)S(1)} %get-tuple-element.37), custom_call_target="InvertDiagBlocksLowerTriangular" | custom-call | tf_op jit(solution)/shard_map/cholesky | solution.py:106
  355.6 11.7 %cholesky.624 = f32[128,128]{1,0:T(8,128)S(1)} custom-call(f32[128,128]{1,0:T(8,128)S(1)} %cholesky.692), custom_call_target="Cholesky" | custom-call | tf_op jit(solution)/shard_map/cholesky | solution.py:106
  368.7 9.8 %custom-call.57 = f32[1,128,128]{1,2,0:T(8,128)S(1)} custom-call(f32[1,128,128]{2,1,0:T(8,128)S(1)} %get-tuple-element.34), custom_call_target="InvertDiagBlocksLowerTriangular" | custom-call | tf_op jit(solution)/shard_map/cholesky | solution.py:106
  381.4 11.7 %cholesky.641 = f32[128,128]{1,0:T(8,128)S(1)} custom-call(f32[128,128]{1,0:T(8,128)S(1)} %convolution_subtract_fusion.4), custom_call_target="Cholesky" | custom-call | tf_op jit(solution)/shard_map/cholesky | solution.py:106
  413.5 3.6 collective-permute-done.11
  420.0 6.9 %collective-permute-start.18 = (f32[128,1024]{1,0:T(8,128)S(1)}, f32[128,1024]{1,0:T(8,128)S(1)}, u32[]{:S(2)}, u32[]{:S(2)}) collective-permute-start(f32[128,1024]{1,0:T(8,128)S(1)} %get-tuple-element.28), channel_id=1, source_target_pairs={{0,32},{16,48},{32,64},{48,80},{64,96},{80,112},{96,0},{112,16},{1... | collective-permute-start | bytes 1572872 | tf_op jit(solution)/shard_map/ppermute | solution.py:127
  426.9 18.8 %collective-permute-start.19 = (f32[128,1024]{1,0:T(8,128)S(1)}, f32[128,1024]{1,0:T(8,128)S(1)}, u32[]{:S(2)}, u32[]{:S(2)}) collective-permute-start(f32[128,1024]{1,0:T(8,128)S(1)} %get-tuple-element.28), channel_id=1, source_target_pairs={{0,64},{16,80},{32,96},{48,112},{64,0},{80,16},{96,32},{112,48},{1... | collective-permute-start | bytes 1572872 | tf_op jit(solution)/shard_map/ppermute | solution.py:127
  445.8 10.6 %collective-permute-done.18 = f32[128,1024]{1,0:T(8,128)S(1)} collective-permute-done((f32[128,1024]{1,0:T(8,128)S(1)}, f32[128,1024]{1,0:T(8,128)S(1)}, u32[]{:S(2)}, u32[]{:S(2)}) %collective-permute-start.18) | collective-permute-done | bytes 524320 | tf_op jit(solution)/shard_map/ppermute | solution.py:127
  456.4 12.1 %collective-permute-done.19 = f32[128,1024]{1,0:T(8,128)S(1)} collective-permute-done((f32[128,1024]{1,0:T(8,128)S(1)}, f32[128,1024]{1,0:T(8,128)S(1)}, u32[]{:S(2)}, u32[]{:S(2)}) %collective-permute-start.19) | collective-permute-done | bytes 524320 | tf_op jit(solution)/shard_map/ppermute | solution.py:127
  477.8 5.1 gather_fusion.2
  482.9 17.7 %all-gather.3.cloned.1.call-done = f32[2048,1024]{1,0:T(8,128)} async-done(((f32[128,1024]{1,0:T(8,128)}), f32[2048,1024]{1,0:T(8,128)}) %all-gather.3.cloned.1.call-update) | async-done | bytes 8388624 | tf_op jit(solution)/shard_map/all_gather | solution.py:112
  500.6 32.0 %bitcast_subtract_fusion = f32[8,4,256,256]{2,3,0,1:T(8,128)} fusion(f32[4,256,1024,1]{2,1,3,0:T(8,128)} %bitcast.118, f32[8,256,1024,1]{2,1,0,3:T(8,128)} %bitcast.116, f32[8,1,4,1,256,256]{4,5,0,2,3,1:T(8,128)} %copy.15), kind=kOutput, calls=%fused_computation.6 | convolution fusion | flops 25771900928 | bytes 29360128 | tf_op jit(solution)/shard_map/aik,bjk->abij/dot_general | solution.py:137
  532.6 9.1 %copy.19 = f32[8,4,256,256]{3,2,1,0:T(8,128)} copy(f32[8,4,256,256]{2,3,0,1:T(8,128)} %bitcast_subtract_fusion) | data formatting | bytes 16777216 | tf_op jit(solution)/shard_map/sub | solution.py:138
  541.7 7.9 %gather_fusion.3 = f32[32,256,256]{2,1,0:T(8,128)} fusion(f32[32,256,256]{2,1,0:T(8,128)} %bitcast.108, s32[1024]{0:T(1024)S(1)} %pad_clamp_fusion.1), kind=kCustom, calls=%fused_computation.3 | custom fusion | bytes 16777344 | tf_op jit(solution)/shard_map/gather | solution.py:142
  549.6 8.0 %broadcast_select_fusion = f32[8,4,256,256]{3,2,1,0:T(8,128)} fusion(f32[8,4,256,256]{3,2,1,0:T(8,128)} %bitcast.107, pred[8,4]{1,0:T(8,128)(4,1)S(1)} %broadcast_and_fusion), kind=kLoop, calls=%fused_computation.12 | loop fusion | flops 2097152 | bytes 16777248 | tf_op jit(solution)/shard_map/jit(_where)/select_n | solution.py:142
  557.6 5.7 all-to-all-start.1
  563.5 93.6 %all-to-all-done.1 = f32[8,4,256,256]{3,2,1,0:T(8,128)} async-done(((f32[8,4,256,256]{3,2,1,0:T(8,128)}), f32[8,4,256,256]{3,2,1,0:T(8,128)}, u32[]{:S(2)}, u32[]{:S(2)}) %all-to-all-start.1) | async-done | bytes 8388640 | tf_op jit(solution)/shard_map/all_to_all | solution.py:143
  657.1 7.9 %gather_fusion.4 = f32[8,4,256,256]{3,2,1,0:T(8,128)} fusion(f32[8,4,256,256]{3,2,1,0:T(8,128)} %all-to-all-done.1, s32[1024]{0:T(1024)S(1)} %pad_clamp_fusion), kind=kCustom, calls=%fused_computation.4 | custom fusion | bytes 16777248 | tf_op jit(solution)/shard_map/gather | solution.py:144
  665.0 8.0 %bitcast_select_fusion = f32[8,1,4,1,256,256]{5,4,3,2,1,0:T(8,128)} fusion(f32[8,4,256,256]{3,2,1,0:T(8,128)} %gather_fusion.4, pred[8]{0:T(512)(128)(4,1)S(1)} %broadcast_compare_fusion.2), kind=kLoop, calls=%fused_computation.5 | loop fusion | flops 2097152 | bytes 16777224 | tf_op jit(solution)/shard_map/jit(_where)/select_n | solution.py:144
  673.0 8.4 %copy.45 = f32[8,1,256,1024]{3,2,1,0:T(8,128)} copy(f32[8,1,256,1024]{3,2,1,0:T(8,128)} %bitcast.117) | data formatting | bytes 16777216
  (135 shorter events, 98.5 us)
Async XLA Ops:
  16.8 10.4 %collective-permute-start = (f32[256,256]{0,1:T(8,128)S(1)}, f32[256,256]{0,1:T(8,128)S(1)}, u32[]{:S(2)}, u32[]{:S(2)}) collective-permute-start(f32[256,256]{0,1:T(8,128)S(1)} %slice_bitcast_fusion), channel_id=1, source_target_pairs={{0,64},{16,80},{32,96},{48,112},{1,65},{17,81},{33,97},{49,113},{2... | collective-permute-start | bytes 786440 | tf_op jit(solution)/shard_map/ppermute | solution.py:26
  28.3 7.3 %collective-permute-start.1 = (f32[256,256]{0,1:T(8,128)S(1)}, f32[256,256]{0,1:T(8,128)S(1)}, u32[]{:S(2)}, u32[]{:S(2)}) collective-permute-start(f32[256,256]{0,1:T(8,128)S(1)} %select_add_fusion), channel_id=1, source_target_pairs={{0,16},{16,32},{32,48},{48,0},{64,80},{80,96},{96,112},{112,64},{1... | collective-permute-start | bytes 786440 | tf_op jit(solution)/shard_map/ppermute | solution.py:30
  30.0 12.7 %collective-permute-start.2 = (f32[256,256]{0,1:T(8,128)S(1)}, f32[256,256]{0,1:T(8,128)S(1)}, u32[]{:S(2)}, u32[]{:S(2)}) collective-permute-start(f32[256,256]{0,1:T(8,128)S(1)} %select_add_fusion), channel_id=1, source_target_pairs={{0,32},{16,48},{32,0},{48,16},{64,96},{80,112},{96,64},{112,80},{1... | collective-permute-start | bytes 786440 | tf_op jit(solution)/shard_map/ppermute | solution.py:30
  31.2 12.2 %collective-permute-start.3 = (f32[256,256]{0,1:T(8,128)S(1)}, f32[256,256]{0,1:T(8,128)S(1)}, u32[]{:S(2)}, u32[]{:S(2)}) collective-permute-start(f32[256,256]{0,1:T(8,128)S(1)} %select_add_fusion), channel_id=1, source_target_pairs={{0,48},{16,0},{32,16},{48,32},{64,112},{80,64},{96,80},{112,96},{1... | collective-permute-start | bytes 786440 | tf_op jit(solution)/shard_map/ppermute | solution.py:30
  44.1 26.2 %collective-permute-start.4 = (f32[4,256,256]{1,2,0:T(8,128)S(1)}, f32[4,256,256]{1,2,0:T(8,128)}, u32[]{:S(2)}, u32[]{:S(2)}) collective-permute-start(f32[4,256,256]{1,2,0:T(8,128)S(1)} %gather_fusion), channel_id=1, source_target_pairs={{0,4},{1,5},{2,6},{3,7},{16,20},{17,21},{18,22},{19,23},{32,36},{3... | collective-permute-start | bytes 3145736 | tf_op jit(solution)/shard_map/ppermute | solution.py:26
  48.3 44.5 %collective-permute-start.5 = (f32[4,256,256]{1,2,0:T(8,128)S(1)}, f32[4,256,256]{1,2,0:T(8,128)}, u32[]{:S(2)}, u32[]{:S(2)}) collective-permute-start(f32[4,256,256]{1,2,0:T(8,128)S(1)} %gather_fusion), channel_id=1, source_target_pairs={{0,8},{1,9},{2,10},{3,11},{16,24},{17,25},{18,26},{19,27},{32,40},... | collective-permute-start | bytes 3145736 | tf_op jit(solution)/shard_map/ppermute | solution.py:26
  51.5 41.2 %collective-permute-start.6 = (f32[4,256,256]{1,2,0:T(8,128)S(1)}, f32[4,256,256]{1,2,0:T(8,128)}, u32[]{:S(2)}, u32[]{:S(2)}) collective-permute-start(f32[4,256,256]{1,2,0:T(8,128)S(1)} %gather_fusion), channel_id=1, source_target_pairs={{0,12},{1,13},{2,14},{3,15},{16,28},{17,29},{18,30},{19,31},{32,44... | collective-permute-start | bytes 3145736 | tf_op jit(solution)/shard_map/ppermute | solution.py:26
  57.4 42.6 %copy-start.4 = (s32[60]{0:T(128)S(1)}, s32[60]{0:T(128)}, u32[]{:S(2)}) copy-start(s32[60]{0:T(128)} %param.5) | copy-start | bytes 724
  57.5 57.3 %all-to-all-start = ((f32[16,128,256]{2,1,0:T(8,128)}), f32[16,128,256]{2,1,0:T(8,128)}, u32[]{:S(2)}, u32[]{:S(2)}) async-start(f32[16,128,256]{2,1,0:T(8,128)} %bitcast.13), calls=%async_computation | async-start | bytes 4194304 | tf_op jit(solution)/shard_map/all_to_all | solution.py:89
  62.8 437.9 %all-gather.3.cloned.1.call-start = ((), (), s32[]{:S(2)}) async-start(), calls=%async_computation.2 | async-start | bytes 8912896 | tf_op jit(solution)/shard_map/all_gather | solution.py:112
  94.9 48.7 %collective-permute-start.9 = (f32[4,256,256]{1,2,0:T(8,128)S(1)}, f32[4,256,256]{1,2,0:T(8,128)S(1)}, u32[]{:S(2)}, u32[]{:S(2)}) collective-permute-start(f32[4,256,256]{1,2,0:T(8,128)S(1)} %add_add_fusion), channel_id=1, source_target_pairs={{0,3},{1,0},{2,1},{3,2},{4,7},{5,4},{6,5},{7,6},{8,11},{9,8},{10,9... | collective-permute-start | bytes 3145736 | tf_op jit(solution)/shard_map/ppermute | solution.py:30
  98.7 48.3 %collective-permute-start.7 = (f32[4,256,256]{1,2,0:T(8,128)S(1)}, f32[4,256,256]{1,2,0:T(8,128)}, u32[]{:S(2)}, u32[]{:S(2)}) collective-permute-start(f32[4,256,256]{1,2,0:T(8,128)S(1)} %add_add_fusion), channel_id=1, source_target_pairs={{0,1},{1,2},{2,3},{3,0},{4,5},{5,6},{6,7},{7,4},{8,9},{9,10},{10,1... | collective-permute-start | bytes 3145736 | tf_op jit(solution)/shard_map/ppermute | solution.py:30
  98.7 48.3 %collective-permute-start.8 = (f32[4,256,256]{1,2,0:T(8,128)S(1)}, f32[4,256,256]{1,2,0:T(8,128)}, u32[]{:S(2)}, u32[]{:S(2)}) collective-permute-start(f32[4,256,256]{1,2,0:T(8,128)S(1)} %add_add_fusion), channel_id=1, source_target_pairs={{0,2},{1,3},{2,0},{3,1},{4,6},{5,7},{6,4},{7,5},{8,10},{9,11},{10,... | collective-permute-start | bytes 3145736 | tf_op jit(solution)/shard_map/ppermute | solution.py:30
  164.8 1.9 copy-start
  193.7 2.5 copy-start.1
  403.5 15.0 %copy-start.5 = (s32[60]{0:T(128)S(1)}, s32[60]{0:T(128)}, u32[]{:S(2)}) copy-start(s32[60]{0:T(128)} %param.7) | copy-start | bytes 724
  403.5 15.0 %copy-start.3 = (s32[60]{0:T(128)S(1)}, s32[60]{0:T(128)}, u32[]{:S(2)}) copy-start(s32[60]{0:T(128)} %param.6) | copy-start | bytes 724
  405.1 7.7 %collective-permute-start.10 = (f32[128,1024]{1,0:T(8,128)}, f32[128,1024]{1,0:T(8,128)S(1)}, u32[]{:S(2)}, u32[]{:S(2)}) collective-permute-start(f32[128,1024]{1,0:T(8,128)} %slice_select_fusion), channel_id=1, source_target_pairs={{0,0},{16,17},{32,34},{48,51},{64,68},{80,85},{96,102},{112,119},{... | collective-permute-start | bytes 1572872 | tf_op jit(solution)/shard_map/ppermute | solution.py:122
  406.4 10.7 %collective-permute-start.11 = (f32[128,1024]{1,0:T(8,128)}, f32[128,1024]{1,0:T(8,128)S(1)}, u32[]{:S(2)}, u32[]{:S(2)}) collective-permute-start(f32[128,1024]{1,0:T(8,128)} %slice_select_fusion), channel_id=1, source_target_pairs={{1,16},{17,33},{33,50},{49,67},{65,84},{81,101},{97,118},{113,7},{... | collective-permute-start | bytes 1572872 | tf_op jit(solution)/shard_map/ppermute | solution.py:122
  407.7 10.1 %collective-permute-start.12 = (f32[128,1024]{1,0:T(8,128)}, f32[128,1024]{1,0:T(8,128)S(1)}, u32[]{:S(2)}, u32[]{:S(2)}) collective-permute-start(f32[128,1024]{1,0:T(8,128)} %slice_select_fusion), channel_id=1, source_target_pairs={{4,32},{20,49},{36,66},{52,83},{68,100},{84,117},{100,6},{116,23},... | collective-permute-start | bytes 1572872 | tf_op jit(solution)/shard_map/ppermute | solution.py:122
  408.4 10.3 %collective-permute-start.13 = (f32[128,1024]{1,0:T(8,128)}, f32[128,1024]{1,0:T(8,128)S(1)}, u32[]{:S(2)}, u32[]{:S(2)}) collective-permute-start(f32[128,1024]{1,0:T(8,128)} %slice_select_fusion), channel_id=1, source_target_pairs={{5,48},{21,65},{37,82},{53,99},{69,116},{85,5},{101,22},{117,39},{... | collective-permute-start | bytes 1572872 | tf_op jit(solution)/shard_map/ppermute | solution.py:122
  409.1 9.6 %collective-permute-start.14 = (f32[128,1024]{1,0:T(8,128)}, f32[128,1024]{1,0:T(8,128)S(1)}, u32[]{:S(2)}, u32[]{:S(2)}) collective-permute-start(f32[128,1024]{1,0:T(8,128)} %slice_select_fusion), channel_id=1, source_target_pairs={{8,64},{24,81},{40,98},{56,115},{72,4},{88,21},{104,38},{120,55},{... | collective-permute-start | bytes 1572872 | tf_op jit(solution)/shard_map/ppermute | solution.py:122
  412.8 6.0 collective-permute-start.15
  417.1 1.7 collective-permute-start.16
  417.8 1.0 collective-permute-start.17
  420.0 36.4 %collective-permute-start.18 = (f32[128,1024]{1,0:T(8,128)S(1)}, f32[128,1024]{1,0:T(8,128)S(1)}, u32[]{:S(2)}, u32[]{:S(2)}) collective-permute-start(f32[128,1024]{1,0:T(8,128)S(1)} %get-tuple-element.28), channel_id=1, source_target_pairs={{0,32},{16,48},{32,64},{48,80},{64,96},{80,112},{96,0},{112,16},{1... | collective-permute-start | bytes 1572872 | tf_op jit(solution)/shard_map/ppermute | solution.py:127
  426.9 41.7 %collective-permute-start.19 = (f32[128,1024]{1,0:T(8,128)S(1)}, f32[128,1024]{1,0:T(8,128)S(1)}, u32[]{:S(2)}, u32[]{:S(2)}) collective-permute-start(f32[128,1024]{1,0:T(8,128)S(1)} %get-tuple-element.28), channel_id=1, source_target_pairs={{0,64},{16,80},{32,96},{48,112},{64,0},{80,16},{96,32},{112,48},{1... | collective-permute-start | bytes 1572872 | tf_op jit(solution)/shard_map/ppermute | solution.py:127
  445.6 22.9 %collective-permute-start.20 = (f32[128,1024]{1,0:T(8,128)S(1)}, f32[128,1024]{1,0:T(8,128)S(1)}, u32[]{:S(2)}, u32[]{:S(2)}) collective-permute-start(f32[128,1024]{1,0:T(8,128)S(1)} %get-tuple-element.28), channel_id=1, source_target_pairs={{0,96},{16,112},{32,0},{48,16},{64,32},{80,48},{96,64},{112,80},{1... | collective-permute-start | bytes 1572872 | tf_op jit(solution)/shard_map/ppermute | solution.py:127
  468.6 0.8 copy-start.2
  469.4 5.2 collective-permute-start.21
  557.6 99.5 %all-to-all-start.1 = ((f32[8,4,256,256]{3,2,1,0:T(8,128)}), f32[8,4,256,256]{3,2,1,0:T(8,128)}, u32[]{:S(2)}, u32[]{:S(2)}) async-start(f32[8,4,256,256]{3,2,1,0:T(8,128)} %broadcast_select_fusion), calls=%async_computation.1 | async-start | bytes 16777216 | tf_op jit(solution)/shard_map/all_to_all | solution.py:143
Sparse Core Ops, SparseCore 0:
  405.2 95.4 all-gather.2

commit v6 on v4

--- a/solution.py
+++ b/solution.py
@@ -4,7 +4,7 @@
 from jax.sharding import PartitionSpec as P
 
 LEAD = 4
-PRECISE = lax.Precision.HIGHEST
+SCHUR_PRECISION = lax.Precision.HIGH
 
 
 def valid_gain(valid_flags, ndims):
@@ -120,7 +120,13 @@
     pos = jnp.where(own_d % 2 == 0, own_d // 2, grid_rows // 2 + par_d // 2)
     col_factor = combined[pos].reshape(cols_dev, tile, lead_w)
 
-    prod = jnp.einsum("aik,bjk->abij", factor_rows, col_factor, precision=PRECISE)
+    prod = lax.dot_general(
+        factor_rows.reshape(rows_dev * tile, lead_w),
+        col_factor.reshape(cols_dev * tile, lead_w),
+        (((1,), (1,)), ((), ())),
+        precision=SCHUR_PRECISION,
+    )
+    prod = prod.reshape(rows_dev, tile, cols_dev, tile).transpose(0, 2, 1, 3)
     schur = (current - prod).reshape((rows_dev * cols_dev,) + current.shape[2:])
 
     flat_idx = send_local[:, None] * cols_dev + col_local[None, :]

time: 660 us -> 631 us (0.956)
  local copies, waits for them, and re-layouts: 76.3 us -> 57.7 us
  matrix products: 58.5 us -> 46.4 us
    dot_general x1, matrix products: 31.7 us -> 19.6 us  [local(): lax.dot_general(factor_rows.reshape(rows_dev * tile, lead_w), col_factor....]
    sub x1 -> x0, local copies, waits for them, and re-layouts: 9.13 us -> none  [local(): schur = (current - prod).reshape((rows_dev * cols_dev,) + current.shape[2:])]
    unnamed x20 -> x19, local copies, waits for them, and re-layouts: 26 us -> 17.4 us
where the time goes in v6:
time: 631 us; the launch traced here: 621 us
  waiting for transfers between devices  230 us (36%)
  other arithmetic  219 us (35%)
  local copies, waits for them, and re-layouts  57.7 us (9%)
  starting transfers between devices  46.4 us (7%)
  matrix products  46.4 us (7%)
  between operations  21.5 us (3%)
    another operation x34, other arithmetic, local(): aug_factor = lax.linalg.cholesky(aug, symmetrize_input=False)  195 us
    all_to_all x1, waiting for transfers between devices, local(): lax.all_to_all(outgoing, 'row', split_axis=0, concat_axis=0, tiled=True)  93.6 us
    all_gather x1, waiting for transfers between devices, local(): row_tiles = lax.all_gather(lead_tile, 'col')[:LEAD]  56.3 us
    another operation x16, matrix products, local(): aug_factor = lax.linalg.cholesky(aug, symmetrize_input=False)  26.8 us
    all_to_all x1, waiting for transfers between devices, local(): lax.all_to_all(panel_col, 'col', split_axis=0, concat_axis=0, tiled=True)  25.7 us
    ppermute x3, starting transfers between devices, local(): ring.append(lax.ppermute(mine, 'row', perm))  24.6 us
    ppermute x3, waiting for transfers between devices, local(): ring.append(lax.ppermute(mine, 'row', perm))  21.8 us
    dot_general x1, matrix products, local(): lax.dot_general(factor_rows.reshape(rows_dev * tile, lead_w), col_factor....  19.6 us
  transfers between devices with their start and end apart: 17, of which 10 were waited for; matrix products, arithmetic and copies ran while one was open for 3% of the time, Pallas kernels for 0%

profile of v6, /device:TPU:1, one launch (start us, length us, event | category | flops | bytes accessed | tf_op | source)
XLA Modules:
  0.0 620.5 jit_solution(6305689834713117443)
XLA Ops:
  9.0 56.3 %all-gather.8.cloned.1.call-done = f32[16,1,256,256]{3,2,1,0:T(8,128)} async-done(((f32[1,1,256,256]{3,2,1,0:T(8,128)}), f32[16,1,256,256]{3,2,1,0:T(8,128)}) %all-gather.8.cloned.1.call-update) | async-done | bytes 4194320 | tf_op jit(solution)/shard_map/all_gather | solution.py:69
  67.6 3.1 slice.191
  70.6 5.0 all-to-all-start
  77.0 25.7 %all-to-all-done = f32[16,128,256]{2,1,0:T(8,128)S(1)} async-done(((f32[16,128,256]{2,1,0:T(8,128)}), f32[16,128,256]{2,1,0:T(8,128)S(1)}, u32[]{:S(2)}, u32[]{:S(2)}) %all-to-all-start) | async-done | bytes 2097184 | tf_op jit(solution)/shard_map/all_to_all | solution.py:75
  104.2 13.3 %all-gather.12.cloned.1.call-done = f32[32,1,256,256]{3,2,1,0:T(8,128)} async-done(((f32[4,1,256,256]{3,2,1,0:T(8,128)}), f32[32,1,256,256]{3,2,1,0:T(8,128)}) %all-gather.12.cloned.1.call-update) | async-done | bytes 8388624 | tf_op jit(solution)/shard_map/all_gather | solution.py:70
  119.7 2.7 copy.15
  125.4 11.7 %cholesky.252 = f32[128,128]{1,0:T(8,128)S(1)} custom-call(f32[128,128]{1,0:T(8,128)S(1)} %cholesky.658), custom_call_target="Cholesky" | custom-call | tf_op jit(solution)/shard_map/cholesky | solution.py:92
  137.2 9.8 %custom-call.50 = f32[1,128,128]{1,2,0:T(8,128)S(1)} custom-call(f32[1,128,128]{2,1,0:T(8,128)S(1)} %get-tuple-element.57), custom_call_target="InvertDiagBlocksLowerTriangular" | custom-call | tf_op jit(solution)/shard_map/cholesky | solution.py:92
  147.0 3.0 cholesky.281
  155.1 11.7 %cholesky.274 = f32[128,128]{1,0:T(8,128)S(1)} custom-call(f32[128,128]{1,0:T(8,128)S(1)} %cholesky.662), custom_call_target="Cholesky" | custom-call | tf_op jit(solution)/shard_map/cholesky | solution.py:92
  167.4 9.8 %custom-call.51 = f32[1,128,128]{1,2,0:T(8,128)S(1)} custom-call(f32[1,128,128]{2,1,0:T(8,128)S(1)} %get-tuple-element.54), custom_call_target="InvertDiagBlocksLowerTriangular" | custom-call | tf_op jit(solution)/shard_map/cholesky | solution.py:92
  180.8 11.7 %cholesky.526 = f32[128,128]{1,0:T(8,128)S(1)} custom-call(f32[128,128]{1,0:T(8,128)S(1)} %cholesky.667), custom_call_target="Cholesky" | custom-call | tf_op jit(solution)/shard_map/cholesky | solution.py:92
  193.8 9.9 %custom-call.52 = f32[1,128,128]{1,2,0:T(8,128)S(1)} custom-call(f32[1,128,128]{2,1,0:T(8,128)S(1)} %get-tuple-element.51), custom_call_target="InvertDiagBlocksLowerTriangular" | custom-call | tf_op jit(solution)/shard_map/cholesky | solution.py:92
  205.0 2.6 convolution_subtract_fusion.2
  207.6 11.7 %cholesky.545 = f32[128,128]{1,0:T(8,128)S(1)} custom-call(f32[128,128]{1,0:T(8,128)S(1)} %cholesky.672), custom_call_target="Cholesky" | custom-call | tf_op jit(solution)/shard_map/cholesky | solution.py:92
  220.6 9.8 %custom-call.53 = f32[1,128,128]{1,2,0:T(8,128)S(1)} custom-call(f32[1,128,128]{2,1,0:T(8,128)S(1)} %get-tuple-element.48), custom_call_target="InvertDiagBlocksLowerTriangular" | custom-call | tf_op jit(solution)/shard_map/cholesky | solution.py:92
  231.6 2.6 fusion.4
  234.2 11.9 %cholesky.564 = f32[128,128]{1,0:T(8,128)S(1)} custom-call(f32[128,128]{1,0:T(8,128)S(1)} %cholesky.677), custom_call_target="Cholesky" | custom-call | tf_op jit(solution)/shard_map/cholesky | solution.py:92
  247.4 9.8 %custom-call.54 = f32[1,128,128]{1,2,0:T(8,128)S(1)} custom-call(f32[1,128,128]{2,1,0:T(8,128)S(1)} %get-tuple-element.45), custom_call_target="InvertDiagBlocksLowerTriangular" | custom-call | tf_op jit(solution)/shard_map/cholesky | solution.py:92
  258.3 2.6 fusion.10
  261.0 11.7 %cholesky.584 = f32[128,128]{1,0:T(8,128)S(1)} custom-call(f32[128,128]{1,0:T(8,128)S(1)} %cholesky.682), custom_call_target="Cholesky" | custom-call | tf_op jit(solution)/shard_map/cholesky | solution.py:92
  274.0 10.2 %custom-call.55 = f32[1,128,128]{1,2,0:T(8,128)S(1)} custom-call(f32[1,128,128]{2,1,0:T(8,128)S(1)} %get-tuple-element.42), custom_call_target="InvertDiagBlocksLowerTriangular" | custom-call | tf_op jit(solution)/shard_map/cholesky | solution.py:92
  285.2 2.5 fusion.13
  287.8 11.7 %cholesky.604 = f32[128,128]{1,0:T(8,128)S(1)} custom-call(f32[128,128]{1,0:T(8,128)S(1)} %cholesky.687), custom_call_target="Cholesky" | custom-call | tf_op jit(solution)/shard_map/cholesky | solution.py:92
  300.8 9.8 %custom-call.56 = f32[1,128,128]{1,2,0:T(8,128)S(1)} custom-call(f32[1,128,128]{2,1,0:T(8,128)S(1)} %get-tuple-element.39), custom_call_target="InvertDiagBlocksLowerTriangular" | custom-call | tf_op jit(solution)/shard_map/cholesky | solution.py:92
  313.8 11.8 %cholesky.624 = f32[128,128]{1,0:T(8,128)S(1)} custom-call(f32[128,128]{1,0:T(8,128)S(1)} %cholesky.692), custom_call_target="Cholesky" | custom-call | tf_op jit(solution)/shard_map/cholesky | solution.py:92
  326.9 9.8 %custom-call.57 = f32[1,128,128]{1,2,0:T(8,128)S(1)} custom-call(f32[1,128,128]{2,1,0:T(8,128)S(1)} %get-tuple-element.36), custom_call_target="InvertDiagBlocksLowerTriangular" | custom-call | tf_op jit(solution)/shard_map/cholesky | solution.py:92
  339.4 11.7 %cholesky.641 = f32[128,128]{1,0:T(8,128)S(1)} custom-call(f32[128,128]{1,0:T(8,128)S(1)} %convolution_subtract_fusion.4), custom_call_target="Cholesky" | custom-call | tf_op jit(solution)/shard_map/cholesky | solution.py:92
  358.7 2.9 select_select_fusion
  363.1 3.2 collective-permute-start
  369.8 2.9 collective-permute-done
  373.5 5.5 collective-permute-done.1
  381.9 6.7 %collective-permute-start.8 = (f32[128,1024]{1,0:T(8,128)S(1)}, f32[128,1024]{1,0:T(8,128)S(1)}, u32[]{:S(2)}, u32[]{:S(2)}) collective-permute-start(f32[128,1024]{1,0:T(8,128)S(1)} %get-tuple-element.30), channel_id=1, source_target_pairs={{0,32},{16,48},{32,64},{48,80},{64,96},{80,112},{96,0},{112,16},{1... | collective-permute-start | bytes 1572872 | tf_op jit(solution)/shard_map/ppermute | solution.py:113
  388.6 17.8 %collective-permute-start.9 = (f32[128,1024]{1,0:T(8,128)S(1)}, f32[128,1024]{1,0:T(8,128)S(1)}, u32[]{:S(2)}, u32[]{:S(2)}) collective-permute-start(f32[128,1024]{1,0:T(8,128)S(1)} %get-tuple-element.30), channel_id=1, source_target_pairs={{0,64},{16,80},{32,96},{48,112},{64,0},{80,16},{96,32},{112,48},{1... | collective-permute-start | bytes 1572872 | tf_op jit(solution)/shard_map/ppermute | solution.py:113
  406.6 9.3 %collective-permute-done.8 = f32[128,1024]{1,0:T(8,128)S(1)} collective-permute-done((f32[128,1024]{1,0:T(8,128)S(1)}, f32[128,1024]{1,0:T(8,128)S(1)}, u32[]{:S(2)}, u32[]{:S(2)}) %collective-permute-start.8) | collective-permute-done | bytes 524320 | tf_op jit(solution)/shard_map/ppermute | solution.py:113
  416.0 12.1 %collective-permute-done.9 = f32[128,1024]{1,0:T(8,128)S(1)} collective-permute-done((f32[128,1024]{1,0:T(8,128)S(1)}, f32[128,1024]{1,0:T(8,128)S(1)}, u32[]{:S(2)}, u32[]{:S(2)}) %collective-permute-start.9) | collective-permute-done | bytes 524320 | tf_op jit(solution)/shard_map/ppermute | solution.py:113
  429.2 2.3 collective-permute-start.11
  435.6 3.2 constant_dynamic-update-slice_fusion
  438.8 5.0 gather_fusion
  443.8 10.7 %all-gather.10.cloned.1.call-done = f32[2048,1024]{1,0:T(8,128)} async-done(((f32[128,1024]{1,0:T(8,128)}), f32[2048,1024]{1,0:T(8,128)}) %all-gather.10.cloned.1.call-update) | async-done | bytes 8388624 | tf_op jit(solution)/shard_map/all_gather | solution.py:98
  454.5 19.6 %bitcast_subtract_fusion = f32[8,4,256,256]{3,2,1,0:T(8,128)} fusion(f32[8,256,1024,1]{2,1,3,0:T(8,128)} %bitcast.98, f32[4,256,1024,1]{2,1,0,3:T(8,128)} %bitcast.100, f32[8,1,4,1,256,256]{5,4,3,2,1,0:T(8,128)} %param.4), kind=kOutput, calls=%fused_computation.4 | convolution fusion | flops 12886999040 | bytes 29360128 | tf_op jit(solution)/shard_map/dot_general | solution.py:123
  474.1 7.9 %gather_fusion.1 = f32[32,256,256]{2,1,0:T(8,128)} fusion(f32[32,256,256]{2,1,0:T(8,128)} %bitcast.97, s32[1024]{0:T(1024)S(1)} %pad_clamp_fusion.1), kind=kCustom, calls=%fused_computation.1 | custom fusion | bytes 16777344 | tf_op jit(solution)/shard_map/gather | solution.py:134
  481.9 8.0 %broadcast_select_fusion = f32[8,4,256,256]{3,2,1,0:T(8,128)} fusion(f32[8,4,256,256]{3,2,1,0:T(8,128)} %bitcast.92, pred[8,4]{1,0:T(8,128)(4,1)S(1)} %broadcast_and_fusion), kind=kLoop, calls=%fused_computation.9 | loop fusion | flops 2097152 | bytes 16777248 | tf_op jit(solution)/shard_map/jit(_where)/select_n | solution.py:134
  489.9 5.7 all-to-all-start.1
  495.9 93.6 %all-to-all-done.1 = f32[8,4,256,256]{3,2,1,0:T(8,128)} async-done(((f32[8,4,256,256]{3,2,1,0:T(8,128)}), f32[8,4,256,256]{3,2,1,0:T(8,128)}, u32[]{:S(2)}, u32[]{:S(2)}) %all-to-all-start.1) | async-done | bytes 8388640 | tf_op jit(solution)/shard_map/all_to_all | solution.py:135
  589.4 7.9 %gather_fusion.2 = f32[8,4,256,256]{3,2,1,0:T(8,128)} fusion(f32[8,4,256,256]{3,2,1,0:T(8,128)} %all-to-all-done.1, s32[1024]{0:T(1024)S(1)} %pad_clamp_fusion), kind=kCustom, calls=%fused_computation.2 | custom fusion | bytes 16777248 | tf_op jit(solution)/shard_map/gather | solution.py:136
  597.3 8.0 %bitcast_select_fusion = f32[8,1,4,1,256,256]{5,4,3,2,1,0:T(8,128)} fusion(f32[8,4,256,256]{3,2,1,0:T(8,128)} %gather_fusion.2, pred[8]{0:T(512)(128)(4,1)S(1)} %broadcast_compare_fusion.2), kind=kLoop, calls=%fused_computation.3 | loop fusion | flops 2097152 | bytes 16777224 | tf_op jit(solution)/shard_map/jit(_where)/select_n | solution.py:136
  605.3 8.4 %copy.42 = f32[8,1,256,1024]{3,2,1,0:T(8,128)} copy(f32[8,1,256,1024]{3,2,1,0:T(8,128)} %bitcast.99) | data formatting | bytes 16777216
  (113 shorter events, 53.8 us)
Async XLA Ops:
  7.2 58.1 %all-gather.8.cloned.1.call-start = ((), (), s32[]{:S(2)}) async-start(), calls=%async_computation.2 | async-start | bytes 4456448 | tf_op jit(solution)/shard_map/all_gather | solution.py:69
  8.9 66.8 %copy-start.5 = (s32[60]{0:T(128)S(1)}, s32[60]{0:T(128)}, u32[]{:S(2)}) copy-start(s32[60]{0:T(128)} %param.5) | copy-start | bytes 724
  8.9 108.6 %all-gather.12.cloned.1.call-start = ((), (), s32[]{:S(2)}) async-start(), calls=%async_computation.4 | async-start | bytes 9437184 | tf_op jit(solution)/shard_map/all_gather | solution.py:70
  70.6 32.1 %all-to-all-start = ((f32[16,128,256]{2,1,0:T(8,128)}), f32[16,128,256]{2,1,0:T(8,128)S(1)}, u32[]{:S(2)}, u32[]{:S(2)}) async-start(f32[16,128,256]{2,1,0:T(8,128)} %bitcast.3), calls=%async_computation | async-start | bytes 4194304 | tf_op jit(solution)/shard_map/all_to_all | solution.py:75
  75.6 378.9 %all-gather.10.cloned.1.call-start = ((), (), s32[]{:S(2)}) async-start(), calls=%async_computation.3 | async-start | bytes 8912896 | tf_op jit(solution)/shard_map/all_gather | solution.py:98
  117.5 2.2 slice-start
  123.4 2.0 copy-start
  147.0 4.1 copy-start.1
  151.6 2.5 copy-start.2
  361.6 18.8 %copy-start.4 = (s32[60]{0:T(128)S(1)}, s32[60]{0:T(128)}, u32[]{:S(2)}) copy-start(s32[60]{0:T(128)} %param.6) | copy-start | bytes 724
  361.6 18.8 %copy-start.6 = (s32[60]{0:T(128)S(1)}, s32[60]{0:T(128)}, u32[]{:S(2)}) copy-start(s32[60]{0:T(128)} %param.7) | copy-start | bytes 724
  363.1 9.6 %collective-permute-start = (f32[128,1024]{1,0:T(8,128)}, f32[128,1024]{1,0:T(8,128)S(1)}, u32[]{:S(2)}, u32[]{:S(2)}) collective-permute-start(f32[128,1024]{1,0:T(8,128)} %slice_select_fusion), channel_id=1, source_target_pairs={{0,0},{16,17},{32,34},{48,51},{64,68},{80,85},{96,102},{112,119},{... | collective-permute-start | bytes 1572872 | tf_op jit(solution)/shard_map/ppermute | solution.py:108
  366.4 12.6 %collective-permute-start.1 = (f32[128,1024]{1,0:T(8,128)}, f32[128,1024]{1,0:T(8,128)S(1)}, u32[]{:S(2)}, u32[]{:S(2)}) collective-permute-start(f32[128,1024]{1,0:T(8,128)} %slice_select_fusion), channel_id=1, source_target_pairs={{1,16},{17,33},{33,50},{49,67},{65,84},{81,101},{97,118},{113,7},{... | collective-permute-start | bytes 1572872 | tf_op jit(solution)/shard_map/ppermute | solution.py:108
  367.7 12.0 %collective-permute-start.2 = (f32[128,1024]{1,0:T(8,128)}, f32[128,1024]{1,0:T(8,128)S(1)}, u32[]{:S(2)}, u32[]{:S(2)}) collective-permute-start(f32[128,1024]{1,0:T(8,128)} %slice_select_fusion), channel_id=1, source_target_pairs={{4,32},{20,49},{36,66},{52,83},{68,100},{84,117},{100,6},{116,23},... | collective-permute-start | bytes 1572872 | tf_op jit(solution)/shard_map/ppermute | solution.py:108
  368.4 12.2 %collective-permute-start.3 = (f32[128,1024]{1,0:T(8,128)}, f32[128,1024]{1,0:T(8,128)S(1)}, u32[]{:S(2)}, u32[]{:S(2)}) collective-permute-start(f32[128,1024]{1,0:T(8,128)} %slice_select_fusion), channel_id=1, source_target_pairs={{5,48},{21,65},{37,82},{53,99},{69,116},{85,5},{101,22},{117,39},{... | collective-permute-start | bytes 1572872 | tf_op jit(solution)/shard_map/ppermute | solution.py:108
  369.1 11.5 %collective-permute-start.4 = (f32[128,1024]{1,0:T(8,128)}, f32[128,1024]{1,0:T(8,128)S(1)}, u32[]{:S(2)}, u32[]{:S(2)}) collective-permute-start(f32[128,1024]{1,0:T(8,128)} %slice_select_fusion), channel_id=1, source_target_pairs={{8,64},{24,81},{40,98},{56,115},{72,4},{88,21},{104,38},{120,55},{... | collective-permute-start | bytes 1572872 | tf_op jit(solution)/shard_map/ppermute | solution.py:108
  372.8 7.9 %collective-permute-start.5 = (f32[128,1024]{1,0:T(8,128)}, f32[128,1024]{1,0:T(8,128)S(1)}, u32[]{:S(2)}, u32[]{:S(2)}) collective-permute-start(f32[128,1024]{1,0:T(8,128)} %slice_select_fusion), channel_id=1, source_target_pairs={{9,80},{25,97},{41,114},{57,3},{73,20},{89,37},{105,54},{121,71},{... | collective-permute-start | bytes 1572872 | tf_op jit(solution)/shard_map/ppermute | solution.py:108
  379.0 1.7 collective-permute-start.6
  379.7 1.0 collective-permute-start.7
  381.9 34.1 %collective-permute-start.8 = (f32[128,1024]{1,0:T(8,128)S(1)}, f32[128,1024]{1,0:T(8,128)S(1)}, u32[]{:S(2)}, u32[]{:S(2)}) collective-permute-start(f32[128,1024]{1,0:T(8,128)S(1)} %get-tuple-element.30), channel_id=1, source_target_pairs={{0,32},{16,48},{32,64},{48,80},{64,96},{80,112},{96,0},{112,16},{1... | collective-permute-start | bytes 1572872 | tf_op jit(solution)/shard_map/ppermute | solution.py:113
  388.6 39.5 %collective-permute-start.9 = (f32[128,1024]{1,0:T(8,128)S(1)}, f32[128,1024]{1,0:T(8,128)S(1)}, u32[]{:S(2)}, u32[]{:S(2)}) collective-permute-start(f32[128,1024]{1,0:T(8,128)S(1)} %get-tuple-element.30), channel_id=1, source_target_pairs={{0,64},{16,80},{32,96},{48,112},{64,0},{80,16},{96,32},{112,48},{1... | collective-permute-start | bytes 1572872 | tf_op jit(solution)/shard_map/ppermute | solution.py:113
  406.5 22.0 %collective-permute-start.10 = (f32[128,1024]{1,0:T(8,128)S(1)}, f32[128,1024]{1,0:T(8,128)S(1)}, u32[]{:S(2)}, u32[]{:S(2)}) collective-permute-start(f32[128,1024]{1,0:T(8,128)S(1)} %get-tuple-element.30), channel_id=1, source_target_pairs={{0,96},{16,112},{32,0},{48,16},{64,32},{80,48},{96,64},{112,80},{1... | collective-permute-start | bytes 1572872 | tf_op jit(solution)/shard_map/ppermute | solution.py:113
  428.4 0.8 copy-start.3
  429.2 6.3 %collective-permute-start.11 = (f32[4,128,1024]{2,1,0:T(8,128)S(1)}, f32[4,128,1024]{2,1,0:T(8,128)}, u32[]{:S(2)}, u32[]{:S(2)}) collective-permute-start(f32[4,128,1024]{2,1,0:T(8,128)S(1)} %pad_maximum_fusion), channel_id=1, source_target_pairs={{0,16},{16,0},{32,48},{48,32},{64,80},{80,64},{96,112},{112,96},{1... | collective-permute-start | bytes 6291464 | tf_op jit(solution)/shard_map/ppermute | solution.py:115
  489.9 99.5 %all-to-all-start.1 = ((f32[8,4,256,256]{3,2,1,0:T(8,128)}), f32[8,4,256,256]{3,2,1,0:T(8,128)}, u32[]{:S(2)}, u32[]{:S(2)}) async-start(f32[8,4,256,256]{3,2,1,0:T(8,128)} %broadcast_select_fusion), calls=%async_computation.1 | async-start | bytes 16777216 | tf_op jit(solution)/shard_map/all_to_all | solution.py:135
Sparse Core Ops, SparseCore 0:
  10.7 54.5 all-gather.7
  67.7 49.7 all-gather.11
  363.3 91.1 all-gather.9

commit v7 on v6

--- a/solution.py
+++ b/solution.py
@@ -130,10 +130,10 @@
     schur = (current - prod).reshape((rows_dev * cols_dev,) + current.shape[2:])
 
     flat_idx = send_local[:, None] * cols_dev + col_local[None, :]
-    keep = (send_valid[:, None] & col_valid[None, :])[:, :, None, None]
-    outgoing = jnp.where(keep, schur[flat_idx], 0.0)
+    outgoing = schur[flat_idx]
     incoming = lax.all_to_all(outgoing, "row", split_axis=0, concat_axis=0, tiled=True)
-    parent = jnp.where(recv_valid[:, None, None, None], incoming[recv_source], 0.0)
+    keep = (recv_valid[:, None] & col_valid[None, :])[:, :, None, None]
+    parent = jnp.where(keep, incoming[recv_source], 0.0)
     return (factor_rows[:, None], parent[:, None, :, None])
 
 

time: 631 us -> 623 us (0.987)
  other arithmetic: 219 us -> 212 us
    select_n x5 -> x4, other arithmetic: 16.1 us -> 8.09 us  [the longest x2 8 us: local(): parent = jnp.where(keep, incoming[recv_source], 0.0)]
where the time goes in v7:
time: 623 us; the launch traced here: 612 us
  waiting for transfers between devices  229 us (37%)
  other arithmetic  212 us (34%)
  local copies, waits for them, and re-layouts  57.1 us (9%)
  starting transfers between devices  46.9 us (8%)
  matrix products  46.4 us (7%)
  between operations  21.4 us (3%)
    another operation x34, other arithmetic, local(): aug_factor = lax.linalg.cholesky(aug, symmetrize_input=False)  195 us
    all_to_all x1, waiting for transfers between devices, local(): lax.all_to_all(outgoing, 'row', split_axis=0, concat_axis=0, tiled=True)  93.5 us
    all_gather x1, waiting for transfers between devices, local(): row_tiles = lax.all_gather(lead_tile, 'col')[:LEAD]  56.3 us
    another operation x16, matrix products, local(): aug_factor = lax.linalg.cholesky(aug, symmetrize_input=False)  26.8 us
    all_to_all x1, waiting for transfers between devices, local(): lax.all_to_all(panel_col, 'col', split_axis=0, concat_axis=0, tiled=True)  25.7 us
    ppermute x3, starting transfers between devices, local(): ring.append(lax.ppermute(mine, 'row', perm))  23.3 us
    ppermute x3, waiting for transfers between devices, local(): ring.append(lax.ppermute(mine, 'row', perm))  21.9 us
    dot_general x1, matrix products, local(): lax.dot_general(factor_rows.reshape(rows_dev * tile, lead_w), col_factor....  19.6 us
  transfers between devices with their start and end apart: 17, of which 10 were waited for; matrix products, arithmetic and copies ran while one was open for 3% of the time, Pallas kernels for 0%

profile of v7, /device:TPU:1, one launch (start us, length us, event | category | flops | bytes accessed | tf_op | source)
XLA Modules:
  0.0 612.5 jit_solution(6354192236598113050)
XLA Ops:
  9.0 56.3 %all-gather.8.cloned.1.call-done = f32[16,1,256,256]{3,2,1,0:T(8,128)} async-done(((f32[1,1,256,256]{3,2,1,0:T(8,128)}), f32[16,1,256,256]{3,2,1,0:T(8,128)}) %all-gather.8.cloned.1.call-update) | async-done | bytes 4194320 | tf_op jit(solution)/shard_map/all_gather | solution.py:69
  67.6 3.1 slice.191
  70.6 5.0 all-to-all-start
  77.0 25.7 %all-to-all-done = f32[16,128,256]{2,1,0:T(8,128)S(1)} async-done(((f32[16,128,256]{2,1,0:T(8,128)}), f32[16,128,256]{2,1,0:T(8,128)S(1)}, u32[]{:S(2)}, u32[]{:S(2)}) %all-to-all-start) | async-done | bytes 2097184 | tf_op jit(solution)/shard_map/all_to_all | solution.py:75
  104.2 13.3 %all-gather.12.cloned.1.call-done = f32[32,1,256,256]{3,2,1,0:T(8,128)} async-done(((f32[4,1,256,256]{3,2,1,0:T(8,128)}), f32[32,1,256,256]{3,2,1,0:T(8,128)}) %all-gather.12.cloned.1.call-update) | async-done | bytes 8388624 | tf_op jit(solution)/shard_map/all_gather | solution.py:70
  119.7 2.7 copy.15
  125.4 11.7 %cholesky.252 = f32[128,128]{1,0:T(8,128)S(1)} custom-call(f32[128,128]{1,0:T(8,128)S(1)} %cholesky.658), custom_call_target="Cholesky" | custom-call | tf_op jit(solution)/shard_map/cholesky | solution.py:92
  137.2 9.8 %custom-call.50 = f32[1,128,128]{1,2,0:T(8,128)S(1)} custom-call(f32[1,128,128]{2,1,0:T(8,128)S(1)} %get-tuple-element.55), custom_call_target="InvertDiagBlocksLowerTriangular" | custom-call | tf_op jit(solution)/shard_map/cholesky | solution.py:92
  147.0 3.0 cholesky.281
  155.1 11.7 %cholesky.274 = f32[128,128]{1,0:T(8,128)S(1)} custom-call(f32[128,128]{1,0:T(8,128)S(1)} %cholesky.662), custom_call_target="Cholesky" | custom-call | tf_op jit(solution)/shard_map/cholesky | solution.py:92
  167.4 9.8 %custom-call.51 = f32[1,128,128]{1,2,0:T(8,128)S(1)} custom-call(f32[1,128,128]{2,1,0:T(8,128)S(1)} %get-tuple-element.52), custom_call_target="InvertDiagBlocksLowerTriangular" | custom-call | tf_op jit(solution)/shard_map/cholesky | solution.py:92
  180.8 11.7 %cholesky.526 = f32[128,128]{1,0:T(8,128)S(1)} custom-call(f32[128,128]{1,0:T(8,128)S(1)} %cholesky.667), custom_call_target="Cholesky" | custom-call | tf_op jit(solution)/shard_map/cholesky | solution.py:92
  193.8 9.9 %custom-call.52 = f32[1,128,128]{1,2,0:T(8,128)S(1)} custom-call(f32[1,128,128]{2,1,0:T(8,128)S(1)} %get-tuple-element.49), custom_call_target="InvertDiagBlocksLowerTriangular" | custom-call | tf_op jit(solution)/shard_map/cholesky | solution.py:92
  205.0 2.6 convolution_subtract_fusion.2
  207.6 11.7 %cholesky.545 = f32[128,128]{1,0:T(8,128)S(1)} custom-call(f32[128,128]{1,0:T(8,128)S(1)} %cholesky.672), custom_call_target="Cholesky" | custom-call | tf_op jit(solution)/shard_map/cholesky | solution.py:92
  220.6 9.8 %custom-call.53 = f32[1,128,128]{1,2,0:T(8,128)S(1)} custom-call(f32[1,128,128]{2,1,0:T(8,128)S(1)} %get-tuple-element.46), custom_call_target="InvertDiagBlocksLowerTriangular" | custom-call | tf_op jit(solution)/shard_map/cholesky | solution.py:92
  231.6 2.6 fusion.4
  234.2 11.9 %cholesky.564 = f32[128,128]{1,0:T(8,128)S(1)} custom-call(f32[128,128]{1,0:T(8,128)S(1)} %cholesky.677), custom_call_target="Cholesky" | custom-call | tf_op jit(solution)/shard_map/cholesky | solution.py:92
  247.4 9.8 %custom-call.54 = f32[1,128,128]{1,2,0:T(8,128)S(1)} custom-call(f32[1,128,128]{2,1,0:T(8,128)S(1)} %get-tuple-element.43), custom_call_target="InvertDiagBlocksLowerTriangular" | custom-call | tf_op jit(solution)/shard_map/cholesky | solution.py:92
  258.3 2.6 fusion.10
  261.0 11.7 %cholesky.584 = f32[128,128]{1,0:T(8,128)S(1)} custom-call(f32[128,128]{1,0:T(8,128)S(1)} %cholesky.682), custom_call_target="Cholesky" | custom-call | tf_op jit(solution)/shard_map/cholesky | solution.py:92
  274.0 10.2 %custom-call.55 = f32[1,128,128]{1,2,0:T(8,128)S(1)} custom-call(f32[1,128,128]{2,1,0:T(8,128)S(1)} %get-tuple-element.40), custom_call_target="InvertDiagBlocksLowerTriangular" | custom-call | tf_op jit(solution)/shard_map/cholesky | solution.py:92
  285.2 2.5 fusion.13
  287.8 11.7 %cholesky.604 = f32[128,128]{1,0:T(8,128)S(1)} custom-call(f32[128,128]{1,0:T(8,128)S(1)} %cholesky.687), custom_call_target="Cholesky" | custom-call | tf_op jit(solution)/shard_map/cholesky | solution.py:92
  300.8 9.8 %custom-call.56 = f32[1,128,128]{1,2,0:T(8,128)S(1)} custom-call(f32[1,128,128]{2,1,0:T(8,128)S(1)} %get-tuple-element.37), custom_call_target="InvertDiagBlocksLowerTriangular" | custom-call | tf_op jit(solution)/shard_map/cholesky | solution.py:92
  313.8 11.8 %cholesky.624 = f32[128,128]{1,0:T(8,128)S(1)} custom-call(f32[128,128]{1,0:T(8,128)S(1)} %cholesky.692), custom_call_target="Cholesky" | custom-call | tf_op jit(solution)/shard_map/cholesky | solution.py:92
  326.9 9.8 %custom-call.57 = f32[1,128,128]{1,2,0:T(8,128)S(1)} custom-call(f32[1,128,128]{2,1,0:T(8,128)S(1)} %get-tuple-element.34), custom_call_target="InvertDiagBlocksLowerTriangular" | custom-call | tf_op jit(solution)/shard_map/cholesky | solution.py:92
  339.4 11.7 %cholesky.641 = f32[128,128]{1,0:T(8,128)S(1)} custom-call(f32[128,128]{1,0:T(8,128)S(1)} %convolution_subtract_fusion.4), custom_call_target="Cholesky" | custom-call | tf_op jit(solution)/shard_map/cholesky | solution.py:92
  358.7 2.9 select_select_fusion
  363.1 3.2 collective-permute-start
  369.8 3.0 collective-permute-done
  373.5 5.5 collective-permute-done.1
  382.1 2.4 constant_dynamic-update-slice_fusion.4
  384.5 5.3 collective-permute-start.8
  389.8 18.0 %collective-permute-start.9 = (f32[128,1024]{1,0:T(8,128)S(1)}, f32[128,1024]{1,0:T(8,128)S(1)}, u32[]{:S(2)}, u32[]{:S(2)}) collective-permute-start(f32[128,1024]{1,0:T(8,128)S(1)} %get-tuple-element.28), channel_id=1, source_target_pairs={{0,64},{16,80},{32,96},{48,112},{64,0},{80,16},{96,32},{112,48},{1... | collective-permute-start | bytes 1572872 | tf_op jit(solution)/shard_map/ppermute | solution.py:113
  407.8 9.5 %collective-permute-done.8 = f32[128,1024]{1,0:T(8,128)S(1)} collective-permute-done((f32[128,1024]{1,0:T(8,128)S(1)}, f32[128,1024]{1,0:T(8,128)S(1)}, u32[]{:S(2)}, u32[]{:S(2)}) %collective-permute-start.8) | collective-permute-done | bytes 524320 | tf_op jit(solution)/shard_map/ppermute | solution.py:113
  417.3 12.1 %collective-permute-done.9 = f32[128,1024]{1,0:T(8,128)S(1)} collective-permute-done((f32[128,1024]{1,0:T(8,128)S(1)}, f32[128,1024]{1,0:T(8,128)S(1)}, u32[]{:S(2)}, u32[]{:S(2)}) %collective-permute-start.9) | collective-permute-done | bytes 524320 | tf_op jit(solution)/shard_map/ppermute | solution.py:113
  430.0 2.4 collective-permute-start.11
  436.6 3.2 constant_dynamic-update-slice_fusion
  439.8 5.1 gather_fusion
  444.9 9.6 %all-gather.10.cloned.1.call-done = f32[2048,1024]{1,0:T(8,128)} async-done(((f32[128,1024]{1,0:T(8,128)}), f32[2048,1024]{1,0:T(8,128)}) %all-gather.10.cloned.1.call-update) | async-done | bytes 8388624 | tf_op jit(solution)/shard_map/all_gather | solution.py:98
  454.5 19.6 %bitcast_subtract_fusion = f32[8,4,256,256]{3,2,1,0:T(8,128)} fusion(f32[8,256,1024,1]{2,1,3,0:T(8,128)} %bitcast.98, f32[4,256,1024,1]{2,1,0,3:T(8,128)} %bitcast.100, f32[8,1,4,1,256,256]{5,4,3,2,1,0:T(8,128)} %param.4), kind=kOutput, calls=%fused_computation.4 | convolution fusion | flops 12886999040 | bytes 29360128 | tf_op jit(solution)/shard_map/dot_general | solution.py:123
  474.1 7.9 %gather_fusion.1 = f32[32,256,256]{2,1,0:T(8,128)} fusion(f32[32,256,256]{2,1,0:T(8,128)} %bitcast.97, s32[1024]{0:T(1024)S(1)} %pad_clamp_fusion.1), kind=kCustom, calls=%fused_computation.1 | custom fusion | bytes 16777344 | tf_op jit(solution)/shard_map/gather | solution.py:133
  481.9 5.8 all-to-all-start.1
  488.0 93.5 %all-to-all-done.1 = f32[8,4,256,256]{3,2,1,0:T(8,128)} async-done(((f32[8,4,256,256]{3,2,1,0:T(8,128)}), f32[8,4,256,256]{3,2,1,0:T(8,128)}, u32[]{:S(2)}, u32[]{:S(2)}) %all-to-all-start.1) | async-done | bytes 8388640 | tf_op jit(solution)/shard_map/all_to_all | solution.py:134
  581.4 7.9 %gather_fusion.2 = f32[8,4,256,256]{3,2,1,0:T(8,128)} fusion(f32[8,4,256,256]{3,2,1,0:T(8,128)} %all-to-all-done.1, s32[1024]{0:T(1024)S(1)} %pad_clamp_fusion), kind=kCustom, calls=%fused_computation.2 | custom fusion | bytes 16777248 | tf_op jit(solution)/shard_map/gather | solution.py:136
  589.3 8.0 %bitcast_select_fusion = f32[8,1,4,1,256,256]{5,4,3,2,1,0:T(8,128)} fusion(f32[8,4,256,256]{3,2,1,0:T(8,128)} %gather_fusion.2, pred[8,4]{1,0:T(8,128)(4,1)S(1)} %broadcast_and_fusion), kind=kLoop, calls=%fused_computation.3 | loop fusion | flops 2097152 | bytes 16777248 | tf_op jit(solution)/shard_map/jit(_where)/select_n | solution.py:136
  597.3 8.4 %copy.42 = f32[8,1,256,1024]{3,2,1,0:T(8,128)} copy(f32[8,1,256,1024]{3,2,1,0:T(8,128)} %bitcast.99) | data formatting | bytes 16777216
  (111 shorter events, 53.7 us)
Async XLA Ops:
  7.2 58.1 %all-gather.8.cloned.1.call-start = ((), (), s32[]{:S(2)}) async-start(), calls=%async_computation.2 | async-start | bytes 4456448 | tf_op jit(solution)/shard_map/all_gather | solution.py:69
  8.9 66.8 %copy-start.5 = (s32[60]{0:T(128)S(1)}, s32[60]{0:T(128)}, u32[]{:S(2)}) copy-start(s32[60]{0:T(128)} %param.5) | copy-start | bytes 724
  8.9 108.6 %all-gather.12.cloned.1.call-start = ((), (), s32[]{:S(2)}) async-start(), calls=%async_computation.4 | async-start | bytes 9437184 | tf_op jit(solution)/shard_map/all_gather | solution.py:70
  70.6 32.1 %all-to-all-start = ((f32[16,128,256]{2,1,0:T(8,128)}), f32[16,128,256]{2,1,0:T(8,128)S(1)}, u32[]{:S(2)}, u32[]{:S(2)}) async-start(f32[16,128,256]{2,1,0:T(8,128)} %bitcast.3), calls=%async_computation | async-start | bytes 4194304 | tf_op jit(solution)/shard_map/all_to_all | solution.py:75
  75.6 378.9 %all-gather.10.cloned.1.call-start = ((), (), s32[]{:S(2)}) async-start(), calls=%async_computation.3 | async-start | bytes 8912896 | tf_op jit(solution)/shard_map/all_gather | solution.py:98
  117.5 2.2 slice-start
  123.4 2.0 copy-start
  147.0 4.1 copy-start.1
  151.6 2.5 copy-start.2
  362.2 45.6 %copy-start.4 = (s32[60]{0:T(128)S(1)}, s32[60]{0:T(128)}, u32[]{:S(2)}) copy-start(s32[60]{0:T(128)} %param.6) | copy-start | bytes 724
  362.2 45.6 %copy-start.6 = (s32[60]{0:T(128)S(1)}, s32[60]{0:T(128)}, u32[]{:S(2)}) copy-start(s32[60]{0:T(128)} %param.7) | copy-start | bytes 724
  363.1 9.6 %collective-permute-start = (f32[128,1024]{1,0:T(8,128)}, f32[128,1024]{1,0:T(8,128)S(1)}, u32[]{:S(2)}, u32[]{:S(2)}) collective-permute-start(f32[128,1024]{1,0:T(8,128)} %slice_select_fusion), channel_id=1, source_target_pairs={{0,0},{16,17},{32,34},{48,51},{64,68},{80,85},{96,102},{112,119},{... | collective-permute-start | bytes 1572872 | tf_op jit(solution)/shard_map/ppermute | solution.py:108
  366.4 12.6 %collective-permute-start.1 = (f32[128,1024]{1,0:T(8,128)}, f32[128,1024]{1,0:T(8,128)S(1)}, u32[]{:S(2)}, u32[]{:S(2)}) collective-permute-start(f32[128,1024]{1,0:T(8,128)} %slice_select_fusion), channel_id=1, source_target_pairs={{1,16},{17,33},{33,50},{49,67},{65,84},{81,101},{97,118},{113,7},{... | collective-permute-start | bytes 1572872 | tf_op jit(solution)/shard_map/ppermute | solution.py:108
  367.7 12.9 %collective-permute-start.2 = (f32[128,1024]{1,0:T(8,128)}, f32[128,1024]{1,0:T(8,128)S(1)}, u32[]{:S(2)}, u32[]{:S(2)}) collective-permute-start(f32[128,1024]{1,0:T(8,128)} %slice_select_fusion), channel_id=1, source_target_pairs={{4,32},{20,49},{36,66},{52,83},{68,100},{84,117},{100,6},{116,23},... | collective-permute-start | bytes 1572872 | tf_op jit(solution)/shard_map/ppermute | solution.py:108
  368.4 13.7 %collective-permute-start.3 = (f32[128,1024]{1,0:T(8,128)}, f32[128,1024]{1,0:T(8,128)S(1)}, u32[]{:S(2)}, u32[]{:S(2)}) collective-permute-start(f32[128,1024]{1,0:T(8,128)} %slice_select_fusion), channel_id=1, source_target_pairs={{5,48},{21,65},{37,82},{53,99},{69,116},{85,5},{101,22},{117,39},{... | collective-permute-start | bytes 1572872 | tf_op jit(solution)/shard_map/ppermute | solution.py:108
  369.1 13.0 %collective-permute-start.4 = (f32[128,1024]{1,0:T(8,128)}, f32[128,1024]{1,0:T(8,128)S(1)}, u32[]{:S(2)}, u32[]{:S(2)}) collective-permute-start(f32[128,1024]{1,0:T(8,128)} %slice_select_fusion), channel_id=1, source_target_pairs={{8,64},{24,81},{40,98},{56,115},{72,4},{88,21},{104,38},{120,55},{... | collective-permute-start | bytes 1572872 | tf_op jit(solution)/shard_map/ppermute | solution.py:108
  372.8 9.3 %collective-permute-start.5 = (f32[128,1024]{1,0:T(8,128)}, f32[128,1024]{1,0:T(8,128)S(1)}, u32[]{:S(2)}, u32[]{:S(2)}) collective-permute-start(f32[128,1024]{1,0:T(8,128)} %slice_select_fusion), channel_id=1, source_target_pairs={{9,80},{25,97},{41,114},{57,3},{73,20},{89,37},{105,54},{121,71},{... | collective-permute-start | bytes 1572872 | tf_op jit(solution)/shard_map/ppermute | solution.py:108
  379.0 3.1 collective-permute-start.6
  380.5 1.6 collective-permute-start.7
  384.5 32.8 %collective-permute-start.8 = (f32[128,1024]{1,0:T(8,128)S(1)}, f32[128,1024]{1,0:T(8,128)S(1)}, u32[]{:S(2)}, u32[]{:S(2)}) collective-permute-start(f32[128,1024]{1,0:T(8,128)S(1)} %get-tuple-element.28), channel_id=1, source_target_pairs={{0,32},{16,48},{32,64},{48,80},{64,96},{80,112},{96,0},{112,16},{1... | collective-permute-start | bytes 1572872 | tf_op jit(solution)/shard_map/ppermute | solution.py:113
  389.8 39.7 %collective-permute-start.9 = (f32[128,1024]{1,0:T(8,128)S(1)}, f32[128,1024]{1,0:T(8,128)S(1)}, u32[]{:S(2)}, u32[]{:S(2)}) collective-permute-start(f32[128,1024]{1,0:T(8,128)S(1)} %get-tuple-element.28), channel_id=1, source_target_pairs={{0,64},{16,80},{32,96},{48,112},{64,0},{80,16},{96,32},{112,48},{1... | collective-permute-start | bytes 1572872 | tf_op jit(solution)/shard_map/ppermute | solution.py:113
  407.8 22.0 %collective-permute-start.10 = (f32[128,1024]{1,0:T(8,128)S(1)}, f32[128,1024]{1,0:T(8,128)S(1)}, u32[]{:S(2)}, u32[]{:S(2)}) collective-permute-start(f32[128,1024]{1,0:T(8,128)S(1)} %get-tuple-element.28), channel_id=1, source_target_pairs={{0,96},{16,112},{32,0},{48,16},{64,32},{80,48},{96,64},{112,80},{1... | collective-permute-start | bytes 1572872 | tf_op jit(solution)/shard_map/ppermute | solution.py:113
  429.7 2.6 copy-start.3
  430.0 6.7 %collective-permute-start.11 = (f32[4,128,1024]{2,1,0:T(8,128)S(1)}, f32[4,128,1024]{2,1,0:T(8,128)}, u32[]{:S(2)}, u32[]{:S(2)}) collective-permute-start(f32[4,128,1024]{2,1,0:T(8,128)S(1)} %pad_maximum_fusion), channel_id=1, source_target_pairs={{0,16},{16,0},{32,48},{48,32},{64,80},{80,64},{96,112},{112,96},{1... | collective-permute-start | bytes 6291464 | tf_op jit(solution)/shard_map/ppermute | solution.py:115
  481.9 99.5 %all-to-all-start.1 = ((f32[8,4,256,256]{3,2,1,0:T(8,128)}), f32[8,4,256,256]{3,2,1,0:T(8,128)}, u32[]{:S(2)}, u32[]{:S(2)}) async-start(f32[8,4,256,256]{3,2,1,0:T(8,128)} %bitcast.92), calls=%async_computation.1 | async-start | bytes 16777216 | tf_op jit(solution)/shard_map/all_to_all | solution.py:134
Sparse Core Ops, SparseCore 0:
  10.7 54.5 all-gather.7
  67.7 49.7 all-gather.11
  363.3 91.1 all-gather.9

commit v8 on v7

--- a/solution.py
+++ b/solution.py
@@ -5,6 +5,7 @@
 
 LEAD = 4
 SCHUR_PRECISION = lax.Precision.HIGH
+PRECISE = lax.Precision.HIGHEST
 
 
 def valid_gain(valid_flags, ndims):
@@ -17,6 +18,31 @@
     incoming = lax.all_to_all(outgoing, "row", split_axis=0, concat_axis=0, tiled=True)
     incoming = incoming.reshape((-1,) + block_now.shape[1:])
     return jnp.take(incoming, recv_source, axis=0) * valid_gain(recv_valid, block_now.ndim)
+
+
+def column_gather(piece, my_row, my_col, grid_rows, grid_cols):
+    src_row = my_col % grid_rows
+    mine = None
+    for j in range(grid_rows):
+        perm = []
+        for c in range(grid_cols):
+            s = c % grid_rows
+            source_col = 4 * (j // 2) + 2 * (c // grid_rows) + j % 2
+            perm.append((s * grid_cols + source_col, ((s + j) % grid_rows) * grid_cols + c))
+        moved = lax.ppermute(piece, ("row", "col"), perm)
+        mine = moved if mine is None else mine + moved
+    ring = [mine]
+    for step in range(1, grid_rows // 2):
+        perm = [(i, (i + 2 * step) % grid_rows) for i in range(grid_rows)]
+        ring.append(lax.ppermute(mine, "row", perm))
+    ring = jnp.stack(ring)
+    partner = lax.ppermute(ring, "row", [(i, i ^ 1) for i in range(grid_rows)])
+    combined = jnp.concatenate([ring, partner], axis=0)
+    chunk_ids = jnp.arange(grid_rows, dtype=jnp.int32)
+    own_d = (my_row - src_row - chunk_ids) % grid_rows
+    par_d = ((my_row ^ 1) - src_row - chunk_ids) % grid_rows
+    pos = jnp.where(own_d % 2 == 0, own_d // 2, grid_rows // 2 + par_d // 2)
+    return combined[pos].reshape(grid_rows * piece.shape[0], piece.shape[1])
 
 
 def local(front, tile_live, row_target, col_target):
@@ -81,44 +107,34 @@
         1,
     ).astype(jnp.float32)
     masked = panel_rows * live
-    bound = 1.0 + 10.0 * jnp.sum(masked * masked)
-    aug = jnp.concatenate(
-        [
-            jnp.concatenate([lead_block, jnp.zeros((lead_w, half), jnp.float32)], axis=1),
-            jnp.concatenate([masked, jnp.where(jnp.eye(half, dtype=jnp.bool_), bound, 0.0)], axis=1),
-        ],
-        axis=0,
-    )
-    aug_factor = lax.linalg.cholesky(aug, symmetrize_input=False)
-    chol = aug_factor[:lead_w, :lead_w]
-    solved = aug_factor[lead_w:, :lead_w]
-    start = jnp.clip(my_tile_row * tile + (my_col % 2) * half, 0, lead_w - half)
-    chol_rows = lax.dynamic_slice(chol, (start, 0), (half, lead_w))
-    piece = jnp.where(my_tile_row < LEAD, chol_rows, solved)
-    factor_rows = lax.all_gather(piece, "col").reshape(rows_dev, tile, lead_w)
-
-    src_row = my_col % grid_rows
-    mine = None
-    for j in range(grid_rows):
-        perm = []
-        for c in range(grid_cols):
-            s = c % grid_rows
-            source_col = 4 * (j // 2) + 2 * (c // grid_rows) + j % 2
-            perm.append((s * grid_cols + source_col, ((s + j) % grid_rows) * grid_cols + c))
-        moved = lax.ppermute(piece, ("row", "col"), perm)
-        mine = moved if mine is None else mine + moved
-    ring = [mine]
-    for step in range(1, grid_rows // 2):
-        perm = [(i, (i + 2 * step) % grid_rows) for i in range(grid_rows)]
-        ring.append(lax.ppermute(mine, "row", perm))
-    ring = jnp.stack(ring)
-    partner = lax.ppermute(ring, "row", [(i, i ^ 1) for i in range(grid_rows)])
-    combined = jnp.concatenate([ring, partner], axis=0)
-    chunk_ids = jnp.arange(grid_rows, dtype=jnp.int32)
-    own_d = (my_row - src_row - chunk_ids) % grid_rows
-    par_d = ((my_row ^ 1) - src_row - chunk_ids) % grid_rows
-    pos = jnp.where(own_d % 2 == 0, own_d // 2, grid_rows // 2 + par_d // 2)
-    col_factor = combined[pos].reshape(cols_dev, tile, lead_w)
+    block = 128
+    groups = 4
+    steps = lead_w // block
+    work = jnp.concatenate([lead_block, masked], axis=0)
+    row_start = jnp.clip(my_tile_row * tile + (my_col % 2) * half, 0, lead_w - half)
+    use_chol = my_tile_row < LEAD
+    blocks = []
+    row_parts = []
+    col_parts = []
+    for k in range(steps):
+        lo = k * block
+        diag = lax.linalg.cholesky(work[lo:lo + block, lo:lo + block], symmetrize_input=False)
+        below = lax.linalg.triangular_solve(
+            diag, work[lo + block:, lo:lo + block], left_side=False, lower=True, transpose_a=True
+        )
+        if k + 1 < steps:
+            upd = jnp.dot(below, below[: lead_w - lo - block].T, precision=PRECISE)
+            work = work.at[lo + block:, lo + block:lead_w].add(-upd)
+        column = jnp.concatenate([jnp.zeros((lo, block), jnp.float32), diag, below], axis=0)
+        chol_rows = lax.dynamic_slice(column, (row_start, 0), (half, block))
+        blocks.append(jnp.where(use_chol, chol_rows, column[lead_w:]))
+        if (k + 1) % (steps // groups) == 0:
+            piece = jnp.concatenate(blocks, axis=1)
+            blocks = []
+            row_parts.append(lax.all_gather(piece, "col").reshape(rows_dev * tile, -1))
+            col_parts.append(column_gather(piece, my_row, my_col, grid_rows, grid_cols))
+    factor_rows = jnp.concatenate(row_parts, axis=1).reshape(rows_dev, tile, lead_w)
+    col_factor = jnp.concatenate(col_parts, axis=1).reshape(cols_dev, tile, lead_w)
 
     prod = lax.dot_general(
         factor_rows.reshape(rows_dev * tile, lead_w),

time: 623 us -> 627 us (level)
  the two profiles are of different devices: /device:TPU:1 before, /device:TPU:8 now
where the time goes in v8:
time: 627 us; the launch traced here: 616 us
  other arithmetic  218 us (35%)
  waiting for transfers between devices  195 us (31%)
  starting transfers between devices  90.8 us (14%)
  local copies, waits for them, and re-layouts  56.6 us (9%)
  matrix products  39.5 us (6%)
  between operations  16.4 us (3%)
    another operation x24, other arithmetic, local(): lax.linalg.cholesky(work[lo:lo + block, lo:lo + block], symmetrize_input=...  99.6 us
    all_to_all x1, waiting for transfers between devices, local(): lax.all_to_all(outgoing, 'row', split_axis=0, concat_axis=0, tiled=True)  88.6 us
    another operation x16, other arithmetic, local(): lax.linalg.triangular_solve(diag, work[lo + block:, lo:lo + block], left_...  83.7 us
    all_gather x1, waiting for transfers between devices, local(): row_tiles = lax.all_gather(lead_tile, 'col')[:LEAD]  55.6 us
    ppermute x12, starting transfers between devices, column_gather(): ring.append(lax.ppermute(mine, 'row', perm))  42.7 us
    ppermute x32, starting transfers between devices, column_gather(): moved = lax.ppermute(piece, ('row', 'col'), perm)  35.9 us
    all_to_all x1, waiting for transfers between devices, local(): lax.all_to_all(panel_col, 'col', split_axis=0, concat_axis=0, tiled=True)  25.5 us
    dot_general x1, matrix products, local(): lax.dot_general(factor_rows.reshape(rows_dev * tile, lead_w), col_factor....  17.8 us
  transfers between devices with their start and end apart: 56, of which 9 were waited for; matrix products, arithmetic and copies ran while one was open for 29% of the time, Pallas kernels for 0%

profile of v8, /device:TPU:8, one launch (start us, length us, event | category | flops | bytes accessed | tf_op | source)
XLA Modules:
  0.0 616.2 jit_solution(2616083737845075528)
XLA Ops:
  9.0 55.6 %all-gather.14.cloned.1.call-done = f32[16,1,256,256]{3,2,1,0:T(8,128)} async-done(((f32[1,1,256,256]{3,2,1,0:T(8,128)}), f32[16,1,256,256]{3,2,1,0:T(8,128)}) %all-gather.14.cloned.1.call-update) | async-done | bytes 4194320 | tf_op jit(solution)/shard_map/all_gather | solution.py:95
  64.5 2.3 slice.367
  66.8 3.1 slice.370
  69.9 5.7 all-to-all-start
  77.1 25.5 %all-to-all-done = f32[16,128,256]{2,1,0:T(8,128)S(1)} async-done(((f32[16,128,256]{2,1,0:T(8,128)}), f32[16,128,256]{2,1,0:T(8,128)S(1)}, u32[]{:S(2)}, u32[]{:S(2)}) %all-to-all-start) | async-done | bytes 2097184 | tf_op jit(solution)/shard_map/all_to_all | solution.py:101
  102.7 13.5 %all-gather.24.cloned.1.call-done = f32[32,1,256,256]{3,2,1,0:T(8,128)} async-done(((f32[4,1,256,256]{3,2,1,0:T(8,128)}), f32[32,1,256,256]{3,2,1,0:T(8,128)}) %all-gather.24.cloned.1.call-update) | async-done | bytes 8388624 | tf_op jit(solution)/shard_map/all_gather | solution.py:96
  116.2 2.2 slice-done
  118.4 2.7 copy.27
  122.1 2.3 constant_dynamic-update-slice_fusion.1
  124.4 11.7 %custom-call.42 = f32[128,128]{1,0:T(8,128)S(1)} custom-call(f32[128,128]{1,0:T(8,128)S(1)} %slice.369), custom_call_target="Cholesky" | custom-call | tf_op jit(solution)/shard_map/cholesky/custom-call.1 | solution.py:121
  137.5 9.8 %custom-call.27 = f32[1,128,128]{1,2,0:T(8,128)S(1)} custom-call(f32[1,128,128]{2,1,0:T(8,128)S(1)} %get-tuple-element.126), custom_call_target="InvertDiagBlocksLowerTriangular" | custom-call | tf_op jit(solution)/shard_map/triangular_solve | solution.py:122
  149.7 5.6 slice_add_fusion
  155.3 1.8 copy-done
  157.2 11.7 %custom-call.43 = f32[128,128]{1,0:T(8,128)S(1)} custom-call(f32[128,128]{1,0:T(8,128)S(1)} %slice.375), custom_call_target="Cholesky" | custom-call | tf_op jit(solution)/shard_map/cholesky/custom-call.1 | solution.py:121
  170.2 9.8 %custom-call.28 = f32[1,128,128]{1,2,0:T(8,128)S(1)} custom-call(f32[1,128,128]{2,1,0:T(8,128)S(1)} %get-tuple-element.124), custom_call_target="InvertDiagBlocksLowerTriangular" | custom-call | tf_op jit(solution)/shard_map/triangular_solve | solution.py:122
  183.0 4.1 slice_add_fusion.1
  187.1 11.7 %custom-call.44 = f32[128,128]{1,0:T(8,128)S(1)} custom-call(f32[128,128]{1,0:T(8,128)S(1)} %slice.379), custom_call_target="Cholesky" | custom-call | tf_op jit(solution)/shard_map/cholesky/custom-call.1 | solution.py:121
  200.2 9.8 %custom-call.29 = f32[1,128,128]{1,2,0:T(8,128)S(1)} custom-call(f32[1,128,128]{2,1,0:T(8,128)S(1)} %get-tuple-element.122), custom_call_target="InvertDiagBlocksLowerTriangular" | custom-call | tf_op jit(solution)/shard_map/triangular_solve | solution.py:122
  213.5 11.9 %custom-call.45 = f32[128,128]{1,0:T(8,128)S(1)} custom-call(f32[128,128]{1,0:T(8,128)S(1)} %slice.383), custom_call_target="Cholesky" | custom-call | tf_op jit(solution)/shard_map/cholesky/custom-call.1 | solution.py:121
  226.7 9.8 %custom-call.30 = f32[1,128,128]{1,2,0:T(8,128)S(1)} custom-call(f32[1,128,128]{2,1,0:T(8,128)S(1)} %get-tuple-element.120), custom_call_target="InvertDiagBlocksLowerTriangular" | custom-call | tf_op jit(solution)/shard_map/triangular_solve | solution.py:122
  239.3 2.6 fusion.15
  241.9 11.7 %custom-call.46 = f32[128,128]{1,0:T(8,128)S(1)} custom-call(f32[128,128]{1,0:T(8,128)S(1)} %slice.387), custom_call_target="Cholesky" | custom-call | tf_op jit(solution)/shard_map/cholesky/custom-call.1 | solution.py:121
  254.9 9.8 %custom-call.31 = f32[1,128,128]{1,2,0:T(8,128)S(1)} custom-call(f32[1,128,128]{2,1,0:T(8,128)S(1)} %get-tuple-element.118), custom_call_target="InvertDiagBlocksLowerTriangular" | custom-call | tf_op jit(solution)/shard_map/triangular_solve | solution.py:122
  265.9 12.1 %custom-call.47 = f32[128,128]{1,0:T(8,128)S(1)} custom-call(f32[128,128]{1,0:T(8,128)S(1)} %slice.391), custom_call_target="Cholesky" | custom-call | tf_op jit(solution)/shard_map/cholesky/custom-call.1 | solution.py:121
  279.4 9.8 %custom-call.32 = f32[1,128,128]{1,2,0:T(8,128)S(1)} custom-call(f32[1,128,128]{2,1,0:T(8,128)S(1)} %get-tuple-element.116), custom_call_target="InvertDiagBlocksLowerTriangular" | custom-call | tf_op jit(solution)/shard_map/triangular_solve | solution.py:122
  293.0 7.0 %collective-permute-start.2 = (f32[128,256]{1,0:T(8,128)S(1)}, f32[128,256]{1,0:T(8,128)S(1)}, u32[]{:S(2)}, u32[]{:S(2)}) collective-permute-start(f32[128,256]{1,0:T(8,128)S(1)} %copy-done.6), channel_id=1, source_target_pairs={{4,32},{20,49},{36,66},{52,83},{68,100},{84,117},{100,6},{116,23},... | collective-permute-start | bytes 393224 | tf_op jit(solution)/shard_map/ppermute | solution.py:32
  302.5 11.7 %custom-call.48 = f32[128,128]{1,0:T(8,128)S(1)} custom-call(f32[128,128]{1,0:T(8,128)S(1)} %slice.395), custom_call_target="Cholesky" | custom-call | tf_op jit(solution)/shard_map/cholesky/custom-call.1 | solution.py:121
  315.6 9.8 %custom-call.33 = f32[1,128,128]{1,2,0:T(8,128)S(1)} custom-call(f32[1,128,128]{2,1,0:T(8,128)S(1)} %get-tuple-element.114), custom_call_target="InvertDiagBlocksLowerTriangular" | custom-call | tf_op jit(solution)/shard_map/triangular_solve | solution.py:122
  325.9 11.7 %custom-call.49 = f32[128,128]{1,0:T(8,128)S(1)} custom-call(f32[128,128]{1,0:T(8,128)S(1)} %slice.399), custom_call_target="Cholesky" | custom-call | tf_op jit(solution)/shard_map/cholesky/custom-call.1 | solution.py:121
  341.9 9.8 %custom-call.34 = f32[1,128,128]{1,2,0:T(8,128)S(1)} custom-call(f32[1,128,128]{2,1,0:T(8,128)S(1)} %get-tuple-element.112), custom_call_target="InvertDiagBlocksLowerTriangular" | custom-call | tf_op jit(solution)/shard_map/triangular_solve | solution.py:122
  352.4 4.3 collective-permute-start.14
  362.3 4.4 collective-permute-done.16
  374.4 5.3 collective-permute-done.28
  386.9 22.0 %collective-permute-start.8 = (f32[128,256]{1,0:T(8,128)S(1)}, f32[128,256]{1,0:T(8,128)S(1)}, u32[]{:S(2)}, u32[]{:S(2)}) collective-permute-start(f32[128,256]{1,0:T(8,128)S(1)} %get-tuple-element.105), channel_id=1, source_target_pairs={{0,32},{16,48},{32,64},{48,80},{64,96},{80,112},{96,0},{112,16},{1... | collective-permute-start | bytes 393224 | tf_op jit(solution)/shard_map/ppermute | solution.py:37
  410.0 2.8 collective-permute-start.10
  412.8 6.9 %collective-permute-start.20 = (f32[128,256]{1,0:T(8,128)S(1)}, f32[128,256]{1,0:T(8,128)S(1)}, u32[]{:S(2)}, u32[]{:S(2)}) collective-permute-start(f32[128,256]{1,0:T(8,128)S(1)} %get-tuple-element.107), channel_id=1, source_target_pairs={{0,32},{16,48},{32,64},{48,80},{64,96},{80,112},{96,0},{112,16},{1... | collective-permute-start | bytes 393224 | tf_op jit(solution)/shard_map/ppermute | solution.py:37
  419.7 2.7 collective-permute-start.22
  422.5 3.0 collective-permute-start.33
  429.9 1.7 collective-permute-start.46
  446.2 17.8 %fusion = f32[2048,1024]{1,0:T(8,128)} fusion(f32[2048,256]{1,0:T(8,128)} %all-gather.22.cloned.1.call-done, f32[2048,256]{1,0:T(8,128)} %all-gather.20.cloned.1.call-done, f32[2048,256]{1,0:T(8,128)} %all-gather.18.cloned.1.call-done, f32[2048,256]{1,0:T(8,128)} %all-gather.16.cloned.1.call-done, f32[1024,256]{1,0:T(8,128)S(1)} %bitcast.139, ...), kind=kOutput, calls=%fused_computation.7 | convolution fusion | flops 12894339072 | bytes 20971520 | tf_op jit(solution)/shard_map/dot_general | solution.py:139
  464.0 10.5 %reshape.711 = f32[8,256,4,256]{3,2,1,0:T(4,128)} reshape(f32[2048,1024]{1,0:T(8,128)} %fusion) | data formatting | bytes 16777216 | tf_op jit(solution)/shard_map/reshape | solution.py:145
  474.5 11.3 %bitcast_subtract_fusion = f32[8,4,256,256]{3,2,1,0:T(8,128)} fusion(f32[8,256,4,256]{3,2,1,0:T(4,128)} %reshape.711, f32[8,1,4,1,256,256]{5,4,3,2,1,0:T(8,128)} %param.19), kind=kLoop, calls=%fused_computation.16 | loop fusion | flops 2097152 | bytes 25165824 | tf_op jit(solution)/shard_map/sub | solution.py:146
  485.9 7.7 %gather_fusion.4 = f32[32,256,256]{2,1,0:T(8,128)} fusion(f32[32,256,256]{2,1,0:T(8,128)} %bitcast.123, s32[1024]{0:T(1024)S(1)} %pad_clamp_fusion.1), kind=kCustom, calls=%fused_computation.4 | custom fusion | bytes 16777344 | tf_op jit(solution)/shard_map/gather | solution.py:149
  493.6 5.1 all-to-all-start.1
  498.8 5.9 pad_maximum_fusion
  504.7 88.6 %all-to-all-done.1 = f32[8,4,256,256]{3,2,1,0:T(8,128)} async-done(((f32[8,4,256,256]{3,2,1,0:T(8,128)}), f32[8,4,256,256]{3,2,1,0:T(8,128)}, u32[]{:S(2)}, u32[]{:S(2)}) %all-to-all-start.1) | async-done | bytes 8388640 | tf_op jit(solution)/shard_map/all_to_all | solution.py:150
  593.3 7.9 %gather_fusion.5 = f32[8,4,256,256]{3,2,1,0:T(8,128)} fusion(f32[8,4,256,256]{3,2,1,0:T(8,128)} %all-to-all-done.1, s32[1024]{0:T(1024)S(1)} %pad_clamp_fusion), kind=kCustom, calls=%fused_computation.5 | custom fusion | bytes 16777248 | tf_op jit(solution)/shard_map/gather | solution.py:152
  601.1 8.0 %bitcast_select_fusion = f32[8,1,4,1,256,256]{5,4,3,2,1,0:T(8,128)} fusion(f32[8,4,256,256]{3,2,1,0:T(8,128)} %gather_fusion.5, pred[8,4]{1,0:T(8,128)(4,1)S(1)} %broadcast_and_fusion), kind=kLoop, calls=%fused_computation.15 | loop fusion | flops 2097152 | bytes 16777248 | tf_op jit(solution)/shard_map/jit(_where)/select_n | solution.py:152
  (256 shorter events, 77.3 us)
Async XLA Ops:
  7.2 57.4 %all-gather.14.cloned.1.call-start = ((), (), s32[]{:S(2)}) async-start(), calls=%async_computation.2 | async-start | bytes 4456448 | tf_op jit(solution)/shard_map/all_gather | solution.py:95
  8.9 107.3 %all-gather.24.cloned.1.call-start = ((), (), s32[]{:S(2)}) async-start(), calls=%async_computation.7 | async-start | bytes 9437184 | tf_op jit(solution)/shard_map/all_gather | solution.py:96
  69.9 32.7 %all-to-all-start = ((f32[16,128,256]{2,1,0:T(8,128)}), f32[16,128,256]{2,1,0:T(8,128)S(1)}, u32[]{:S(2)}, u32[]{:S(2)}) async-start(f32[16,128,256]{2,1,0:T(8,128)} %bitcast.3), calls=%async_computation | async-start | bytes 4194304 | tf_op jit(solution)/shard_map/all_to_all | solution.py:101
  75.6 370.4 %all-gather.16.cloned.1.call-start = ((), (), s32[]{:S(2)}) async-start(), calls=%async_computation.3 | async-start | bytes 2228224 | tf_op jit(solution)/shard_map/all_gather | solution.py:134
  182.4 263.7 %all-gather.18.cloned.1.call-start = ((), (), s32[]{:S(2)}) async-start(), calls=%async_computation.4 | async-start | bytes 2228224 | tf_op jit(solution)/shard_map/all_gather | solution.py:134
  238.8 207.4 %all-gather.20.cloned.1.call-start = ((), (), s32[]{:S(2)}) async-start(), calls=%async_computation.5 | async-start | bytes 2228224 | tf_op jit(solution)/shard_map/all_gather | solution.py:134
  290.3 155.8 %all-gather.22.cloned.1.call-start = ((), (), s32[]{:S(2)}) async-start(), calls=%async_computation.6 | async-start | bytes 2228224 | tf_op jit(solution)/shard_map/all_gather | solution.py:134
  291.7 46.7 %collective-permute-start = (f32[128,256]{1,0:T(8,128)S(1)}, f32[128,256]{1,0:T(8,128)S(1)}, u32[]{:S(2)}, u32[]{:S(2)}) collective-permute-start(f32[128,256]{1,0:T(8,128)S(1)} %copy-done.6), channel_id=1, source_target_pairs={{0,0},{16,17},{32,34},{48,51},{64,68},{80,85},{96,102},{112,119},{... | collective-permute-start | bytes 393224 | tf_op jit(solution)/shard_map/ppermute | solution.py:32
  292.4 46.6 %collective-permute-start.1 = (f32[128,256]{1,0:T(8,128)S(1)}, f32[128,256]{1,0:T(8,128)S(1)}, u32[]{:S(2)}, u32[]{:S(2)}) collective-permute-start(f32[128,256]{1,0:T(8,128)S(1)} %copy-done.6), channel_id=1, source_target_pairs={{1,16},{17,33},{33,50},{49,67},{65,84},{81,101},{97,118},{113,7},{... | collective-permute-start | bytes 393224 | tf_op jit(solution)/shard_map/ppermute | solution.py:32
  293.0 46.7 %collective-permute-start.2 = (f32[128,256]{1,0:T(8,128)S(1)}, f32[128,256]{1,0:T(8,128)S(1)}, u32[]{:S(2)}, u32[]{:S(2)}) collective-permute-start(f32[128,256]{1,0:T(8,128)S(1)} %copy-done.6), channel_id=1, source_target_pairs={{4,32},{20,49},{36,66},{52,83},{68,100},{84,117},{100,6},{116,23},... | collective-permute-start | bytes 393224 | tf_op jit(solution)/shard_map/ppermute | solution.py:32
  300.0 40.4 %collective-permute-start.3 = (f32[128,256]{1,0:T(8,128)S(1)}, f32[128,256]{1,0:T(8,128)S(1)}, u32[]{:S(2)}, u32[]{:S(2)}) collective-permute-start(f32[128,256]{1,0:T(8,128)S(1)} %copy-done.6), channel_id=1, source_target_pairs={{5,48},{21,65},{37,82},{53,99},{69,116},{85,5},{101,22},{117,39},{... | collective-permute-start | bytes 393224 | tf_op jit(solution)/shard_map/ppermute | solution.py:32
  300.7 51.0 %collective-permute-start.4 = (f32[128,256]{1,0:T(8,128)S(1)}, f32[128,256]{1,0:T(8,128)S(1)}, u32[]{:S(2)}, u32[]{:S(2)}) collective-permute-start(f32[128,256]{1,0:T(8,128)S(1)} %copy-done.6), channel_id=1, source_target_pairs={{8,64},{24,81},{40,98},{56,115},{72,4},{88,21},{104,38},{120,55},{... | collective-permute-start | bytes 393224 | tf_op jit(solution)/shard_map/ppermute | solution.py:32
  338.3 14.1 %collective-permute-start.5 = (f32[128,256]{1,0:T(8,128)S(1)}, f32[128,256]{1,0:T(8,128)S(1)}, u32[]{:S(2)}, u32[]{:S(2)}) collective-permute-start(f32[128,256]{1,0:T(8,128)S(1)} %copy-done.6), channel_id=1, source_target_pairs={{9,80},{25,97},{41,114},{57,3},{73,20},{89,37},{105,54},{121,71},{... | collective-permute-start | bytes 393224 | tf_op jit(solution)/shard_map/ppermute | solution.py:32
  339.0 17.7 %collective-permute-start.6 = (f32[128,256]{1,0:T(8,128)S(1)}, f32[128,256]{1,0:T(8,128)S(1)}, u32[]{:S(2)}, u32[]{:S(2)}) collective-permute-start(f32[128,256]{1,0:T(8,128)S(1)} %copy-done.6), channel_id=1, source_target_pairs={{12,96},{28,113},{44,2},{60,19},{76,36},{92,53},{108,70},{124,87},... | collective-permute-start | bytes 393224 | tf_op jit(solution)/shard_map/ppermute | solution.py:32
  339.7 17.7 %collective-permute-start.7 = (f32[128,256]{1,0:T(8,128)S(1)}, f32[128,256]{1,0:T(8,128)S(1)}, u32[]{:S(2)}, u32[]{:S(2)}) collective-permute-start(f32[128,256]{1,0:T(8,128)S(1)} %copy-done.6), channel_id=1, source_target_pairs={{13,112},{29,1},{45,18},{61,35},{77,52},{93,69},{109,86},{125,103}... | collective-permute-start | bytes 393224 | tf_op jit(solution)/shard_map/ppermute | solution.py:32
  340.4 18.3 %collective-permute-start.12 = (f32[128,256]{1,0:T(8,128)S(1)}, f32[128,256]{1,0:T(8,128)S(1)}, u32[]{:S(2)}, u32[]{:S(2)}) collective-permute-start(f32[128,256]{1,0:T(8,128)S(1)} %copy-done.7), channel_id=1, source_target_pairs={{0,0},{16,17},{32,34},{48,51},{64,68},{80,85},{96,102},{112,119},{... | collective-permute-start | bytes 393224 | tf_op jit(solution)/shard_map/ppermute | solution.py:32
  351.7 8.5 %collective-permute-start.13 = (f32[128,256]{1,0:T(8,128)S(1)}, f32[128,256]{1,0:T(8,128)S(1)}, u32[]{:S(2)}, u32[]{:S(2)}) collective-permute-start(f32[128,256]{1,0:T(8,128)S(1)} %copy-done.7), channel_id=1, source_target_pairs={{1,16},{17,33},{33,50},{49,67},{65,84},{81,101},{97,118},{113,7},{... | collective-permute-start | bytes 393224 | tf_op jit(solution)/shard_map/ppermute | solution.py:32
  352.4 8.5 %collective-permute-start.14 = (f32[128,256]{1,0:T(8,128)S(1)}, f32[128,256]{1,0:T(8,128)S(1)}, u32[]{:S(2)}, u32[]{:S(2)}) collective-permute-start(f32[128,256]{1,0:T(8,128)S(1)} %copy-done.7), channel_id=1, source_target_pairs={{4,32},{20,49},{36,66},{52,83},{68,100},{84,117},{100,6},{116,23},... | collective-permute-start | bytes 393224 | tf_op jit(solution)/shard_map/ppermute | solution.py:32
  357.4 9.3 %collective-permute-start.16 = (f32[128,256]{1,0:T(8,128)S(1)}, f32[128,256]{1,0:T(8,128)S(1)}, u32[]{:S(2)}, u32[]{:S(2)}) collective-permute-start(f32[128,256]{1,0:T(8,128)S(1)} %copy-done.7), channel_id=1, source_target_pairs={{8,64},{24,81},{40,98},{56,115},{72,4},{88,21},{104,38},{120,55},{... | collective-permute-start | bytes 393224 | tf_op jit(solution)/shard_map/ppermute | solution.py:32
  358.7 8.6 %collective-permute-start.17 = (f32[128,256]{1,0:T(8,128)S(1)}, f32[128,256]{1,0:T(8,128)}, u32[]{:S(2)}, u32[]{:S(2)}) collective-permute-start(f32[128,256]{1,0:T(8,128)S(1)} %copy-done.7), channel_id=1, source_target_pairs={{9,80},{25,97},{41,114},{57,3},{73,20},{89,37},{105,54},{121,71},{... | collective-permute-start | bytes 393224 | tf_op jit(solution)/shard_map/ppermute | solution.py:32
  360.3 9.2 %collective-permute-start.18 = (f32[128,256]{1,0:T(8,128)S(1)}, f32[128,256]{1,0:T(8,128)S(1)}, u32[]{:S(2)}, u32[]{:S(2)}) collective-permute-start(f32[128,256]{1,0:T(8,128)S(1)} %copy-done.7), channel_id=1, source_target_pairs={{12,96},{28,113},{44,2},{60,19},{76,36},{92,53},{108,70},{124,87},... | collective-permute-start | bytes 393224 | tf_op jit(solution)/shard_map/ppermute | solution.py:32
  360.9 9.3 %collective-permute-start.19 = (f32[128,256]{1,0:T(8,128)S(1)}, f32[128,256]{1,0:T(8,128)S(1)}, u32[]{:S(2)}, u32[]{:S(2)}) collective-permute-start(f32[128,256]{1,0:T(8,128)S(1)} %copy-done.7), channel_id=1, source_target_pairs={{13,112},{29,1},{45,18},{61,35},{77,52},{93,69},{109,86},{125,103}... | collective-permute-start | bytes 393224 | tf_op jit(solution)/shard_map/ppermute | solution.py:32
  361.6 9.9 %collective-permute-start.24 = (f32[128,256]{1,0:T(8,128)}, f32[128,256]{1,0:T(8,128)S(1)}, u32[]{:S(2)}, u32[]{:S(2)}) collective-permute-start(f32[128,256]{1,0:T(8,128)} %pad_maximum_fusion.7), channel_id=1, source_target_pairs={{0,0},{16,17},{32,34},{48,51},{64,68},{80,85},{96,102},{112,119},{... | collective-permute-start | bytes 393224 | tf_op jit(solution)/shard_map/ppermute | solution.py:32
  370.2 9.5 %collective-permute-start.28 = (f32[128,256]{1,0:T(8,128)}, f32[128,256]{1,0:T(8,128)S(1)}, u32[]{:S(2)}, u32[]{:S(2)}) collective-permute-start(f32[128,256]{1,0:T(8,128)} %pad_maximum_fusion.7), channel_id=1, source_target_pairs={{8,64},{24,81},{40,98},{56,115},{72,4},{88,21},{104,38},{120,55},{... | collective-permute-start | bytes 393224 | tf_op jit(solution)/shard_map/ppermute | solution.py:32
  371.5 8.8 %collective-permute-start.29 = (f32[128,256]{1,0:T(8,128)}, f32[128,256]{1,0:T(8,128)S(1)}, u32[]{:S(2)}, u32[]{:S(2)}) collective-permute-start(f32[128,256]{1,0:T(8,128)} %pad_maximum_fusion.7), channel_id=1, source_target_pairs={{9,80},{25,97},{41,114},{57,3},{73,20},{89,37},{105,54},{121,71},{... | collective-permute-start | bytes 393224 | tf_op jit(solution)/shard_map/ppermute | solution.py:32
  372.2 9.5 %collective-permute-start.30 = (f32[128,256]{1,0:T(8,128)}, f32[128,256]{1,0:T(8,128)S(1)}, u32[]{:S(2)}, u32[]{:S(2)}) collective-permute-start(f32[128,256]{1,0:T(8,128)} %pad_maximum_fusion.7), channel_id=1, source_target_pairs={{12,96},{28,113},{44,2},{60,19},{76,36},{92,53},{108,70},{124,87},... | collective-permute-start | bytes 393224 | tf_op jit(solution)/shard_map/ppermute | solution.py:32
  372.9 9.4 %collective-permute-start.31 = (f32[128,256]{1,0:T(8,128)}, f32[128,256]{1,0:T(8,128)S(1)}, u32[]{:S(2)}, u32[]{:S(2)}) collective-permute-start(f32[128,256]{1,0:T(8,128)} %pad_maximum_fusion.7), channel_id=1, source_target_pairs={{13,112},{29,1},{45,18},{61,35},{77,52},{93,69},{109,86},{125,103}... | collective-permute-start | bytes 393224 | tf_op jit(solution)/shard_map/ppermute | solution.py:32
  373.7 11.2 %collective-permute-start.36 = (f32[128,256]{1,0:T(8,128)}, f32[128,256]{1,0:T(8,128)S(1)}, u32[]{:S(2)}, u32[]{:S(2)}) collective-permute-start(f32[128,256]{1,0:T(8,128)} %pad_maximum_fusion.8), channel_id=1, source_target_pairs={{0,0},{16,17},{32,34},{48,51},{64,68},{80,85},{96,102},{112,119},{... | collective-permute-start | bytes 393224 | tf_op jit(solution)/shard_map/ppermute | solution.py:32
  380.4 5.9 collective-permute-start.38
  382.4 26.6 %collective-permute-start.40 = (f32[128,256]{1,0:T(8,128)}, f32[128,256]{1,0:T(8,128)S(1)}, u32[]{:S(2)}, u32[]{:S(2)}) collective-permute-start(f32[128,256]{1,0:T(8,128)} %pad_maximum_fusion.8), channel_id=1, source_target_pairs={{8,64},{24,81},{40,98},{56,115},{72,4},{88,21},{104,38},{120,55},{... | collective-permute-start | bytes 393224 | tf_op jit(solution)/shard_map/ppermute | solution.py:32
  384.9 25.1 %collective-permute-start.41 = (f32[128,256]{1,0:T(8,128)}, f32[128,256]{1,0:T(8,128)S(1)}, u32[]{:S(2)}, u32[]{:S(2)}) collective-permute-start(f32[128,256]{1,0:T(8,128)} %pad_maximum_fusion.8), channel_id=1, source_target_pairs={{9,80},{25,97},{41,114},{57,3},{73,20},{89,37},{105,54},{121,71},{... | collective-permute-start | bytes 393224 | tf_op jit(solution)/shard_map/ppermute | solution.py:32
  385.6 27.2 %collective-permute-start.42 = (f32[128,256]{1,0:T(8,128)}, f32[128,256]{1,0:T(8,128)S(1)}, u32[]{:S(2)}, u32[]{:S(2)}) collective-permute-start(f32[128,256]{1,0:T(8,128)} %pad_maximum_fusion.8), channel_id=1, source_target_pairs={{12,96},{28,113},{44,2},{60,19},{76,36},{92,53},{108,70},{124,87},... | collective-permute-start | bytes 393224 | tf_op jit(solution)/shard_map/ppermute | solution.py:32
  386.3 33.4 %collective-permute-start.43 = (f32[128,256]{1,0:T(8,128)}, f32[128,256]{1,0:T(8,128)S(1)}, u32[]{:S(2)}, u32[]{:S(2)}) collective-permute-start(f32[128,256]{1,0:T(8,128)} %pad_maximum_fusion.8), channel_id=1, source_target_pairs={{13,112},{29,1},{45,18},{61,35},{77,52},{93,69},{109,86},{125,103}... | collective-permute-start | bytes 393224 | tf_op jit(solution)/shard_map/ppermute | solution.py:32
  386.9 32.7 %collective-permute-start.8 = (f32[128,256]{1,0:T(8,128)S(1)}, f32[128,256]{1,0:T(8,128)S(1)}, u32[]{:S(2)}, u32[]{:S(2)}) collective-permute-start(f32[128,256]{1,0:T(8,128)S(1)} %get-tuple-element.105), channel_id=1, source_target_pairs={{0,32},{16,48},{32,64},{48,80},{64,96},{80,112},{96,0},{112,16},{1... | collective-permute-start | bytes 393224 | tf_op jit(solution)/shard_map/ppermute | solution.py:37
  409.0 13.4 %collective-permute-start.9 = (f32[128,256]{1,0:T(8,128)S(1)}, f32[128,256]{1,0:T(8,128)S(1)}, u32[]{:S(2)}, u32[]{:S(2)}) collective-permute-start(f32[128,256]{1,0:T(8,128)S(1)} %get-tuple-element.105), channel_id=1, source_target_pairs={{0,64},{16,80},{32,96},{48,112},{64,0},{80,16},{96,32},{112,48},{1... | collective-permute-start | bytes 393224 | tf_op jit(solution)/shard_map/ppermute | solution.py:37
  410.0 12.5 %collective-permute-start.10 = (f32[128,256]{1,0:T(8,128)S(1)}, f32[128,256]{1,0:T(8,128)S(1)}, u32[]{:S(2)}, u32[]{:S(2)}) collective-permute-start(f32[128,256]{1,0:T(8,128)S(1)} %get-tuple-element.105), channel_id=1, source_target_pairs={{0,96},{16,112},{32,0},{48,16},{64,32},{80,48},{96,64},{112,80},{1... | collective-permute-start | bytes 393224 | tf_op jit(solution)/shard_map/ppermute | solution.py:37
  412.8 12.6 %collective-permute-start.20 = (f32[128,256]{1,0:T(8,128)S(1)}, f32[128,256]{1,0:T(8,128)S(1)}, u32[]{:S(2)}, u32[]{:S(2)}) collective-permute-start(f32[128,256]{1,0:T(8,128)S(1)} %get-tuple-element.107), channel_id=1, source_target_pairs={{0,32},{16,48},{32,64},{48,80},{64,96},{80,112},{96,0},{112,16},{1... | collective-permute-start | bytes 393224 | tf_op jit(solution)/shard_map/ppermute | solution.py:37
  419.7 6.5 %collective-permute-start.21 = (f32[128,256]{1,0:T(8,128)S(1)}, f32[128,256]{1,0:T(8,128)S(1)}, u32[]{:S(2)}, u32[]{:S(2)}) collective-permute-start(f32[128,256]{1,0:T(8,128)S(1)} %get-tuple-element.107), channel_id=1, source_target_pairs={{0,64},{16,80},{32,96},{48,112},{64,0},{80,16},{96,32},{112,48},{1... | collective-permute-start | bytes 393224 | tf_op jit(solution)/shard_map/ppermute | solution.py:37
  419.7 7.9 %collective-permute-start.22 = (f32[128,256]{1,0:T(8,128)S(1)}, f32[128,256]{1,0:T(8,128)S(1)}, u32[]{:S(2)}, u32[]{:S(2)}) collective-permute-start(f32[128,256]{1,0:T(8,128)S(1)} %get-tuple-element.107), channel_id=1, source_target_pairs={{0,96},{16,112},{32,0},{48,16},{64,32},{80,48},{96,64},{112,80},{1... | collective-permute-start | bytes 393224 | tf_op jit(solution)/shard_map/ppermute | solution.py:37
  422.4 7.6 %collective-permute-start.32 = (f32[128,256]{1,0:T(8,128)S(1)}, f32[128,256]{1,0:T(8,128)S(1)}, u32[]{:S(2)}, u32[]{:S(2)}) collective-permute-start(f32[128,256]{1,0:T(8,128)S(1)} %get-tuple-element.109), channel_id=1, source_target_pairs={{0,32},{16,48},{32,64},{48,80},{64,96},{80,112},{96,0},{112,16},{1... | collective-permute-start | bytes 393224 | tf_op jit(solution)/shard_map/ppermute | solution.py:37
  422.5 10.1 %collective-permute-start.33 = (f32[128,256]{1,0:T(8,128)S(1)}, f32[128,256]{1,0:T(8,128)S(1)}, u32[]{:S(2)}, u32[]{:S(2)}) collective-permute-start(f32[128,256]{1,0:T(8,128)S(1)} %get-tuple-element.109), channel_id=1, source_target_pairs={{0,64},{16,80},{32,96},{48,112},{64,0},{80,16},{96,32},{112,48},{1... | collective-permute-start | bytes 393224 | tf_op jit(solution)/shard_map/ppermute | solution.py:37
  425.4 7.1 %collective-permute-start.34 = (f32[128,256]{1,0:T(8,128)S(1)}, f32[128,256]{1,0:T(8,128)S(1)}, u32[]{:S(2)}, u32[]{:S(2)}) collective-permute-start(f32[128,256]{1,0:T(8,128)S(1)} %get-tuple-element.109), channel_id=1, source_target_pairs={{0,96},{16,112},{32,0},{48,16},{64,32},{80,48},{96,64},{112,80},{1... | collective-permute-start | bytes 393224 | tf_op jit(solution)/shard_map/ppermute | solution.py:37
  426.2 7.7 %collective-permute-start.44 = (f32[128,256]{1,0:T(8,128)S(1)}, f32[128,256]{1,0:T(8,128)S(1)}, u32[]{:S(2)}, u32[]{:S(2)}) collective-permute-start(f32[128,256]{1,0:T(8,128)S(1)} %get-tuple-element.111), channel_id=1, source_target_pairs={{0,32},{16,48},{32,64},{48,80},{64,96},{80,112},{96,0},{112,16},{1... | collective-permute-start | bytes 393224 | tf_op jit(solution)/shard_map/ppermute | solution.py:37
  427.6 6.5 %collective-permute-start.45 = (f32[128,256]{1,0:T(8,128)S(1)}, f32[128,256]{1,0:T(8,128)S(1)}, u32[]{:S(2)}, u32[]{:S(2)}) collective-permute-start(f32[128,256]{1,0:T(8,128)S(1)} %get-tuple-element.111), channel_id=1, source_target_pairs={{0,64},{16,80},{32,96},{48,112},{64,0},{80,16},{96,32},{112,48},{1... | collective-permute-start | bytes 393224 | tf_op jit(solution)/shard_map/ppermute | solution.py:37
  432.5 6.3 %collective-permute-start.23 = (f32[4,128,256]{2,1,0:T(8,128)}, f32[4,128,256]{2,1,0:T(8,128)}, u32[]{:S(2)}, u32[]{:S(2)}) collective-permute-start(f32[4,128,256]{2,1,0:T(8,128)} %pad_maximum_fusion.2), channel_id=1, source_target_pairs={{0,16},{16,0},{32,48},{48,32},{64,80},{80,64},{96,112},{112,96},{1... | collective-permute-start | bytes 1572872 | tf_op jit(solution)/shard_map/ppermute | solution.py:39
  433.9 7.7 %collective-permute-start.35 = (f32[4,128,256]{2,1,0:T(8,128)}, f32[4,128,256]{2,1,0:T(8,128)}, u32[]{:S(2)}, u32[]{:S(2)}) collective-permute-start(f32[4,128,256]{2,1,0:T(8,128)} %pad_maximum_fusion.3), channel_id=1, source_target_pairs={{0,16},{16,0},{32,48},{48,32},{64,80},{80,64},{96,112},{112,96},{1... | collective-permute-start | bytes 1572872 | tf_op jit(solution)/shard_map/ppermute | solution.py:39
  435.8 8.6 %collective-permute-start.47 = (f32[4,128,256]{2,1,0:T(8,128)}, f32[4,128,256]{2,1,0:T(8,128)}, u32[]{:S(2)}, u32[]{:S(2)}) collective-permute-start(f32[4,128,256]{2,1,0:T(8,128)} %pad_maximum_fusion.4), channel_id=1, source_target_pairs={{0,16},{16,0},{32,48},{48,32},{64,80},{80,64},{96,112},{112,96},{1... | collective-permute-start | bytes 1572872 | tf_op jit(solution)/shard_map/ppermute | solution.py:39
  493.6 99.7 %all-to-all-start.1 = ((f32[8,4,256,256]{3,2,1,0:T(8,128)}), f32[8,4,256,256]{3,2,1,0:T(8,128)}, u32[]{:S(2)}, u32[]{:S(2)}) async-start(f32[8,4,256,256]{3,2,1,0:T(8,128)} %bitcast.124), calls=%async_computation.1 | async-start | bytes 16777216 | tf_op jit(solution)/shard_map/all_to_all | solution.py:150
  (25 other events, 348.7 us)
Sparse Core Ops, SparseCore 0:
  10.7 53.7 all-gather.13
  67.0 49.1 all-gather.23
  182.5 45.6 all-gather.15
  238.9 45.3 all-gather.17
  290.4 45.7 all-gather.19
  369.6 58.2 all-gather.21

commit v9 on v7

--- a/solution.py
+++ b/solution.py
@@ -66,9 +66,18 @@
     col_gain = col_valid.astype(jnp.float32)
 
     lead_tile = current[0, 0]
-    row_tiles = lax.all_gather(lead_tile, "col")[:LEAD]
-    lead_tiles = lax.all_gather(row_tiles, "row")[:LEAD]
-    lead_block = lead_tiles.transpose(0, 2, 1, 3).reshape(lead_w, lead_w)
+    slab = tile // grid_rows
+    lead_slabs = lead_tile.reshape(grid_rows, slab, tile)
+    held = None
+    for r in range(grid_rows):
+        perm = [
+            (i * grid_cols + j, r * grid_cols + LEAD * i + j) for i in range(LEAD) for j in range(LEAD)
+        ]
+        moved = lax.ppermute(lead_slabs[r], ("row", "col"), perm)
+        held = moved if held is None else held + moved
+    everything = lax.all_gather(held, ("row", "col"))
+    lead_tiles = everything.reshape(grid_rows, LEAD, LEAD, slab, tile)[:, :, :, :, :]
+    lead_block = lead_tiles.transpose(1, 0, 3, 2, 4).reshape(lead_w, lead_w)
     chunks = rows_dev * 2
     half = tile // 2
     panel_col = current[:, 0].reshape(chunks, half, tile)

time: 623 us -> 614 us (0.986)
    all_gather x2 -> x1, waiting for transfers between devices: 69.6 us -> 53.4 us  [local(): everything = lax.all_gather(held, ('row', 'col'))]
    ppermute x3, starting transfers between devices: 23.3 us -> 7.95 us  [local(): ring.append(lax.ppermute(mine, 'row', perm))]
    ppermute x0 -> x8, starting transfers between devices: none -> 14.3 us  [local(): moved = lax.ppermute(lead_slabs[r], ('row', 'col'), perm)]
    slice x5 -> x0, local copies, waits for them, and re-layouts: 8.84 us -> none  [the longest x3 4.89 us: local(): lead_tiles = lax.all_gather(row_tiles, 'row')[:LEAD]]
    ppermute x8, waiting for transfers between devices: 8.55 us -> 16.3 us  [local(): moved = lax.ppermute(piece, ('row', 'col'), perm)]
    all_gather x1, waiting for transfers between devices: 9.6 us -> 17.1 us  [local(): factor_rows = lax.all_gather(piece, 'col').reshape(rows_dev, tile, lead_w)]
  transfers between devices with their start and end apart: 17 -> 24, of which waited for: 10 -> 9; matrix products, arithmetic and copies ran while one was open for 3% -> 3% of each run, Pallas kernels for 0% -> 0%
where the time goes in v9:
time: 614 us; the launch traced here: 603 us
  waiting for transfers between devices  225 us (37%)
  other arithmetic  212 us (35%)
  local copies, waits for them, and re-layouts  54.6 us (9%)
  matrix products  46.5 us (8%)
  starting transfers between devices  43 us (7%)
  between operations  21.9 us (4%)
    another operation x34, other arithmetic, local(): aug_factor = lax.linalg.cholesky(aug, symmetrize_input=False)  195 us
    all_to_all x1, waiting for transfers between devices, local(): lax.all_to_all(outgoing, 'row', split_axis=0, concat_axis=0, tiled=True)  93.5 us
    all_gather x1, waiting for transfers between devices, local(): everything = lax.all_gather(held, ('row', 'col'))  53.4 us
    another operation x16, matrix products, local(): aug_factor = lax.linalg.cholesky(aug, symmetrize_input=False)  27 us
    all_to_all x1, waiting for transfers between devices, local(): lax.all_to_all(panel_col, 'col', split_axis=0, concat_axis=0, tiled=True)  23.7 us
    ppermute x3, waiting for transfers between devices, local(): ring.append(lax.ppermute(mine, 'row', perm))  20.1 us
    dot_general x1, matrix products, local(): lax.dot_general(factor_rows.reshape(rows_dev * tile, lead_w), col_factor....  19.6 us
    all_gather x1, waiting for transfers between devices, local(): factor_rows = lax.all_gather(piece, 'col').reshape(rows_dev, tile, lead_w)  17.1 us
  transfers between devices with their start and end apart: 24, of which 9 were waited for; matrix products, arithmetic and copies ran while one was open for 3% of the time, Pallas kernels for 0%

profile of v9, /device:TPU:1, one launch (start us, length us, event | category | flops | bytes accessed | tf_op | source)
XLA Modules:
  0.0 603.3 jit_solution(17520873173386563581)
XLA Ops:
  8.1 4.6 collective-permute-start
  24.1 3.1 slice.230
  27.2 5.1 all-to-all-start
  33.7 23.7 %all-to-all-done = f32[16,128,256]{2,1,0:T(8,128)S(1)} async-done(((f32[16,128,256]{2,1,0:T(8,128)}), f32[16,128,256]{2,1,0:T(8,128)S(1)}, u32[]{:S(2)}, u32[]{:S(2)}) %all-to-all-start) | async-done | bytes 2097184 | tf_op jit(solution)/shard_map/all_to_all | solution.py:84
  58.8 53.4 %all-gather.5.cloned.1.call-done = f32[4096,256]{1,0:T(8,128)} async-done(((f32[32,256]{1,0:T(8,128)}), f32[4096,256]{1,0:T(8,128)}) %all-gather.5.cloned.1.call-update) | async-done | bytes 4194320 | tf_op jit(solution)/shard_map/all_gather | solution.py:78
  112.2 5.8 copy.15
  121.1 11.7 %cholesky.252 = f32[128,128]{1,0:T(8,128)S(1)} custom-call(f32[128,128]{1,0:T(8,128)S(1)} %cholesky.658), custom_call_target="Cholesky" | custom-call | tf_op jit(solution)/shard_map/cholesky | solution.py:101
  132.8 9.8 %custom-call.50 = f32[1,128,128]{1,2,0:T(8,128)S(1)} custom-call(f32[1,128,128]{2,1,0:T(8,128)S(1)} %get-tuple-element.63), custom_call_target="InvertDiagBlocksLowerTriangular" | custom-call | tf_op jit(solution)/shard_map/cholesky | solution.py:101
  142.6 3.0 cholesky.281
  150.3 11.7 %cholesky.274 = f32[128,128]{1,0:T(8,128)S(1)} custom-call(f32[128,128]{1,0:T(8,128)S(1)} %cholesky.662), custom_call_target="Cholesky" | custom-call | tf_op jit(solution)/shard_map/cholesky | solution.py:101
  162.7 9.8 %custom-call.51 = f32[1,128,128]{1,2,0:T(8,128)S(1)} custom-call(f32[1,128,128]{2,1,0:T(8,128)S(1)} %get-tuple-element.60), custom_call_target="InvertDiagBlocksLowerTriangular" | custom-call | tf_op jit(solution)/shard_map/cholesky | solution.py:101
  173.8 2.3 convolution_subtract_fusion.1
  176.1 11.9 %cholesky.526 = f32[128,128]{1,0:T(8,128)S(1)} custom-call(f32[128,128]{1,0:T(8,128)S(1)} %cholesky.667), custom_call_target="Cholesky" | custom-call | tf_op jit(solution)/shard_map/cholesky | solution.py:101
  189.3 9.8 %custom-call.52 = f32[1,128,128]{1,2,0:T(8,128)S(1)} custom-call(f32[1,128,128]{2,1,0:T(8,128)S(1)} %get-tuple-element.57), custom_call_target="InvertDiagBlocksLowerTriangular" | custom-call | tf_op jit(solution)/shard_map/cholesky | solution.py:101
  200.3 2.6 convolution_subtract_fusion.2
  202.9 11.7 %cholesky.545 = f32[128,128]{1,0:T(8,128)S(1)} custom-call(f32[128,128]{1,0:T(8,128)S(1)} %cholesky.672), custom_call_target="Cholesky" | custom-call | tf_op jit(solution)/shard_map/cholesky | solution.py:101
  215.9 9.8 %custom-call.53 = f32[1,128,128]{1,2,0:T(8,128)S(1)} custom-call(f32[1,128,128]{2,1,0:T(8,128)S(1)} %get-tuple-element.54), custom_call_target="InvertDiagBlocksLowerTriangular" | custom-call | tf_op jit(solution)/shard_map/cholesky | solution.py:101
  226.8 2.6 fusion.4
  229.5 11.9 %cholesky.564 = f32[128,128]{1,0:T(8,128)S(1)} custom-call(f32[128,128]{1,0:T(8,128)S(1)} %cholesky.677), custom_call_target="Cholesky" | custom-call | tf_op jit(solution)/shard_map/cholesky | solution.py:101
  242.7 9.8 %custom-call.54 = f32[1,128,128]{1,2,0:T(8,128)S(1)} custom-call(f32[1,128,128]{2,1,0:T(8,128)S(1)} %get-tuple-element.51), custom_call_target="InvertDiagBlocksLowerTriangular" | custom-call | tf_op jit(solution)/shard_map/cholesky | solution.py:101
  253.6 2.6 fusion.10
  256.3 11.7 %cholesky.584 = f32[128,128]{1,0:T(8,128)S(1)} custom-call(f32[128,128]{1,0:T(8,128)S(1)} %cholesky.682), custom_call_target="Cholesky" | custom-call | tf_op jit(solution)/shard_map/cholesky | solution.py:101
  269.3 10.2 %custom-call.55 = f32[1,128,128]{1,2,0:T(8,128)S(1)} custom-call(f32[1,128,128]{2,1,0:T(8,128)S(1)} %get-tuple-element.48), custom_call_target="InvertDiagBlocksLowerTriangular" | custom-call | tf_op jit(solution)/shard_map/cholesky | solution.py:101
  280.5 2.5 fusion.13
  283.0 11.7 %cholesky.604 = f32[128,128]{1,0:T(8,128)S(1)} custom-call(f32[128,128]{1,0:T(8,128)S(1)} %cholesky.687), custom_call_target="Cholesky" | custom-call | tf_op jit(solution)/shard_map/cholesky | solution.py:101
  296.1 9.8 %custom-call.56 = f32[1,128,128]{1,2,0:T(8,128)S(1)} custom-call(f32[1,128,128]{2,1,0:T(8,128)S(1)} %get-tuple-element.45), custom_call_target="InvertDiagBlocksLowerTriangular" | custom-call | tf_op jit(solution)/shard_map/cholesky | solution.py:101
  309.0 11.9 %cholesky.624 = f32[128,128]{1,0:T(8,128)S(1)} custom-call(f32[128,128]{1,0:T(8,128)S(1)} %cholesky.692), custom_call_target="Cholesky" | custom-call | tf_op jit(solution)/shard_map/cholesky | solution.py:101
  322.2 9.8 %custom-call.57 = f32[1,128,128]{1,2,0:T(8,128)S(1)} custom-call(f32[1,128,128]{2,1,0:T(8,128)S(1)} %get-tuple-element.42), custom_call_target="InvertDiagBlocksLowerTriangular" | custom-call | tf_op jit(solution)/shard_map/cholesky | solution.py:101
  334.7 11.7 %cholesky.641 = f32[128,128]{1,0:T(8,128)S(1)} custom-call(f32[128,128]{1,0:T(8,128)S(1)} %convolution_subtract_fusion.4), custom_call_target="Cholesky" | custom-call | tf_op jit(solution)/shard_map/cholesky | solution.py:101
  354.0 2.9 select_select_fusion
  362.7 2.4 collective-permute-start.8
  366.4 11.3 %collective-permute-done.8 = f32[128,1024]{1,0:T(8,128)} collective-permute-done((f32[128,1024]{1,0:T(8,128)}, f32[128,1024]{1,0:T(8,128)}, u32[]{:S(2)}, u32[]{:S(2)}) %collective-permute-start.8) | collective-permute-done | bytes 524320 | tf_op jit(solution)/shard_map/ppermute | solution.py:117
  377.7 5.0 collective-permute-done.9
  382.7 2.4 constant_dynamic-update-slice_fusion.4
  385.1 5.6 collective-permute-start.16
  390.7 2.4 collective-permute-start.18
  393.1 9.3 %collective-permute-done.16 = f32[128,1024]{1,0:T(8,128)S(1)} collective-permute-done((f32[128,1024]{1,0:T(8,128)S(1)}, f32[128,1024]{1,0:T(8,128)S(1)}, u32[]{:S(2)}, u32[]{:S(2)}) %collective-permute-start.16) | collective-permute-done | bytes 524320 | tf_op jit(solution)/shard_map/ppermute | solution.py:122
  402.4 10.8 %collective-permute-done.17 = f32[128,1024]{1,0:T(8,128)S(1)} collective-permute-done((f32[128,1024]{1,0:T(8,128)S(1)}, f32[128,1024]{1,0:T(8,128)S(1)}, u32[]{:S(2)}, u32[]{:S(2)}) %collective-permute-start.17) | collective-permute-done | bytes 524320 | tf_op jit(solution)/shard_map/ppermute | solution.py:122
  419.6 3.2 constant_dynamic-update-slice_fusion
  422.8 5.1 gather_fusion
  428.0 17.1 %all-gather.7.cloned.1.call-done = f32[2048,1024]{1,0:T(8,128)} async-done(((f32[128,1024]{1,0:T(8,128)}), f32[2048,1024]{1,0:T(8,128)}) %all-gather.7.cloned.1.call-update) | async-done | bytes 8388624 | tf_op jit(solution)/shard_map/all_gather | solution.py:107
  445.1 19.6 %bitcast_subtract_fusion = f32[8,4,256,256]{3,2,1,0:T(8,128)} fusion(f32[8,256,1024,1]{2,1,3,0:T(8,128)} %bitcast.113, f32[4,256,1024,1]{2,1,0,3:T(8,128)} %bitcast.116, f32[8,1,4,1,256,256]{5,4,3,2,1,0:T(8,128)} %param.4), kind=kOutput, calls=%fused_computation.4 | convolution fusion | flops 12886999040 | bytes 29360128 | tf_op jit(solution)/shard_map/dot_general | solution.py:132
  464.6 7.9 %gather_fusion.1 = f32[32,256,256]{2,1,0:T(8,128)} fusion(f32[32,256,256]{2,1,0:T(8,128)} %bitcast.112, s32[1024]{0:T(1024)S(1)} %pad_clamp_fusion.1), kind=kCustom, calls=%fused_computation.1 | custom fusion | bytes 16777344 | tf_op jit(solution)/shard_map/gather | solution.py:142
  472.5 5.7 all-to-all-start.1
  478.5 93.5 %all-to-all-done.1 = f32[8,4,256,256]{3,2,1,0:T(8,128)} async-done(((f32[8,4,256,256]{3,2,1,0:T(8,128)}), f32[8,4,256,256]{3,2,1,0:T(8,128)}, u32[]{:S(2)}, u32[]{:S(2)}) %all-to-all-start.1) | async-done | bytes 8388640 | tf_op jit(solution)/shard_map/all_to_all | solution.py:143
  572.0 7.9 %gather_fusion.2 = f32[8,4,256,256]{3,2,1,0:T(8,128)} fusion(f32[8,4,256,256]{3,2,1,0:T(8,128)} %all-to-all-done.1, s32[1024]{0:T(1024)S(1)} %pad_clamp_fusion), kind=kCustom, calls=%fused_computation.2 | custom fusion | bytes 16777248 | tf_op jit(solution)/shard_map/gather | solution.py:145
  579.8 8.0 %bitcast_select_fusion = f32[8,1,4,1,256,256]{5,4,3,2,1,0:T(8,128)} fusion(f32[8,4,256,256]{3,2,1,0:T(8,128)} %gather_fusion.2, pred[8,4]{1,0:T(8,128)(4,1)S(1)} %broadcast_and_fusion), kind=kLoop, calls=%fused_computation.3 | loop fusion | flops 2097152 | bytes 16777248 | tf_op jit(solution)/shard_map/jit(_where)/select_n | solution.py:145
  587.8 8.4 %copy.42 = f32[8,1,256,1024]{3,2,1,0:T(8,128)} copy(f32[8,1,256,1024]{3,2,1,0:T(8,128)} %bitcast.114) | data formatting | bytes 16777216
  (122 shorter events, 57.1 us)
Async XLA Ops:
  7.2 25.2 %copy-start.5 = (s32[60]{0:T(128)S(1)}, s32[60]{0:T(128)}, u32[]{:S(2)}) copy-start(s32[60]{0:T(128)} %param.5) | copy-start | bytes 724
  7.2 105.1 %all-gather.5.cloned.1.call-start = ((), (), s32[]{:S(2)}) async-start(), calls=%async_computation.2 | async-start | bytes 4227072 | tf_op jit(solution)/shard_map/all_gather | solution.py:78
  8.1 10.4 %collective-permute-start = (f32[32,256]{1,0:T(8,128)S(1)}, f32[32,256]{1,0:T(8,128)S(1)}, u32[]{:S(2)}, u32[]{:S(2)}) collective-permute-start(f32[32,256]{1,0:T(8,128)S(1)} %get-tuple-element.36), channel_id=1, source_target_pairs={{0,0},{1,1},{2,2},{3,3},{16,4},{17,5},{18,6},{19,7},{32,8},{33,9},... | collective-permute-start | bytes 98312 | tf_op jit(solution)/shard_map/ppermute | solution.py:76
  12.7 7.1 %collective-permute-start.1 = (f32[32,256]{1,0:T(8,128)S(1)}, f32[32,256]{1,0:T(8,128)S(1)}, u32[]{:S(2)}, u32[]{:S(2)}) collective-permute-start(f32[32,256]{1,0:T(8,128)S(1)} %get-tuple-element.29), channel_id=1, source_target_pairs={{0,16},{1,17},{2,18},{3,19},{16,20},{17,21},{18,22},{19,23},{32,24... | collective-permute-start | bytes 98312 | tf_op jit(solution)/shard_map/ppermute | solution.py:76
  14.6 6.5 %collective-permute-start.2 = (f32[32,256]{1,0:T(8,128)S(1)}, f32[32,256]{1,0:T(8,128)S(1)}, u32[]{:S(2)}, u32[]{:S(2)}) collective-permute-start(f32[32,256]{1,0:T(8,128)S(1)} %get-tuple-element.35), channel_id=1, source_target_pairs={{0,32},{1,33},{2,34},{3,35},{16,36},{17,37},{18,38},{19,39},{32,40... | collective-permute-start | bytes 98312 | tf_op jit(solution)/shard_map/ppermute | solution.py:76
  15.9 6.5 %collective-permute-start.3 = (f32[32,256]{1,0:T(8,128)S(1)}, f32[32,256]{1,0:T(8,128)S(1)}, u32[]{:S(2)}, u32[]{:S(2)}) collective-permute-start(f32[32,256]{1,0:T(8,128)S(1)} %get-tuple-element.34), channel_id=1, source_target_pairs={{0,48},{1,49},{2,50},{3,51},{16,52},{17,53},{18,54},{19,55},{32,56... | collective-permute-start | bytes 98312 | tf_op jit(solution)/shard_map/ppermute | solution.py:76
  17.2 5.2 collective-permute-start.4
  18.5 3.9 collective-permute-start.5
  19.9 2.6 collective-permute-start.6
  21.2 2.3 collective-permute-start.7
  27.2 30.2 %all-to-all-start = ((f32[16,128,256]{2,1,0:T(8,128)}), f32[16,128,256]{2,1,0:T(8,128)S(1)}, u32[]{:S(2)}, u32[]{:S(2)}) async-start(f32[16,128,256]{2,1,0:T(8,128)} %bitcast.11), calls=%async_computation | async-start | bytes 4194304 | tf_op jit(solution)/shard_map/all_to_all | solution.py:84
  32.3 412.7 %all-gather.7.cloned.1.call-start = ((), (), s32[]{:S(2)}) async-start(), calls=%async_computation.3 | async-start | bytes 8912896 | tf_op jit(solution)/shard_map/all_gather | solution.py:107
  119.0 2.0 copy-start
  142.6 4.1 copy-start.1
  147.2 2.5 copy-start.2
  357.5 35.6 %copy-start.4 = (s32[60]{0:T(128)S(1)}, s32[60]{0:T(128)}, u32[]{:S(2)}) copy-start(s32[60]{0:T(128)} %param.6) | copy-start | bytes 724
  357.5 35.6 %copy-start.6 = (s32[60]{0:T(128)S(1)}, s32[60]{0:T(128)}, u32[]{:S(2)}) copy-start(s32[60]{0:T(128)} %param.7) | copy-start | bytes 724
  358.4 3.5 collective-permute-start.10
  359.1 3.5 collective-permute-start.11
  359.8 5.2 collective-permute-start.12
  360.5 5.9 collective-permute-start.13
  361.2 5.2 collective-permute-start.14
  362.0 4.5 collective-permute-start.15
  362.7 15.0 %collective-permute-start.8 = (f32[128,1024]{1,0:T(8,128)}, f32[128,1024]{1,0:T(8,128)}, u32[]{:S(2)}, u32[]{:S(2)}) collective-permute-start(f32[128,1024]{1,0:T(8,128)} %slice_select_fusion), channel_id=1, source_target_pairs={{0,0},{16,17},{32,34},{48,51},{64,68},{80,85},{96,102},{112,119},{... | collective-permute-start | bytes 1572872 | tf_op jit(solution)/shard_map/ppermute | solution.py:117
  365.1 17.6 %collective-permute-start.9 = (f32[128,1024]{1,0:T(8,128)}, f32[128,1024]{1,0:T(8,128)}, u32[]{:S(2)}, u32[]{:S(2)}) collective-permute-start(f32[128,1024]{1,0:T(8,128)} %slice_select_fusion), channel_id=1, source_target_pairs={{1,16},{17,33},{33,50},{49,67},{65,84},{81,101},{97,118},{113,7},{... | collective-permute-start | bytes 1572872 | tf_op jit(solution)/shard_map/ppermute | solution.py:117
  385.1 17.3 %collective-permute-start.16 = (f32[128,1024]{1,0:T(8,128)S(1)}, f32[128,1024]{1,0:T(8,128)S(1)}, u32[]{:S(2)}, u32[]{:S(2)}) collective-permute-start(f32[128,1024]{1,0:T(8,128)S(1)} %get-tuple-element.28), channel_id=1, source_target_pairs={{0,32},{16,48},{32,64},{48,80},{64,96},{80,112},{96,0},{112,16},{1... | collective-permute-start | bytes 1572872 | tf_op jit(solution)/shard_map/ppermute | solution.py:122
  390.7 22.5 %collective-permute-start.17 = (f32[128,1024]{1,0:T(8,128)S(1)}, f32[128,1024]{1,0:T(8,128)S(1)}, u32[]{:S(2)}, u32[]{:S(2)}) collective-permute-start(f32[128,1024]{1,0:T(8,128)S(1)} %get-tuple-element.28), channel_id=1, source_target_pairs={{0,64},{16,80},{32,96},{48,112},{64,0},{80,16},{96,32},{112,48},{1... | collective-permute-start | bytes 1572872 | tf_op jit(solution)/shard_map/ppermute | solution.py:122
  390.7 22.5 %collective-permute-start.18 = (f32[128,1024]{1,0:T(8,128)S(1)}, f32[128,1024]{1,0:T(8,128)S(1)}, u32[]{:S(2)}, u32[]{:S(2)}) collective-permute-start(f32[128,1024]{1,0:T(8,128)S(1)} %get-tuple-element.28), channel_id=1, source_target_pairs={{0,96},{16,112},{32,0},{48,16},{64,32},{80,48},{96,64},{112,80},{1... | collective-permute-start | bytes 1572872 | tf_op jit(solution)/shard_map/ppermute | solution.py:122
  413.2 2.2 copy-start.3
  413.4 6.2 %collective-permute-start.19 = (f32[4,128,1024]{2,1,0:T(8,128)S(1)}, f32[4,128,1024]{2,1,0:T(8,128)}, u32[]{:S(2)}, u32[]{:S(2)}) collective-permute-start(f32[4,128,1024]{2,1,0:T(8,128)S(1)} %pad_maximum_fusion), channel_id=1, source_target_pairs={{0,16},{16,0},{32,48},{48,32},{64,80},{80,64},{96,112},{112,96},{1... | collective-permute-start | bytes 6291464 | tf_op jit(solution)/shard_map/ppermute | solution.py:124
  472.5 99.5 %all-to-all-start.1 = ((f32[8,4,256,256]{3,2,1,0:T(8,128)}), f32[8,4,256,256]{3,2,1,0:T(8,128)}, u32[]{:S(2)}, u32[]{:S(2)}) async-start(f32[8,4,256,256]{3,2,1,0:T(8,128)} %bitcast.108), calls=%async_computation.1 | async-start | bytes 16777216 | tf_op jit(solution)/shard_map/all_to_all | solution.py:143
Sparse Core Ops, SparseCore 0:
  24.2 87.9 all-gather.4
  358.6 86.4 all-gather.6

commit v10 on v9

--- a/solution.py
+++ b/solution.py
@@ -142,7 +142,12 @@
     outgoing = schur[flat_idx]
     incoming = lax.all_to_all(outgoing, "row", split_axis=0, concat_axis=0, tiled=True)
     keep = (recv_valid[:, None] & col_valid[None, :])[:, :, None, None]
-    parent = jnp.where(keep, incoming[recv_source], 0.0)
+    parent = jnp.stack(
+        [
+            jnp.where(keep[slot], lax.dynamic_index_in_dim(incoming, recv_source[slot], keepdims=False), 0.0)
+            for slot in range(rows_dev)
+        ]
+    )
     return (factor_rows[:, None], parent[:, None, :, None])
 
 

time: 614 us -> 605 us (0.985)
  between operations: 21.9 us -> 37.2 us
  waiting for transfers between devices: 225 us -> 214 us
  local copies, waits for them, and re-layouts: 54.6 us -> 44.9 us
    all_to_all x1, waiting for transfers between devices: 93.5 us -> 77.8 us  [local(): lax.all_to_all(outgoing, 'row', split_axis=0, concat_axis=0, tiled=True)]
    ppermute x8, waiting for transfers between devices: 16.3 us -> 29.7 us  [local(): moved = lax.ppermute(piece, ('row', 'col'), perm)]
    unnamed x2 -> x10, other arithmetic: 3.16 us -> 11.9 us
    all_gather x1, waiting for transfers between devices: 17.1 us -> 8.35 us  [local(): factor_rows = lax.all_gather(piece, 'col').reshape(rows_dev, tile, lead_w)]
    select_n x2 -> x1, other arithmetic: 8 us -> 0.01 us  [local(): (update_index + LEAD) // grid_rows]
    gather x1 -> x0, local copies, waits for them, and re-layouts: 7.86 us -> none  [local(): parent = jnp.where(keep, incoming[recv_source], 0.0)]
    ppermute x3, starting transfers between devices: 7.95 us -> 1.47 us  [local(): ring.append(lax.ppermute(mine, 'row', perm))]
    unnamed x19 -> x25, local copies, waits for them, and re-layouts: 16.4 us -> 13.8 us
where the time goes in v10:
time: 605 us; the launch traced here: 594 us
  waiting for transfers between devices  214 us (35%)
  other arithmetic  214 us (35%)
  matrix products  46.5 us (8%)
  local copies, waits for them, and re-layouts  44.9 us (7%)
  starting transfers between devices  37.2 us (6%)
  between operations  37.2 us (6%)
    another operation x34, other arithmetic, local(): aug_factor = lax.linalg.cholesky(aug, symmetrize_input=False)  195 us
    all_to_all x1, waiting for transfers between devices, local(): lax.all_to_all(outgoing, 'row', split_axis=0, concat_axis=0, tiled=True)  77.8 us
    all_gather x1, waiting for transfers between devices, local(): everything = lax.all_gather(held, ('row', 'col'))  52.9 us
    ppermute x8, waiting for transfers between devices, local(): moved = lax.ppermute(piece, ('row', 'col'), perm)  29.7 us
    another operation x16, matrix products, local(): aug_factor = lax.linalg.cholesky(aug, symmetrize_input=False)  27 us
    ppermute x3, waiting for transfers between devices, local(): ring.append(lax.ppermute(mine, 'row', perm))  24.1 us
    all_to_all x1, waiting for transfers between devices, local(): lax.all_to_all(panel_col, 'col', split_axis=0, concat_axis=0, tiled=True)  20 us
    dot_general x1, matrix products, local(): lax.dot_general(factor_rows.reshape(rows_dev * tile, lead_w), col_factor....  19.6 us
  transfers between devices with their start and end apart: 24, of which 9 were waited for; matrix products, arithmetic and copies ran while one was open for 3% of the time, Pallas kernels for 0%

profile of v10, /device:TPU:1, one launch (start us, length us, event | category | flops | bytes accessed | tf_op | source)
XLA Modules:
  0.0 593.9 jit_solution(3882915085389467759)
XLA Ops:
  8.1 4.0 collective-permute-start.1
  12.1 2.9 collective-permute-start.7
  24.5 3.1 slice.300
  27.6 5.1 all-to-all-start
  34.0 20.0 %all-to-all-done = f32[16,128,256]{2,1,0:T(8,128)S(1)} async-done(((f32[16,128,256]{2,1,0:T(8,128)}), f32[16,128,256]{2,1,0:T(8,128)S(1)}, u32[]{:S(2)}, u32[]{:S(2)}) %all-to-all-start) | async-done | bytes 2097184 | tf_op jit(solution)/shard_map/all_to_all | solution.py:84
  55.5 52.9 %all-gather.5.cloned.1.call-done = f32[4096,256]{1,0:T(8,128)} async-done(((f32[32,256]{1,0:T(8,128)}), f32[4096,256]{1,0:T(8,128)}) %all-gather.5.cloned.1.call-update) | async-done | bytes 4194320 | tf_op jit(solution)/shard_map/all_gather | solution.py:78
  108.4 5.8 copy.15
  115.2 2.0 copy-done
  117.2 11.7 %cholesky.252 = f32[128,128]{1,0:T(8,128)S(1)} custom-call(f32[128,128]{1,0:T(8,128)S(1)} %cholesky.658), custom_call_target="Cholesky" | custom-call | tf_op jit(solution)/shard_map/cholesky | solution.py:101
  129.0 9.8 %custom-call.50 = f32[1,128,128]{1,2,0:T(8,128)S(1)} custom-call(f32[1,128,128]{2,1,0:T(8,128)S(1)} %get-tuple-element.63), custom_call_target="InvertDiagBlocksLowerTriangular" | custom-call | tf_op jit(solution)/shard_map/cholesky | solution.py:101
  138.8 3.0 cholesky.281
  143.4 2.3 constant_dynamic-update-slice_fusion.5
  146.5 11.7 %cholesky.274 = f32[128,128]{1,0:T(8,128)S(1)} custom-call(f32[128,128]{1,0:T(8,128)S(1)} %cholesky.662), custom_call_target="Cholesky" | custom-call | tf_op jit(solution)/shard_map/cholesky | solution.py:101
  158.9 9.8 %custom-call.51 = f32[1,128,128]{1,2,0:T(8,128)S(1)} custom-call(f32[1,128,128]{2,1,0:T(8,128)S(1)} %get-tuple-element.60), custom_call_target="InvertDiagBlocksLowerTriangular" | custom-call | tf_op jit(solution)/shard_map/cholesky | solution.py:101
  170.0 2.3 convolution_subtract_fusion.1
  172.2 11.9 %cholesky.526 = f32[128,128]{1,0:T(8,128)S(1)} custom-call(f32[128,128]{1,0:T(8,128)S(1)} %cholesky.667), custom_call_target="Cholesky" | custom-call | tf_op jit(solution)/shard_map/cholesky | solution.py:101
  185.4 9.8 %custom-call.52 = f32[1,128,128]{1,2,0:T(8,128)S(1)} custom-call(f32[1,128,128]{2,1,0:T(8,128)S(1)} %get-tuple-element.57), custom_call_target="InvertDiagBlocksLowerTriangular" | custom-call | tf_op jit(solution)/shard_map/cholesky | solution.py:101
  196.5 2.6 convolution_subtract_fusion.2
  199.1 11.7 %cholesky.545 = f32[128,128]{1,0:T(8,128)S(1)} custom-call(f32[128,128]{1,0:T(8,128)S(1)} %cholesky.672), custom_call_target="Cholesky" | custom-call | tf_op jit(solution)/shard_map/cholesky | solution.py:101
  212.1 9.8 %custom-call.53 = f32[1,128,128]{1,2,0:T(8,128)S(1)} custom-call(f32[1,128,128]{2,1,0:T(8,128)S(1)} %get-tuple-element.54), custom_call_target="InvertDiagBlocksLowerTriangular" | custom-call | tf_op jit(solution)/shard_map/cholesky | solution.py:101
  223.0 2.6 fusion.4
  225.7 11.9 %cholesky.564 = f32[128,128]{1,0:T(8,128)S(1)} custom-call(f32[128,128]{1,0:T(8,128)S(1)} %cholesky.677), custom_call_target="Cholesky" | custom-call | tf_op jit(solution)/shard_map/cholesky | solution.py:101
  238.9 9.8 %custom-call.54 = f32[1,128,128]{1,2,0:T(8,128)S(1)} custom-call(f32[1,128,128]{2,1,0:T(8,128)S(1)} %get-tuple-element.51), custom_call_target="InvertDiagBlocksLowerTriangular" | custom-call | tf_op jit(solution)/shard_map/cholesky | solution.py:101
  249.8 2.6 fusion.10
  252.4 11.7 %cholesky.584 = f32[128,128]{1,0:T(8,128)S(1)} custom-call(f32[128,128]{1,0:T(8,128)S(1)} %cholesky.682), custom_call_target="Cholesky" | custom-call | tf_op jit(solution)/shard_map/cholesky | solution.py:101
  265.5 10.2 %custom-call.55 = f32[1,128,128]{1,2,0:T(8,128)S(1)} custom-call(f32[1,128,128]{2,1,0:T(8,128)S(1)} %get-tuple-element.48), custom_call_target="InvertDiagBlocksLowerTriangular" | custom-call | tf_op jit(solution)/shard_map/cholesky | solution.py:101
  276.7 2.5 fusion.13
  279.2 11.7 %cholesky.604 = f32[128,128]{1,0:T(8,128)S(1)} custom-call(f32[128,128]{1,0:T(8,128)S(1)} %cholesky.687), custom_call_target="Cholesky" | custom-call | tf_op jit(solution)/shard_map/cholesky | solution.py:101
  292.2 9.8 %custom-call.56 = f32[1,128,128]{1,2,0:T(8,128)S(1)} custom-call(f32[1,128,128]{2,1,0:T(8,128)S(1)} %get-tuple-element.45), custom_call_target="InvertDiagBlocksLowerTriangular" | custom-call | tf_op jit(solution)/shard_map/cholesky | solution.py:101
  303.0 2.2 convolution_subtract_fusion.3
  305.2 11.9 %cholesky.624 = f32[128,128]{1,0:T(8,128)S(1)} custom-call(f32[128,128]{1,0:T(8,128)S(1)} %cholesky.692), custom_call_target="Cholesky" | custom-call | tf_op jit(solution)/shard_map/cholesky | solution.py:101
  318.4 9.8 %custom-call.57 = f32[1,128,128]{1,2,0:T(8,128)S(1)} custom-call(f32[1,128,128]{2,1,0:T(8,128)S(1)} %get-tuple-element.42), custom_call_target="InvertDiagBlocksLowerTriangular" | custom-call | tf_op jit(solution)/shard_map/cholesky | solution.py:101
  330.8 11.7 %cholesky.641 = f32[128,128]{1,0:T(8,128)S(1)} custom-call(f32[128,128]{1,0:T(8,128)S(1)} %convolution_subtract_fusion.4), custom_call_target="Cholesky" | custom-call | tf_op jit(solution)/shard_map/cholesky | solution.py:101
  350.2 2.9 select_select_fusion
  360.2 3.0 collective-permute-start.8
  363.4 29.7 %collective-permute-done.9 = f32[128,1024]{1,0:T(8,128)S(1)} collective-permute-done((f32[128,1024]{1,0:T(8,128)}, f32[128,1024]{1,0:T(8,128)S(1)}, u32[]{:S(2)}, u32[]{:S(2)}) %collective-permute-start.9) | collective-permute-done | bytes 524320 | tf_op jit(solution)/shard_map/ppermute | solution.py:117
  396.0 6.4 %collective-permute-done.18 = f32[128,1024]{1,0:T(8,128)S(1)} collective-permute-done((f32[128,1024]{1,0:T(8,128)S(1)}, f32[128,1024]{1,0:T(8,128)S(1)}, u32[]{:S(2)}, u32[]{:S(2)}) %collective-permute-start.18) | collective-permute-done | bytes 524320 | tf_op jit(solution)/shard_map/ppermute | solution.py:122
  404.0 16.1 %collective-permute-done.16 = f32[128,1024]{1,0:T(8,128)S(1)} collective-permute-done((f32[128,1024]{1,0:T(8,128)S(1)}, f32[128,1024]{1,0:T(8,128)S(1)}, u32[]{:S(2)}, u32[]{:S(2)}) %collective-permute-start.16) | collective-permute-done | bytes 524320 | tf_op jit(solution)/shard_map/ppermute | solution.py:122
  422.3 1.9 constant_dynamic-update-slice_fusion.3
  425.8 3.2 constant_dynamic-update-slice_fusion
  429.1 5.1 gather_fusion
  434.2 8.4 %all-gather.7.cloned.1.call-done = f32[2048,1024]{1,0:T(8,128)} async-done(((f32[128,1024]{1,0:T(8,128)}), f32[2048,1024]{1,0:T(8,128)}) %all-gather.7.cloned.1.call-update) | async-done | bytes 8388624 | tf_op jit(solution)/shard_map/all_gather | solution.py:107
  442.6 19.6 %bitcast_subtract_fusion = f32[8,4,256,256]{3,2,1,0:T(8,128)} fusion(f32[8,256,1024,1]{2,1,3,0:T(8,128)} %bitcast.132, f32[4,256,1024,1]{2,1,0,3:T(8,128)} %bitcast.137, f32[8,1,4,1,256,256]{5,4,3,2,1,0:T(8,128)} %param.4), kind=kOutput, calls=%fused_computation.2 | convolution fusion | flops 12886999040 | bytes 29360128 | tf_op jit(solution)/shard_map/dot_general | solution.py:132
  462.1 7.9 %gather_fusion.1 = f32[32,256,256]{2,1,0:T(8,128)} fusion(f32[32,256,256]{2,1,0:T(8,128)} %bitcast.131, s32[1024]{0:T(1024)S(1)} %pad_clamp_fusion), kind=kCustom, calls=%fused_computation.1 | custom fusion | bytes 16777344 | tf_op jit(solution)/shard_map/gather | solution.py:142
  470.0 5.7 all-to-all-start.1
  491.7 77.8 %all-to-all-done.1 = f32[8,4,256,256]{3,2,1,0:T(8,128)} async-done(((f32[8,4,256,256]{3,2,1,0:T(8,128)}), f32[8,4,256,256]{3,2,1,0:T(8,128)}, u32[]{:S(2)}, u32[]{:S(2)}) %all-to-all-start.1) | async-done | bytes 8388640 | tf_op jit(solution)/shard_map/all_to_all | solution.py:143
  581.0 3.4 copy.49
  584.4 2.4 copy-done.4
  (136 shorter events, 62.7 us)
Async XLA Ops:
  7.2 25.6 %copy-start.6 = (s32[60]{0:T(128)S(1)}, s32[60]{0:T(128)}, u32[]{:S(2)}) copy-start(s32[60]{0:T(128)} %param.5) | copy-start | bytes 724
  7.2 101.2 %all-gather.5.cloned.1.call-start = ((), (), s32[]{:S(2)}) async-start(), calls=%async_computation.2 | async-start | bytes 4227072 | tf_op jit(solution)/shard_map/all_gather | solution.py:78
  8.1 10.8 %collective-permute-start.1 = (f32[32,256]{1,0:T(8,128)S(1)}, f32[32,256]{1,0:T(8,128)S(1)}, u32[]{:S(2)}, u32[]{:S(2)}) collective-permute-start(f32[32,256]{1,0:T(8,128)S(1)} %get-tuple-element.29), channel_id=1, source_target_pairs={{0,16},{1,17},{2,18},{3,19},{16,20},{17,21},{18,22},{19,23},{32,24... | collective-permute-start | bytes 98312 | tf_op jit(solution)/shard_map/ppermute | solution.py:76
  12.1 8.1 %collective-permute-start.7 = (f32[32,256]{1,0:T(8,128)S(1)}, f32[32,256]{1,0:T(8,128)S(1)}, u32[]{:S(2)}, u32[]{:S(2)}) collective-permute-start(f32[32,256]{1,0:T(8,128)S(1)} %get-tuple-element.30), channel_id=1, source_target_pairs={{0,112},{1,113},{2,114},{3,115},{16,116},{17,117},{18,118},{19,119... | collective-permute-start | bytes 98312 | tf_op jit(solution)/shard_map/ppermute | solution.py:76
  15.0 6.5 %collective-permute-start.6 = (f32[32,256]{1,0:T(8,128)S(1)}, f32[32,256]{1,0:T(8,128)S(1)}, u32[]{:S(2)}, u32[]{:S(2)}) collective-permute-start(f32[32,256]{1,0:T(8,128)S(1)} %get-tuple-element.31), channel_id=1, source_target_pairs={{0,96},{1,97},{2,98},{3,99},{16,100},{17,101},{18,102},{19,103},{3... | collective-permute-start | bytes 98312 | tf_op jit(solution)/shard_map/ppermute | solution.py:76
  16.3 6.5 %collective-permute-start.5 = (f32[32,256]{1,0:T(8,128)S(1)}, f32[32,256]{1,0:T(8,128)S(1)}, u32[]{:S(2)}, u32[]{:S(2)}) collective-permute-start(f32[32,256]{1,0:T(8,128)S(1)} %get-tuple-element.32), channel_id=1, source_target_pairs={{0,80},{1,81},{2,82},{3,83},{16,84},{17,85},{18,86},{19,87},{32,88... | collective-permute-start | bytes 98312 | tf_op jit(solution)/shard_map/ppermute | solution.py:76
  17.6 5.2 collective-permute-start.4
  18.9 3.9 collective-permute-start.3
  20.2 2.6 collective-permute-start.2
  21.5 2.3 collective-permute-start
  27.6 26.5 %all-to-all-start = ((f32[16,128,256]{2,1,0:T(8,128)}), f32[16,128,256]{2,1,0:T(8,128)S(1)}, u32[]{:S(2)}, u32[]{:S(2)}) async-start(f32[16,128,256]{2,1,0:T(8,128)} %bitcast.11), calls=%async_computation | async-start | bytes 4194304 | tf_op jit(solution)/shard_map/all_to_all | solution.py:84
  32.7 409.9 %all-gather.7.cloned.1.call-start = ((), (), s32[]{:S(2)}) async-start(), calls=%async_computation.3 | async-start | bytes 8912896 | tf_op jit(solution)/shard_map/all_gather | solution.py:107
  115.2 2.0 copy-start
  138.8 4.1 copy-start.1
  143.4 2.5 copy-start.2
  353.1 10.2 %copy-start.7 = (s32[60]{0:T(128)S(1)}, s32[60]{0:T(128)}, u32[]{:S(2)}) copy-start(s32[60]{0:T(128)} %param.7) | copy-start | bytes 724
  353.7 42.1 %copy-start.5 = (s32[60]{0:T(128)S(1)}, s32[60]{0:T(128)}, u32[]{:S(2)}) copy-start(s32[60]{0:T(128)} %param.6) | copy-start | bytes 724
  354.6 3.6 collective-permute-start.15
  355.3 3.6 collective-permute-start.14
  356.0 4.2 collective-permute-start.13
  356.8 6.7 %collective-permute-start.12 = (f32[128,1024]{1,0:T(8,128)}, f32[128,1024]{1,0:T(8,128)S(1)}, u32[]{:S(2)}, u32[]{:S(2)}) collective-permute-start(f32[128,1024]{1,0:T(8,128)} %slice_select_fusion), channel_id=1, source_target_pairs={{8,64},{24,81},{40,98},{56,115},{72,4},{88,21},{104,38},{120,55},{... | collective-permute-start | bytes 1572872 | tf_op jit(solution)/shard_map/ppermute | solution.py:117
  357.5 6.0 %collective-permute-start.11 = (f32[128,1024]{1,0:T(8,128)}, f32[128,1024]{1,0:T(8,128)S(1)}, u32[]{:S(2)}, u32[]{:S(2)}) collective-permute-start(f32[128,1024]{1,0:T(8,128)} %slice_select_fusion), channel_id=1, source_target_pairs={{5,48},{21,65},{37,82},{53,99},{69,116},{85,5},{101,22},{117,39},{... | collective-permute-start | bytes 1572872 | tf_op jit(solution)/shard_map/ppermute | solution.py:117
  358.2 5.3 collective-permute-start.10
  358.9 34.2 %collective-permute-start.9 = (f32[128,1024]{1,0:T(8,128)}, f32[128,1024]{1,0:T(8,128)S(1)}, u32[]{:S(2)}, u32[]{:S(2)}) collective-permute-start(f32[128,1024]{1,0:T(8,128)} %slice_select_fusion), channel_id=1, source_target_pairs={{1,16},{17,33},{33,50},{49,67},{65,84},{81,101},{97,118},{113,7},{... | collective-permute-start | bytes 1572872 | tf_op jit(solution)/shard_map/ppermute | solution.py:117
  360.2 32.9 %collective-permute-start.8 = (f32[128,1024]{1,0:T(8,128)}, f32[128,1024]{1,0:T(8,128)S(1)}, u32[]{:S(2)}, u32[]{:S(2)}) collective-permute-start(f32[128,1024]{1,0:T(8,128)} %slice_select_fusion), channel_id=1, source_target_pairs={{0,0},{16,17},{32,34},{48,51},{64,68},{80,85},{96,102},{112,119},{... | collective-permute-start | bytes 1572872 | tf_op jit(solution)/shard_map/ppermute | solution.py:117
  394.3 8.0 %collective-permute-start.18 = (f32[128,1024]{1,0:T(8,128)S(1)}, f32[128,1024]{1,0:T(8,128)S(1)}, u32[]{:S(2)}, u32[]{:S(2)}) collective-permute-start(f32[128,1024]{1,0:T(8,128)S(1)} %get-tuple-element.28), channel_id=1, source_target_pairs={{0,96},{16,112},{32,0},{48,16},{64,32},{80,48},{96,64},{112,80},{1... | collective-permute-start | bytes 1572872 | tf_op jit(solution)/shard_map/ppermute | solution.py:122
  394.3 9.6 %collective-permute-start.17 = (f32[128,1024]{1,0:T(8,128)S(1)}, f32[128,1024]{1,0:T(8,128)S(1)}, u32[]{:S(2)}, u32[]{:S(2)}) collective-permute-start(f32[128,1024]{1,0:T(8,128)S(1)} %get-tuple-element.28), channel_id=1, source_target_pairs={{0,64},{16,80},{32,96},{48,112},{64,0},{80,16},{96,32},{112,48},{1... | collective-permute-start | bytes 1572872 | tf_op jit(solution)/shard_map/ppermute | solution.py:122
  394.3 25.7 %collective-permute-start.16 = (f32[128,1024]{1,0:T(8,128)S(1)}, f32[128,1024]{1,0:T(8,128)S(1)}, u32[]{:S(2)}, u32[]{:S(2)}) collective-permute-start(f32[128,1024]{1,0:T(8,128)S(1)} %get-tuple-element.28), channel_id=1, source_target_pairs={{0,32},{16,48},{32,64},{48,80},{64,96},{80,112},{96,0},{112,16},{1... | collective-permute-start | bytes 1572872 | tf_op jit(solution)/shard_map/ppermute | solution.py:122
  420.0 1.9 copy-start.3
  420.3 5.6 collective-permute-start.19
  470.0 99.5 %all-to-all-start.1 = ((f32[8,4,256,256]{3,2,1,0:T(8,128)}), f32[8,4,256,256]{3,2,1,0:T(8,128)}, u32[]{:S(2)}, u32[]{:S(2)}) async-start(f32[8,4,256,256]{3,2,1,0:T(8,128)} %bitcast.127), calls=%async_computation.1 | async-start | bytes 16777216 | tf_op jit(solution)/shard_map/all_to_all | solution.py:143
  569.5 11.5 %slice-start = ((s8[8388608]{0:T(1024)(128)(4,1)}), s8[4194304]{0:T(1024)(128)(4,1)S(1)}, s32[]{:S(2)}) async-start(s8[8388608]{0:T(1024)(128)(4,1)} %bitcast.133), calls=%async_computation.4 | async-start | bytes 8388608
  575.2 5.7 slice-start.1
  580.9 5.9 copy-start.4
Sparse Core Ops, SparseCore 0:
  24.6 83.7 all-gather.4
  354.7 87.7 all-gather.6

commit v11 on v10

--- a/solution.py
+++ b/solution.py
@@ -129,17 +129,17 @@
     pos = jnp.where(own_d % 2 == 0, own_d // 2, grid_rows // 2 + par_d // 2)
     col_factor = combined[pos].reshape(cols_dev, tile, lead_w)
 
-    prod = lax.dot_general(
-        factor_rows.reshape(rows_dev * tile, lead_w),
-        col_factor.reshape(cols_dev * tile, lead_w),
-        (((1,), (1,)), ((), ())),
-        precision=SCHUR_PRECISION,
-    )
-    prod = prod.reshape(rows_dev, tile, cols_dev, tile).transpose(0, 2, 1, 3)
-    schur = (current - prod).reshape((rows_dev * cols_dev,) + current.shape[2:])
-
-    flat_idx = send_local[:, None] * cols_dev + col_local[None, :]
-    outgoing = schur[flat_idx]
+    col_sorted = col_factor[col_local].reshape(cols_dev * tile, lead_w)
+    rows_out = []
+    for slot in range(rows_dev):
+        src = send_local[slot]
+        left = lax.dynamic_index_in_dim(factor_rows, src, keepdims=False)
+        prod = lax.dot_general(
+            left, col_sorted, (((1,), (1,)), ((), ())), precision=SCHUR_PRECISION
+        ).reshape(tile, cols_dev, tile).transpose(1, 0, 2)
+        front_row = lax.dynamic_index_in_dim(current, src, keepdims=False)[col_local]
+        rows_out.append(front_row - prod)
+    outgoing = jnp.stack(rows_out)
     incoming = lax.all_to_all(outgoing, "row", split_axis=0, concat_axis=0, tiled=True)
     keep = (recv_valid[:, None] & col_valid[None, :])[:, :, None, None]
     parent = jnp.stack(

time: 605 us -> 644 us (1.064)
  the two profiles are of different devices: /device:TPU:1 before, /device:TPU:96 now
where the time goes in v11:
time: 644 us; the launch traced here: 633 us
  other arithmetic  216 us (34%)
  waiting for transfers between devices  184 us (29%)
  local copies, waits for them, and re-layouts  67.5 us (10%)
  starting transfers between devices  57.8 us (9%)
  matrix products  56.6 us (9%)
  between operations  52 us (8%)
    another operation x34, other arithmetic, local(): aug_factor = lax.linalg.cholesky(aug, symmetrize_input=False)  195 us
    all_to_all x1, waiting for transfers between devices, local(): lax.all_to_all(outgoing, 'row', split_axis=0, concat_axis=0, tiled=True)  78.4 us
    all_gather x1, waiting for transfers between devices, local(): everything = lax.all_gather(held, ('row', 'col'))  47.5 us
    dot_general x8, matrix products, local(): lax.dot_general(left, col_sorted, (((1,), (1,)), ((), ())), precision=SCH...  29.6 us
    another operation x16, matrix products, local(): aug_factor = lax.linalg.cholesky(aug, symmetrize_input=False)  27 us
    ppermute x8, starting transfers between devices, local(): moved = lax.ppermute(piece, ('row', 'col'), perm)  23.3 us
    all_to_all x1, waiting for transfers between devices, local(): lax.all_to_all(panel_col, 'col', split_axis=0, concat_axis=0, tiled=True)  23 us
    ppermute x3, waiting for transfers between devices, local(): ring.append(lax.ppermute(mine, 'row', perm))  21.6 us
  transfers between devices with their start and end apart: 24, of which 9 were waited for; matrix products, arithmetic and copies ran while one was open for 8% of the time, Pallas kernels for 0%

profile of v11, /device:TPU:96, one launch (start us, length us, event | category | flops | bytes accessed | tf_op | source)
XLA Modules:
  0.0 633.1 jit_solution(11745632295881198472)
XLA Ops:
  8.8 4.8 collective-permute-start.1
  13.6 4.3 collective-permute-start.2
  26.7 3.1 slice.348
  29.7 4.5 all-to-all-start
  35.7 23.0 %all-to-all-done = f32[16,128,256]{2,1,0:T(8,128)S(1)} async-done(((f32[16,128,256]{2,1,0:T(8,128)}), f32[16,128,256]{2,1,0:T(8,128)S(1)}, u32[]{:S(2)}, u32[]{:S(2)}) %all-to-all-start) | async-done | bytes 2097184 | tf_op jit(solution)/shard_map/all_to_all | solution.py:84
  60.2 47.5 %all-gather.5.cloned.1.call-done = f32[4096,256]{1,0:T(8,128)} async-done(((f32[32,256]{1,0:T(8,128)}), f32[4096,256]{1,0:T(8,128)}) %all-gather.5.cloned.1.call-update) | async-done | bytes 4194320 | tf_op jit(solution)/shard_map/all_gather | solution.py:78
  107.7 5.8 copy.14
  116.6 11.7 %cholesky.252 = f32[128,128]{1,0:T(8,128)S(1)} custom-call(f32[128,128]{1,0:T(8,128)S(1)} %cholesky.658), custom_call_target="Cholesky" | custom-call | tf_op jit(solution)/shard_map/cholesky | solution.py:101
  128.3 9.8 %custom-call.50 = f32[1,128,128]{1,2,0:T(8,128)S(1)} custom-call(f32[1,128,128]{2,1,0:T(8,128)S(1)} %get-tuple-element.69), custom_call_target="InvertDiagBlocksLowerTriangular" | custom-call | tf_op jit(solution)/shard_map/cholesky | solution.py:101
  138.1 3.0 cholesky.281
  145.8 11.7 %cholesky.274 = f32[128,128]{1,0:T(8,128)S(1)} custom-call(f32[128,128]{1,0:T(8,128)S(1)} %cholesky.662), custom_call_target="Cholesky" | custom-call | tf_op jit(solution)/shard_map/cholesky | solution.py:101
  158.2 9.8 %custom-call.51 = f32[1,128,128]{1,2,0:T(8,128)S(1)} custom-call(f32[1,128,128]{2,1,0:T(8,128)S(1)} %get-tuple-element.66), custom_call_target="InvertDiagBlocksLowerTriangular" | custom-call | tf_op jit(solution)/shard_map/cholesky | solution.py:101
  171.6 11.9 %cholesky.526 = f32[128,128]{1,0:T(8,128)S(1)} custom-call(f32[128,128]{1,0:T(8,128)S(1)} %cholesky.667), custom_call_target="Cholesky" | custom-call | tf_op jit(solution)/shard_map/cholesky | solution.py:101
  184.7 9.8 %custom-call.52 = f32[1,128,128]{1,2,0:T(8,128)S(1)} custom-call(f32[1,128,128]{2,1,0:T(8,128)S(1)} %get-tuple-element.63), custom_call_target="InvertDiagBlocksLowerTriangular" | custom-call | tf_op jit(solution)/shard_map/cholesky | solution.py:101
  198.3 11.7 %cholesky.545 = f32[128,128]{1,0:T(8,128)S(1)} custom-call(f32[128,128]{1,0:T(8,128)S(1)} %cholesky.672), custom_call_target="Cholesky" | custom-call | tf_op jit(solution)/shard_map/cholesky | solution.py:101
  211.3 9.8 %custom-call.53 = f32[1,128,128]{1,2,0:T(8,128)S(1)} custom-call(f32[1,128,128]{2,1,0:T(8,128)S(1)} %get-tuple-element.60), custom_call_target="InvertDiagBlocksLowerTriangular" | custom-call | tf_op jit(solution)/shard_map/cholesky | solution.py:101
  225.0 11.9 %cholesky.564 = f32[128,128]{1,0:T(8,128)S(1)} custom-call(f32[128,128]{1,0:T(8,128)S(1)} %cholesky.677), custom_call_target="Cholesky" | custom-call | tf_op jit(solution)/shard_map/cholesky | solution.py:101
  238.2 9.8 %custom-call.54 = f32[1,128,128]{1,2,0:T(8,128)S(1)} custom-call(f32[1,128,128]{2,1,0:T(8,128)S(1)} %get-tuple-element.57), custom_call_target="InvertDiagBlocksLowerTriangular" | custom-call | tf_op jit(solution)/shard_map/cholesky | solution.py:101
  251.9 11.7 %cholesky.584 = f32[128,128]{1,0:T(8,128)S(1)} custom-call(f32[128,128]{1,0:T(8,128)S(1)} %cholesky.682), custom_call_target="Cholesky" | custom-call | tf_op jit(solution)/shard_map/cholesky | solution.py:101
  264.9 10.2 %custom-call.55 = f32[1,128,128]{1,2,0:T(8,128)S(1)} custom-call(f32[1,128,128]{2,1,0:T(8,128)S(1)} %get-tuple-element.54), custom_call_target="InvertDiagBlocksLowerTriangular" | custom-call | tf_op jit(solution)/shard_map/cholesky | solution.py:101
  278.6 11.7 %cholesky.604 = f32[128,128]{1,0:T(8,128)S(1)} custom-call(f32[128,128]{1,0:T(8,128)S(1)} %cholesky.687), custom_call_target="Cholesky" | custom-call | tf_op jit(solution)/shard_map/cholesky | solution.py:101
  291.6 9.8 %custom-call.56 = f32[1,128,128]{1,2,0:T(8,128)S(1)} custom-call(f32[1,128,128]{2,1,0:T(8,128)S(1)} %get-tuple-element.51), custom_call_target="InvertDiagBlocksLowerTriangular" | custom-call | tf_op jit(solution)/shard_map/cholesky | solution.py:101
  304.6 11.9 %cholesky.624 = f32[128,128]{1,0:T(8,128)S(1)} custom-call(f32[128,128]{1,0:T(8,128)S(1)} %cholesky.692), custom_call_target="Cholesky" | custom-call | tf_op jit(solution)/shard_map/cholesky | solution.py:101
  317.7 9.8 %custom-call.57 = f32[1,128,128]{1,2,0:T(8,128)S(1)} custom-call(f32[1,128,128]{2,1,0:T(8,128)S(1)} %get-tuple-element.48), custom_call_target="InvertDiagBlocksLowerTriangular" | custom-call | tf_op jit(solution)/shard_map/cholesky | solution.py:101
  330.1 11.7 %cholesky.641 = f32[128,128]{1,0:T(8,128)S(1)} custom-call(f32[128,128]{1,0:T(8,128)S(1)} %convolution_subtract_fusion.4), custom_call_target="Cholesky" | custom-call | tf_op jit(solution)/shard_map/cholesky | solution.py:101
  349.4 2.9 select_select_fusion
  359.3 17.8 %collective-permute-start.9 = (f32[128,1024]{1,0:T(8,128)}, f32[128,1024]{1,0:T(8,128)S(1)}, u32[]{:S(2)}, u32[]{:S(2)}) collective-permute-start(f32[128,1024]{1,0:T(8,128)} %slice_select_fusion), channel_id=1, source_target_pairs={{1,16},{17,33},{33,50},{49,67},{65,84},{81,101},{97,118},{113,7},{... | collective-permute-start | bytes 1572872 | tf_op jit(solution)/shard_map/ppermute | solution.py:117
  377.2 11.4 %collective-permute-done.9 = f32[128,1024]{1,0:T(8,128)S(1)} collective-permute-done((f32[128,1024]{1,0:T(8,128)}, f32[128,1024]{1,0:T(8,128)S(1)}, u32[]{:S(2)}, u32[]{:S(2)}) %collective-permute-start.9) | collective-permute-done | bytes 524320 | tf_op jit(solution)/shard_map/ppermute | solution.py:117
  389.9 3.5 collective-permute-start.17
  393.6 17.3 %collective-permute-done.16 = f32[128,1024]{1,0:T(8,128)S(1)} collective-permute-done((f32[128,1024]{1,0:T(8,128)S(1)}, f32[128,1024]{1,0:T(8,128)S(1)}, u32[]{:S(2)}, u32[]{:S(2)}) %collective-permute-start.16) | collective-permute-done | bytes 524320 | tf_op jit(solution)/shard_map/ppermute | solution.py:122
  410.8 4.4 collective-permute-done.18
  416.7 5.1 collective-permute-start.19
  437.5 5.9 dynamic-slice_bitcast_fusion
  443.4 2.9 gather_fusion
  466.1 3.2 constant_dynamic-update-slice_fusion
  469.3 5.0 gather_fusion.1
  474.3 5.0 gather_fusion.2
  479.3 5.8 fusion.23
  485.1 4.7 fusion.20
  489.8 3.1 fusion.17
  492.9 3.1 fusion.14
  496.1 3.4 fusion.11
  499.5 3.1 fusion.8
  502.6 3.1 fusion.5
  505.7 3.1 fusion.2
  508.9 5.0 all-to-all-start.1
  530.1 78.4 %all-to-all-done.1 = f32[8,4,256,256]{3,2,1,0:T(8,128)} async-done(((f32[8,4,256,256]{3,2,1,0:T(8,128)}), f32[8,4,256,256]{3,2,1,0:T(8,128)}, u32[]{:S(2)}, u32[]{:S(2)}) %all-to-all-start.1) | async-done | bytes 8388640 | tf_op jit(solution)/shard_map/all_to_all | solution.py:143
  620.0 3.4 copy.55
  (168 shorter events, 99.7 us)
Async XLA Ops:
  7.2 27.2 %copy-start.15 = (s32[60]{0:T(128)S(1)}, s32[60]{0:T(128)}, u32[]{:S(2)}) copy-start(s32[60]{0:T(128)} %param.5) | copy-start | bytes 724
  7.2 100.6 %all-gather.5.cloned.1.call-start = ((), (), s32[]{:S(2)}) async-start(), calls=%async_computation.2 | async-start | bytes 4227072 | tf_op jit(solution)/shard_map/all_gather | solution.py:78
  8.1 12.4 %collective-permute-start = (f32[32,256]{1,0:T(8,128)S(1)}, f32[32,256]{1,0:T(8,128)S(1)}, u32[]{:S(2)}, u32[]{:S(2)}) collective-permute-start(f32[32,256]{1,0:T(8,128)S(1)} %get-tuple-element.42), channel_id=1, source_target_pairs={{0,0},{1,1},{2,2},{3,3},{16,4},{17,5},{18,6},{19,7},{32,8},{33,9},... | collective-permute-start | bytes 98312 | tf_op jit(solution)/shard_map/ppermute | solution.py:76
  8.8 13.0 %collective-permute-start.1 = (f32[32,256]{1,0:T(8,128)S(1)}, f32[32,256]{1,0:T(8,128)S(1)}, u32[]{:S(2)}, u32[]{:S(2)}) collective-permute-start(f32[32,256]{1,0:T(8,128)S(1)} %get-tuple-element.35), channel_id=1, source_target_pairs={{0,16},{1,17},{2,18},{3,19},{16,20},{17,21},{18,22},{19,23},{32,24... | collective-permute-start | bytes 98312 | tf_op jit(solution)/shard_map/ppermute | solution.py:76
  13.6 9.5 %collective-permute-start.2 = (f32[32,256]{1,0:T(8,128)S(1)}, f32[32,256]{1,0:T(8,128)S(1)}, u32[]{:S(2)}, u32[]{:S(2)}) collective-permute-start(f32[32,256]{1,0:T(8,128)S(1)} %get-tuple-element.41), channel_id=1, source_target_pairs={{0,32},{1,33},{2,34},{3,35},{16,36},{17,37},{18,38},{19,39},{32,40... | collective-permute-start | bytes 98312 | tf_op jit(solution)/shard_map/ppermute | solution.py:76
  17.9 6.5 %collective-permute-start.3 = (f32[32,256]{1,0:T(8,128)S(1)}, f32[32,256]{1,0:T(8,128)S(1)}, u32[]{:S(2)}, u32[]{:S(2)}) collective-permute-start(f32[32,256]{1,0:T(8,128)S(1)} %get-tuple-element.40), channel_id=1, source_target_pairs={{0,48},{1,49},{2,50},{3,51},{16,52},{17,53},{18,54},{19,55},{32,56... | collective-permute-start | bytes 98312 | tf_op jit(solution)/shard_map/ppermute | solution.py:76
  19.2 5.2 collective-permute-start.4
  20.5 3.9 collective-permute-start.5
  21.8 3.1 collective-permute-start.6
  23.1 2.9 collective-permute-start.7
  29.7 29.0 %all-to-all-start = ((f32[16,128,256]{2,1,0:T(8,128)}), f32[16,128,256]{2,1,0:T(8,128)S(1)}, u32[]{:S(2)}, u32[]{:S(2)}) async-start(f32[16,128,256]{2,1,0:T(8,128)} %bitcast.11), calls=%async_computation | async-start | bytes 4194304 | tf_op jit(solution)/shard_map/all_to_all | solution.py:84
  34.2 445.0 %all-gather.7.cloned.1.call-start = ((), (), s32[]{:S(2)}) async-start(), calls=%async_computation.3 | async-start | bytes 8912896 | tf_op jit(solution)/shard_map/all_gather | solution.py:107
  114.5 2.0 copy-start.2
  138.1 4.1 copy-start.3
  142.7 2.5 copy-start.4
  352.2 24.9 %copy-start.16 = (s32[60]{0:T(128)S(1)}, s32[60]{0:T(128)}, u32[]{:S(2)}) copy-start(s32[60]{0:T(128)} %param.7) | copy-start | bytes 724
  352.8 40.5 %copy-start.14 = (s32[60]{0:T(128)S(1)}, s32[60]{0:T(128)}, u32[]{:S(2)}) copy-start(s32[60]{0:T(128)} %param.6) | copy-start | bytes 724
  353.7 4.1 collective-permute-start.10
  354.4 4.1 collective-permute-start.11
  355.2 4.1 collective-permute-start.12
  355.9 21.4 %collective-permute-start.13 = (f32[128,1024]{1,0:T(8,128)}, f32[128,1024]{1,0:T(8,128)S(1)}, u32[]{:S(2)}, u32[]{:S(2)}) collective-permute-start(f32[128,1024]{1,0:T(8,128)} %slice_select_fusion), channel_id=1, source_target_pairs={{9,80},{25,97},{41,114},{57,3},{73,20},{89,37},{105,54},{121,71},{... | collective-permute-start | bytes 1572872 | tf_op jit(solution)/shard_map/ppermute | solution.py:117
  357.2 20.1 %collective-permute-start.14 = (f32[128,1024]{1,0:T(8,128)}, f32[128,1024]{1,0:T(8,128)S(1)}, u32[]{:S(2)}, u32[]{:S(2)}) collective-permute-start(f32[128,1024]{1,0:T(8,128)} %slice_select_fusion), channel_id=1, source_target_pairs={{12,96},{28,113},{44,2},{60,19},{76,36},{92,53},{108,70},{124,87},... | collective-permute-start | bytes 1572872 | tf_op jit(solution)/shard_map/ppermute | solution.py:117
  357.9 19.4 %collective-permute-start.15 = (f32[128,1024]{1,0:T(8,128)}, f32[128,1024]{1,0:T(8,128)S(1)}, u32[]{:S(2)}, u32[]{:S(2)}) collective-permute-start(f32[128,1024]{1,0:T(8,128)} %slice_select_fusion), channel_id=1, source_target_pairs={{13,112},{29,1},{45,18},{61,35},{77,52},{93,69},{109,86},{125,103}... | collective-permute-start | bytes 1572872 | tf_op jit(solution)/shard_map/ppermute | solution.py:117
  358.6 18.6 %collective-permute-start.8 = (f32[128,1024]{1,0:T(8,128)}, f32[128,1024]{1,0:T(8,128)S(1)}, u32[]{:S(2)}, u32[]{:S(2)}) collective-permute-start(f32[128,1024]{1,0:T(8,128)} %slice_select_fusion), channel_id=1, source_target_pairs={{0,0},{16,17},{32,34},{48,51},{64,68},{80,85},{96,102},{112,119},{... | collective-permute-start | bytes 1572872 | tf_op jit(solution)/shard_map/ppermute | solution.py:117
  359.3 29.4 %collective-permute-start.9 = (f32[128,1024]{1,0:T(8,128)}, f32[128,1024]{1,0:T(8,128)S(1)}, u32[]{:S(2)}, u32[]{:S(2)}) collective-permute-start(f32[128,1024]{1,0:T(8,128)} %slice_select_fusion), channel_id=1, source_target_pairs={{1,16},{17,33},{33,50},{49,67},{65,84},{81,101},{97,118},{113,7},{... | collective-permute-start | bytes 1572872 | tf_op jit(solution)/shard_map/ppermute | solution.py:117
  389.9 21.0 %collective-permute-start.16 = (f32[128,1024]{1,0:T(8,128)S(1)}, f32[128,1024]{1,0:T(8,128)S(1)}, u32[]{:S(2)}, u32[]{:S(2)}) collective-permute-start(f32[128,1024]{1,0:T(8,128)S(1)} %get-tuple-element.26), channel_id=1, source_target_pairs={{0,32},{16,48},{32,64},{48,80},{64,96},{80,112},{96,0},{112,16},{1... | collective-permute-start | bytes 1572872 | tf_op jit(solution)/shard_map/ppermute | solution.py:122
  389.9 21.0 %collective-permute-start.17 = (f32[128,1024]{1,0:T(8,128)S(1)}, f32[128,1024]{1,0:T(8,128)S(1)}, u32[]{:S(2)}, u32[]{:S(2)}) collective-permute-start(f32[128,1024]{1,0:T(8,128)S(1)} %get-tuple-element.26), channel_id=1, source_target_pairs={{0,64},{16,80},{32,96},{48,112},{64,0},{80,16},{96,32},{112,48},{1... | collective-permute-start | bytes 1572872 | tf_op jit(solution)/shard_map/ppermute | solution.py:122
  393.4 21.8 %collective-permute-start.18 = (f32[128,1024]{1,0:T(8,128)S(1)}, f32[128,1024]{1,0:T(8,128)S(1)}, u32[]{:S(2)}, u32[]{:S(2)}) collective-permute-start(f32[128,1024]{1,0:T(8,128)S(1)} %get-tuple-element.26), channel_id=1, source_target_pairs={{0,96},{16,112},{32,0},{48,16},{64,32},{80,48},{96,64},{112,80},{1... | collective-permute-start | bytes 1572872 | tf_op jit(solution)/shard_map/ppermute | solution.py:122
  410.8 5.9 copy-start.10
  410.8 11.0 %copy-start.11 = (f32[128,1024]{1,0:T(8,128)}, f32[128,1024]{1,0:T(8,128)S(1)}, u32[]{:S(2)}) copy-start(f32[128,1024]{1,0:T(8,128)S(1)} %collective-permute-done.17) | copy-start | bytes 1572868
  415.2 6.6 %copy-start.12 = (f32[128,1024]{1,0:T(8,128)}, f32[128,1024]{1,0:T(8,128)S(1)}, u32[]{:S(2)}) copy-start(f32[128,1024]{1,0:T(8,128)S(1)} %collective-permute-done.18) | copy-start | bytes 1572868
  416.7 49.4 %collective-permute-start.19 = (f32[4,128,1024]{2,1,0:T(8,128)}, f32[4,128,1024]{2,1,0:T(8,128)}, u32[]{:S(2)}, u32[]{:S(2)}) collective-permute-start(f32[4,128,1024]{2,1,0:T(8,128)} %pad_maximum_fusion), channel_id=1, source_target_pairs={{0,16},{16,0},{32,48},{48,32},{64,80},{80,64},{96,112},{112,96},{1... | collective-permute-start | bytes 6291464 | tf_op jit(solution)/shard_map/ppermute | solution.py:124
  479.2 5.8 copy-start.9
  479.3 5.8 copy-start
  479.3 10.5 %copy-start.1 = (f32[2048,1024]{1,0:T(8,128)S(1)}, f32[2048,1024]{1,0:T(8,128)}, u32[]{:S(2)}) copy-start(f32[2048,1024]{1,0:T(8,128)} %all-gather.7.cloned.1.call-done) | copy-start | bytes 25165828
  485.1 4.7 copy-start.8
  489.8 3.1 copy-start.7
  492.9 3.2 copy-start.6
  496.1 3.4 copy-start.5
  508.9 99.6 %all-to-all-start.1 = ((f32[8,4,256,256]{3,2,1,0:T(8,128)}), f32[8,4,256,256]{3,2,1,0:T(8,128)}, u32[]{:S(2)}, u32[]{:S(2)}) async-start(f32[8,4,256,256]{3,2,1,0:T(8,128)} %fusion.2), calls=%async_computation.1 | async-start | bytes 16777216 | tf_op jit(solution)/shard_map/all_to_all | solution.py:143
  608.5 11.5 %slice-start = ((s8[8388608]{0:T(1024)(128)(4,1)}), s8[4194304]{0:T(1024)(128)(4,1)S(1)}, s32[]{:S(2)}) async-start(s8[8388608]{0:T(1024)(128)(4,1)} %bitcast.286), calls=%async_computation.4 | async-start | bytes 8388608
  614.2 5.7 slice-start.1
  619.9 5.9 copy-start.13
Sparse Core Ops, SparseCore 0:
  26.8 80.9 all-gather.4
  353.9 88.9 all-gather.6

commit v12 on v10

--- a/solution.py
+++ b/solution.py
@@ -104,7 +104,9 @@
     start = jnp.clip(my_tile_row * tile + (my_col % 2) * half, 0, lead_w - half)
     chol_rows = lax.dynamic_slice(chol, (start, 0), (half, lead_w))
     piece = jnp.where(my_tile_row < LEAD, chol_rows, solved)
-    factor_rows = lax.all_gather(piece, "col").reshape(rows_dev, tile, lead_w)
+    copies = jnp.broadcast_to(piece[None], (grid_cols,) + piece.shape)
+    factor_rows = lax.all_to_all(copies, "col", split_axis=0, concat_axis=0, tiled=True)
+    factor_rows = factor_rows.reshape(rows_dev, tile, lead_w)
 
     src_row = my_col % grid_rows
     mine = None

time: 605 us -> 727 us (1.20)
  waiting for transfers between devices: 214 us -> 278 us
  starting transfers between devices: 37.2 us -> 86.4 us
  local copies, waits for them, and re-layouts: 44.9 us -> 54.7 us
    ppermute x8, waiting for transfers between devices: 29.7 us -> 101 us  [local(): moved = lax.ppermute(piece, ('row', 'col'), perm)]
    ppermute x3, starting transfers between devices: 1.47 us -> 45.9 us  [local(): ring.append(lax.ppermute(mine, 'row', perm))]
    all_gather x1 -> x0, waiting for transfers between devices: 8.35 us -> none  [local(): factor_rows = lax.all_gather(piece, 'col').reshape(rows_dev, tile, lead_w)]
    unnamed x25 -> x21, local copies, waits for them, and re-layouts: 13.8 us -> 19.4 us
  transfers between devices with their start and end apart: 24 -> 24, of which waited for: 9 -> 7; matrix products, arithmetic and copies ran while one was open for 3% -> 3% of each run, Pallas kernels for 0% -> 0%
where the time goes in v12:
time: 727 us; the launch traced here: 716 us
  waiting for transfers between devices  278 us (38%)
  other arithmetic  213 us (29%)
  starting transfers between devices  86.4 us (12%)
  local copies, waits for them, and re-layouts  54.7 us (8%)
  matrix products  46.5 us (6%)
  between operations  37.1 us (5%)
    another operation x34, other arithmetic, local(): aug_factor = lax.linalg.cholesky(aug, symmetrize_input=False)  195 us
    ppermute x8, waiting for transfers between devices, local(): moved = lax.ppermute(piece, ('row', 'col'), perm)  101 us
    all_to_all x1, waiting for transfers between devices, local(): lax.all_to_all(outgoing, 'row', split_axis=0, concat_axis=0, tiled=True)  77.8 us
    all_gather x1, waiting for transfers between devices, local(): everything = lax.all_gather(held, ('row', 'col'))  52.9 us
    ppermute x3, starting transfers between devices, local(): ring.append(lax.ppermute(mine, 'row', perm))  45.9 us
    another operation x16, matrix products, local(): aug_factor = lax.linalg.cholesky(aug, symmetrize_input=False)  27 us
    ppermute x3, waiting for transfers between devices, local(): ring.append(lax.ppermute(mine, 'row', perm))  25.4 us
    all_to_all x1, waiting for transfers between devices, local(): lax.all_to_all(panel_col, 'col', split_axis=0, concat_axis=0, tiled=True)  20 us
  transfers between devices with their start and end apart: 24, of which 7 were waited for; matrix products, arithmetic and copies ran while one was open for 3% of the time, Pallas kernels for 0%

profile of v12, /device:TPU:1, one launch (start us, length us, event | category | flops | bytes accessed | tf_op | source)
XLA Modules:
  0.0 715.7 jit_solution(9319654642655583531)
XLA Ops:
  8.1 4.0 collective-permute-start.1
  12.1 2.9 collective-permute-start.7
  24.5 3.1 slice.300
  27.6 5.1 all-to-all-start
  34.0 20.0 %all-to-all-done = f32[16,128,256]{2,1,0:T(8,128)S(1)} async-done(((f32[16,128,256]{2,1,0:T(8,128)}), f32[16,128,256]{2,1,0:T(8,128)S(1)}, u32[]{:S(2)}, u32[]{:S(2)}) %all-to-all-start) | async-done | bytes 2097184 | tf_op jit(solution)/shard_map/all_to_all | solution.py:84
  55.5 52.9 %all-gather.3.cloned.1.call-done = f32[4096,256]{1,0:T(8,128)} async-done(((f32[32,256]{1,0:T(8,128)}), f32[4096,256]{1,0:T(8,128)}) %all-gather.3.cloned.1.call-update) | async-done | bytes 4194320 | tf_op jit(solution)/shard_map/all_gather | solution.py:78
  108.4 5.8 copy.12
  115.2 2.0 copy-done
  117.2 11.7 %cholesky.252 = f32[128,128]{1,0:T(8,128)S(1)} custom-call(f32[128,128]{1,0:T(8,128)S(1)} %cholesky.658), custom_call_target="Cholesky" | custom-call | tf_op jit(solution)/shard_map/cholesky | solution.py:101
  129.0 9.8 %custom-call.50 = f32[1,128,128]{1,2,0:T(8,128)S(1)} custom-call(f32[1,128,128]{2,1,0:T(8,128)S(1)} %get-tuple-element.55), custom_call_target="InvertDiagBlocksLowerTriangular" | custom-call | tf_op jit(solution)/shard_map/cholesky | solution.py:101
  138.8 3.0 cholesky.281
  143.4 2.3 constant_dynamic-update-slice_fusion.5
  146.5 11.7 %cholesky.274 = f32[128,128]{1,0:T(8,128)S(1)} custom-call(f32[128,128]{1,0:T(8,128)S(1)} %cholesky.662), custom_call_target="Cholesky" | custom-call | tf_op jit(solution)/shard_map/cholesky | solution.py:101
  158.9 9.8 %custom-call.51 = f32[1,128,128]{1,2,0:T(8,128)S(1)} custom-call(f32[1,128,128]{2,1,0:T(8,128)S(1)} %get-tuple-element.52), custom_call_target="InvertDiagBlocksLowerTriangular" | custom-call | tf_op jit(solution)/shard_map/cholesky | solution.py:101
  170.0 2.3 convolution_subtract_fusion.1
  172.2 11.9 %cholesky.526 = f32[128,128]{1,0:T(8,128)S(1)} custom-call(f32[128,128]{1,0:T(8,128)S(1)} %cholesky.667), custom_call_target="Cholesky" | custom-call | tf_op jit(solution)/shard_map/cholesky | solution.py:101
  185.4 9.8 %custom-call.52 = f32[1,128,128]{1,2,0:T(8,128)S(1)} custom-call(f32[1,128,128]{2,1,0:T(8,128)S(1)} %get-tuple-element.49), custom_call_target="InvertDiagBlocksLowerTriangular" | custom-call | tf_op jit(solution)/shard_map/cholesky | solution.py:101
  196.5 2.6 convolution_subtract_fusion.2
  199.1 11.7 %cholesky.545 = f32[128,128]{1,0:T(8,128)S(1)} custom-call(f32[128,128]{1,0:T(8,128)S(1)} %cholesky.672), custom_call_target="Cholesky" | custom-call | tf_op jit(solution)/shard_map/cholesky | solution.py:101
  212.1 9.8 %custom-call.53 = f32[1,128,128]{1,2,0:T(8,128)S(1)} custom-call(f32[1,128,128]{2,1,0:T(8,128)S(1)} %get-tuple-element.46), custom_call_target="InvertDiagBlocksLowerTriangular" | custom-call | tf_op jit(solution)/shard_map/cholesky | solution.py:101
  223.0 2.6 fusion.4
  225.7 11.9 %cholesky.564 = f32[128,128]{1,0:T(8,128)S(1)} custom-call(f32[128,128]{1,0:T(8,128)S(1)} %cholesky.677), custom_call_target="Cholesky" | custom-call | tf_op jit(solution)/shard_map/cholesky | solution.py:101
  238.9 9.8 %custom-call.54 = f32[1,128,128]{1,2,0:T(8,128)S(1)} custom-call(f32[1,128,128]{2,1,0:T(8,128)S(1)} %get-tuple-element.43), custom_call_target="InvertDiagBlocksLowerTriangular" | custom-call | tf_op jit(solution)/shard_map/cholesky | solution.py:101
  249.8 2.6 fusion.10
  252.4 11.7 %cholesky.584 = f32[128,128]{1,0:T(8,128)S(1)} custom-call(f32[128,128]{1,0:T(8,128)S(1)} %cholesky.682), custom_call_target="Cholesky" | custom-call | tf_op jit(solution)/shard_map/cholesky | solution.py:101
  265.5 10.2 %custom-call.55 = f32[1,128,128]{1,2,0:T(8,128)S(1)} custom-call(f32[1,128,128]{2,1,0:T(8,128)S(1)} %get-tuple-element.40), custom_call_target="InvertDiagBlocksLowerTriangular" | custom-call | tf_op jit(solution)/shard_map/cholesky | solution.py:101
  276.7 2.5 fusion.13
  279.3 11.7 %cholesky.604 = f32[128,128]{1,0:T(8,128)S(1)} custom-call(f32[128,128]{1,0:T(8,128)S(1)} %cholesky.687), custom_call_target="Cholesky" | custom-call | tf_op jit(solution)/shard_map/cholesky | solution.py:101
  292.3 9.8 %custom-call.56 = f32[1,128,128]{1,2,0:T(8,128)S(1)} custom-call(f32[1,128,128]{2,1,0:T(8,128)S(1)} %get-tuple-element.37), custom_call_target="InvertDiagBlocksLowerTriangular" | custom-call | tf_op jit(solution)/shard_map/cholesky | solution.py:101
  303.0 2.2 convolution_subtract_fusion.3
  305.3 11.9 %cholesky.624 = f32[128,128]{1,0:T(8,128)S(1)} custom-call(f32[128,128]{1,0:T(8,128)S(1)} %cholesky.692), custom_call_target="Cholesky" | custom-call | tf_op jit(solution)/shard_map/cholesky | solution.py:101
  318.4 9.8 %custom-call.57 = f32[1,128,128]{1,2,0:T(8,128)S(1)} custom-call(f32[1,128,128]{2,1,0:T(8,128)S(1)} %get-tuple-element.34), custom_call_target="InvertDiagBlocksLowerTriangular" | custom-call | tf_op jit(solution)/shard_map/cholesky | solution.py:101
  330.9 11.7 %cholesky.641 = f32[128,128]{1,0:T(8,128)S(1)} custom-call(f32[128,128]{1,0:T(8,128)S(1)} %convolution_subtract_fusion.4), custom_call_target="Cholesky" | custom-call | tf_op jit(solution)/shard_map/cholesky | solution.py:101
  350.2 2.9 select_select_fusion
  353.8 4.5 broadcast_in_dim.123
  358.3 4.9 all-to-all-start.1
  368.8 4.2 collective-permute-start.8
  373.2 100.6 %collective-permute-done.9 = f32[128,1024]{1,0:T(8,128)S(1)} collective-permute-done((f32[128,1024]{1,0:T(8,128)S(1)}, f32[128,1024]{1,0:T(8,128)S(1)}, u32[]{:S(2)}, u32[]{:S(2)}) %collective-permute-start.9) | collective-permute-done | bytes 524320 | tf_op jit(solution)/shard_map/ppermute | solution.py:119
  475.0 45.2 %collective-permute-start.18 = (f32[128,1024]{1,0:T(8,128)S(1)}, f32[128,1024]{1,0:T(8,128)S(1)}, u32[]{:S(2)}, u32[]{:S(2)}) collective-permute-start(f32[128,1024]{1,0:T(8,128)S(1)} %get-tuple-element.20), channel_id=1, source_target_pairs={{0,96},{16,112},{32,0},{48,16},{64,32},{80,48},{96,64},{112,80},{1... | collective-permute-start | bytes 1572872 | tf_op jit(solution)/shard_map/ppermute | solution.py:124
  521.1 21.6 %collective-permute-done.18 = f32[128,1024]{1,0:T(8,128)S(1)} collective-permute-done((f32[128,1024]{1,0:T(8,128)S(1)}, f32[128,1024]{1,0:T(8,128)S(1)}, u32[]{:S(2)}, u32[]{:S(2)}) %collective-permute-start.18) | collective-permute-done | bytes 524320 | tf_op jit(solution)/shard_map/ppermute | solution.py:124
  542.7 3.8 collective-permute-done.16
  551.4 3.2 constant_dynamic-update-slice_fusion
  554.5 5.0 gather_fusion
  559.5 19.6 %bitcast_subtract_fusion = f32[8,4,256,256]{3,2,1,0:T(8,128)} fusion(f32[8,256,1024,1]{2,1,3,0:T(8,128)} %bitcast.35, f32[4,256,1024,1]{2,1,0,3:T(8,128)} %bitcast.131, f32[8,1,4,1,256,256]{5,4,3,2,1,0:T(8,128)} %param.4), kind=kOutput, calls=%fused_computation.2 | convolution fusion | flops 12886999040 | bytes 29360128 | tf_op jit(solution)/shard_map/dot_general | solution.py:134
  579.1 7.9 %gather_fusion.1 = f32[32,256,256]{2,1,0:T(8,128)} fusion(f32[32,256,256]{2,1,0:T(8,128)} %bitcast.129, s32[1024]{0:T(1024)S(1)} %pad_clamp_fusion), kind=kCustom, calls=%fused_computation.1 | custom fusion | bytes 16777344 | tf_op jit(solution)/shard_map/gather | solution.py:144
  586.9 5.4 all-to-all-start.2
  608.3 77.8 %all-to-all-done.2 = f32[8,4,256,256]{3,2,1,0:T(8,128)} async-done(((f32[8,4,256,256]{3,2,1,0:T(8,128)}), f32[8,4,256,256]{3,2,1,0:T(8,128)}, u32[]{:S(2)}, u32[]{:S(2)}) %all-to-all-start.2) | async-done | bytes 8388640 | tf_op jit(solution)/shard_map/all_to_all | solution.py:145
  697.2 11.5 %copy.45 = f32[8,1,256,1024]{3,2,1,0:T(8,128)} copy(f32[8,1,256,1024]{3,2,1,0:T(8,128)} %bitcast.31) | data formatting | bytes 16777216
  (131 shorter events, 60.0 us)
Async XLA Ops:
  7.2 25.6 %copy-start.6 = (s32[60]{0:T(128)S(1)}, s32[60]{0:T(128)}, u32[]{:S(2)}) copy-start(s32[60]{0:T(128)} %param.5) | copy-start | bytes 724
  7.2 101.2 %all-gather.3.cloned.1.call-start = ((), (), s32[]{:S(2)}) async-start(), calls=%async_computation.3 | async-start | bytes 4227072 | tf_op jit(solution)/shard_map/all_gather | solution.py:78
  8.1 10.8 %collective-permute-start.1 = (f32[32,256]{1,0:T(8,128)S(1)}, f32[32,256]{1,0:T(8,128)S(1)}, u32[]{:S(2)}, u32[]{:S(2)}) collective-permute-start(f32[32,256]{1,0:T(8,128)S(1)} %get-tuple-element.21), channel_id=1, source_target_pairs={{0,16},{1,17},{2,18},{3,19},{16,20},{17,21},{18,22},{19,23},{32,24... | collective-permute-start | bytes 98312 | tf_op jit(solution)/shard_map/ppermute | solution.py:76
  12.1 8.1 %collective-permute-start.7 = (f32[32,256]{1,0:T(8,128)S(1)}, f32[32,256]{1,0:T(8,128)S(1)}, u32[]{:S(2)}, u32[]{:S(2)}) collective-permute-start(f32[32,256]{1,0:T(8,128)S(1)} %get-tuple-element.22), channel_id=1, source_target_pairs={{0,112},{1,113},{2,114},{3,115},{16,116},{17,117},{18,118},{19,119... | collective-permute-start | bytes 98312 | tf_op jit(solution)/shard_map/ppermute | solution.py:76
  15.0 6.5 collective-permute-start.6
  16.3 6.5 collective-permute-start.5
  17.6 5.2 collective-permute-start.4
  18.9 3.9 collective-permute-start.3
  20.2 2.6 collective-permute-start.2
  21.5 2.3 collective-permute-start
  27.6 26.5 %all-to-all-start = ((f32[16,128,256]{2,1,0:T(8,128)}), f32[16,128,256]{2,1,0:T(8,128)S(1)}, u32[]{:S(2)}, u32[]{:S(2)}) async-start(f32[16,128,256]{2,1,0:T(8,128)} %bitcast.11), calls=%async_computation | async-start | bytes 4194304 | tf_op jit(solution)/shard_map/all_to_all | solution.py:84
  115.2 2.0 copy-start
  138.8 4.1 copy-start.1
  143.4 2.5 copy-start.2
  358.3 14.7 %copy-start.7 = (s32[60]{0:T(128)S(1)}, s32[60]{0:T(128)}, u32[]{:S(2)}) copy-start(s32[60]{0:T(128)} %param.7) | copy-start | bytes 724
  358.3 162.6 %copy-start.5 = (s32[60]{0:T(128)S(1)}, s32[60]{0:T(128)}, u32[]{:S(2)}) copy-start(s32[60]{0:T(128)} %param.6) | copy-start | bytes 724
  358.3 201.2 %all-to-all-start.1 = ((f32[16,128,1024]{2,1,0:T(8,128)}), f32[16,128,1024]{2,1,0:T(8,128)}, u32[]{:S(2)}, u32[]{:S(2)}) async-start(f32[16,128,1024]{2,1,0:T(8,128)} %broadcast_in_dim.123), calls=%async_computation.1 | async-start | bytes 16777216 | tf_op jit(solution)/shard_map/all_to_all | solution.py:108
  363.2 3.6 collective-permute-start.15
  363.9 3.6 collective-permute-start.14
  364.6 4.2 collective-permute-start.13
  365.3 7.9 %collective-permute-start.12 = (f32[128,1024]{1,0:T(8,128)S(1)}, f32[128,1024]{1,0:T(8,128)S(1)}, u32[]{:S(2)}, u32[]{:S(2)}) collective-permute-start(f32[128,1024]{1,0:T(8,128)S(1)} %slice_select_fusion), channel_id=1, source_target_pairs={{8,64},{24,81},{40,98},{56,115},{72,4},{88,21},{104,38},{120,55},{... | collective-permute-start | bytes 1572872 | tf_op jit(solution)/shard_map/ppermute | solution.py:119
  366.0 7.2 %collective-permute-start.11 = (f32[128,1024]{1,0:T(8,128)S(1)}, f32[128,1024]{1,0:T(8,128)S(1)}, u32[]{:S(2)}, u32[]{:S(2)}) collective-permute-start(f32[128,1024]{1,0:T(8,128)S(1)} %slice_select_fusion), channel_id=1, source_target_pairs={{5,48},{21,65},{37,82},{53,99},{69,116},{85,5},{101,22},{117,39},{... | collective-permute-start | bytes 1572872 | tf_op jit(solution)/shard_map/ppermute | solution.py:119
  366.7 6.5 collective-permute-start.10
  367.4 106.3 %collective-permute-start.9 = (f32[128,1024]{1,0:T(8,128)S(1)}, f32[128,1024]{1,0:T(8,128)S(1)}, u32[]{:S(2)}, u32[]{:S(2)}) collective-permute-start(f32[128,1024]{1,0:T(8,128)S(1)} %slice_select_fusion), channel_id=1, source_target_pairs={{1,16},{17,33},{33,50},{49,67},{65,84},{81,101},{97,118},{113,7},{... | collective-permute-start | bytes 1572872 | tf_op jit(solution)/shard_map/ppermute | solution.py:119
  368.8 105.0 %collective-permute-start.8 = (f32[128,1024]{1,0:T(8,128)S(1)}, f32[128,1024]{1,0:T(8,128)S(1)}, u32[]{:S(2)}, u32[]{:S(2)}) collective-permute-start(f32[128,1024]{1,0:T(8,128)S(1)} %slice_select_fusion), channel_id=1, source_target_pairs={{0,0},{16,17},{32,34},{48,51},{64,68},{80,85},{96,102},{112,119},{... | collective-permute-start | bytes 1572872 | tf_op jit(solution)/shard_map/ppermute | solution.py:119
  475.0 67.7 %collective-permute-start.18 = (f32[128,1024]{1,0:T(8,128)S(1)}, f32[128,1024]{1,0:T(8,128)S(1)}, u32[]{:S(2)}, u32[]{:S(2)}) collective-permute-start(f32[128,1024]{1,0:T(8,128)S(1)} %get-tuple-element.20), channel_id=1, source_target_pairs={{0,96},{16,112},{32,0},{48,16},{64,32},{80,48},{96,64},{112,80},{1... | collective-permute-start | bytes 1572872 | tf_op jit(solution)/shard_map/ppermute | solution.py:124
  520.1 22.6 %collective-permute-start.17 = (f32[128,1024]{1,0:T(8,128)S(1)}, f32[128,1024]{1,0:T(8,128)S(1)}, u32[]{:S(2)}, u32[]{:S(2)}) collective-permute-start(f32[128,1024]{1,0:T(8,128)S(1)} %get-tuple-element.20), channel_id=1, source_target_pairs={{0,64},{16,80},{32,96},{48,112},{64,0},{80,16},{96,32},{112,48},{1... | collective-permute-start | bytes 1572872 | tf_op jit(solution)/shard_map/ppermute | solution.py:124
  520.1 26.4 %collective-permute-start.16 = (f32[128,1024]{1,0:T(8,128)S(1)}, f32[128,1024]{1,0:T(8,128)S(1)}, u32[]{:S(2)}, u32[]{:S(2)}) collective-permute-start(f32[128,1024]{1,0:T(8,128)S(1)} %get-tuple-element.20), channel_id=1, source_target_pairs={{0,32},{16,48},{32,64},{48,80},{64,96},{80,112},{96,0},{112,16},{1... | collective-permute-start | bytes 1572872 | tf_op jit(solution)/shard_map/ppermute | solution.py:124
  546.5 0.9 copy-start.3
  546.8 4.6 collective-permute-start.19
  586.9 99.2 %all-to-all-start.2 = ((f32[8,4,256,256]{3,2,1,0:T(8,128)}), f32[8,4,256,256]{3,2,1,0:T(8,128)}, u32[]{:S(2)}, u32[]{:S(2)}) async-start(f32[8,4,256,256]{3,2,1,0:T(8,128)} %bitcast.125), calls=%async_computation.2 | async-start | bytes 16777216 | tf_op jit(solution)/shard_map/all_to_all | solution.py:145
  697.2 11.5 %copy-start.4 = (f32[8,4,256,256]{3,2,1,0:T(8,128)}, f32[8,4,256,256]{3,2,1,0:T(8,128)S(1)}, u32[]{:S(2)}) copy-start(f32[8,4,256,256]{3,2,1,0:T(8,128)S(1)} %select_dynamic-update-slice_fusion) | copy-start | bytes 25165828
Sparse Core Ops, SparseCore 0:
  24.6 83.7 all-gather.2

commit v13 on v10

--- a/solution.py
+++ b/solution.py
@@ -139,7 +139,14 @@
     schur = (current - prod).reshape((rows_dev * cols_dev,) + current.shape[2:])
 
     flat_idx = send_local[:, None] * cols_dev + col_local[None, :]
-    outgoing = schur[flat_idx]
+    outgoing = jnp.stack(
+        [
+            jnp.stack(
+                [lax.dynamic_index_in_dim(schur, flat_idx[slot, b], keepdims=False) for b in range(cols_dev)]
+            )
+            for slot in range(rows_dev)
+        ]
+    )
     incoming = lax.all_to_all(outgoing, "row", split_axis=0, concat_axis=0, tiled=True)
     keep = (recv_valid[:, None] & col_valid[None, :])[:, :, None, None]
     parent = jnp.stack(

time: 605 us -> 660 us (1.091)
  the two profiles are of different devices: /device:TPU:1 before, /device:TPU:64 now
where the time goes in v13:
time: 660 us; the launch traced here: 648 us
  other arithmetic  223 us (34%)
  waiting for transfers between devices  198 us (30%)
  between operations  97.3 us (15%)
  starting transfers between devices  47 us (7%)
  matrix products  44.5 us (7%)
  local copies, waits for them, and re-layouts  39.1 us (6%)
    another operation x34, other arithmetic, local(): aug_factor = lax.linalg.cholesky(aug, symmetrize_input=False)  195 us
    all_to_all x1, waiting for transfers between devices, local(): lax.all_to_all(outgoing, 'row', split_axis=0, concat_axis=0, tiled=True)  78.6 us
    all_gather x1, waiting for transfers between devices, local(): everything = lax.all_gather(held, ('row', 'col'))  43.7 us
    ppermute x8, waiting for transfers between devices, local(): moved = lax.ppermute(piece, ('row', 'col'), perm)  28.2 us
    another operation x16, matrix products, local(): aug_factor = lax.linalg.cholesky(aug, symmetrize_input=False)  27 us
    ppermute x3, waiting for transfers between devices, local(): ring.append(lax.ppermute(mine, 'row', perm))  25.7 us
    all_to_all x1, waiting for transfers between devices, local(): lax.all_to_all(panel_col, 'col', split_axis=0, concat_axis=0, tiled=True)  20.5 us
    unnamed x17, other arithmetic  19.2 us
  transfers between devices with their start and end apart: 24, of which 8 were waited for; matrix products, arithmetic and copies ran while one was open for 3% of the time, Pallas kernels for 0%

profile of v13, /device:TPU:64, one launch (start us, length us, event | category | flops | bytes accessed | tf_op | source)
XLA Modules:
  0.0 648.3 jit_solution(2033706438824551239)
XLA Ops:
  9.9 3.0 collective-permute-start.7
  16.8 4.9 collective-permute-start.3
  25.8 3.1 slice.426
  28.8 9.0 %all-to-all-start = ((f32[16,128,256]{2,1,0:T(8,128)}), f32[16,128,256]{2,1,0:T(8,128)S(1)}, u32[]{:S(2)}, u32[]{:S(2)}) async-start(f32[16,128,256]{2,1,0:T(8,128)} %bitcast.11), calls=%async_computation | async-start | bytes 4194304 | tf_op jit(solution)/shard_map/all_to_all | solution.py:84
  39.1 20.5 %all-to-all-done = f32[16,128,256]{2,1,0:T(8,128)S(1)} async-done(((f32[16,128,256]{2,1,0:T(8,128)}), f32[16,128,256]{2,1,0:T(8,128)S(1)}, u32[]{:S(2)}, u32[]{:S(2)}) %all-to-all-start) | async-done | bytes 2097184 | tf_op jit(solution)/shard_map/all_to_all | solution.py:84
  61.1 43.7 %all-gather.5.cloned.1.call-done = f32[4096,256]{1,0:T(8,128)} async-done(((f32[32,256]{1,0:T(8,128)}), f32[4096,256]{1,0:T(8,128)}) %all-gather.5.cloned.1.call-update) | async-done | bytes 4194320 | tf_op jit(solution)/shard_map/all_gather | solution.py:78
  104.8 5.8 copy.12
  111.6 2.0 copy-done
  113.6 11.7 %cholesky.252 = f32[128,128]{1,0:T(8,128)S(1)} custom-call(f32[128,128]{1,0:T(8,128)S(1)} %cholesky.658), custom_call_target="Cholesky" | custom-call | tf_op jit(solution)/shard_map/cholesky | solution.py:101
  125.3 9.8 %custom-call.50 = f32[1,128,128]{1,2,0:T(8,128)S(1)} custom-call(f32[1,128,128]{2,1,0:T(8,128)S(1)} %get-tuple-element.93), custom_call_target="InvertDiagBlocksLowerTriangular" | custom-call | tf_op jit(solution)/shard_map/cholesky | solution.py:101
  135.2 3.0 cholesky.281
  139.7 2.3 constant_dynamic-update-slice_fusion.5
  142.9 11.7 %cholesky.274 = f32[128,128]{1,0:T(8,128)S(1)} custom-call(f32[128,128]{1,0:T(8,128)S(1)} %cholesky.662), custom_call_target="Cholesky" | custom-call | tf_op jit(solution)/shard_map/cholesky | solution.py:101
  155.2 9.8 %custom-call.51 = f32[1,128,128]{1,2,0:T(8,128)S(1)} custom-call(f32[1,128,128]{2,1,0:T(8,128)S(1)} %get-tuple-element.90), custom_call_target="InvertDiagBlocksLowerTriangular" | custom-call | tf_op jit(solution)/shard_map/cholesky | solution.py:101
  166.3 2.3 convolution_subtract_fusion.1
  168.6 11.9 %cholesky.526 = f32[128,128]{1,0:T(8,128)S(1)} custom-call(f32[128,128]{1,0:T(8,128)S(1)} %cholesky.667), custom_call_target="Cholesky" | custom-call | tf_op jit(solution)/shard_map/cholesky | solution.py:101
  181.8 9.8 %custom-call.52 = f32[1,128,128]{1,2,0:T(8,128)S(1)} custom-call(f32[1,128,128]{2,1,0:T(8,128)S(1)} %get-tuple-element.87), custom_call_target="InvertDiagBlocksLowerTriangular" | custom-call | tf_op jit(solution)/shard_map/cholesky | solution.py:101
  192.8 2.6 convolution_subtract_fusion.2
  195.4 11.7 %cholesky.545 = f32[128,128]{1,0:T(8,128)S(1)} custom-call(f32[128,128]{1,0:T(8,128)S(1)} %cholesky.672), custom_call_target="Cholesky" | custom-call | tf_op jit(solution)/shard_map/cholesky | solution.py:101
  208.4 9.8 %custom-call.53 = f32[1,128,128]{1,2,0:T(8,128)S(1)} custom-call(f32[1,128,128]{2,1,0:T(8,128)S(1)} %get-tuple-element.84), custom_call_target="InvertDiagBlocksLowerTriangular" | custom-call | tf_op jit(solution)/shard_map/cholesky | solution.py:101
  219.4 2.6 fusion.4
  222.0 11.9 %cholesky.564 = f32[128,128]{1,0:T(8,128)S(1)} custom-call(f32[128,128]{1,0:T(8,128)S(1)} %cholesky.677), custom_call_target="Cholesky" | custom-call | tf_op jit(solution)/shard_map/cholesky | solution.py:101
  235.2 9.8 %custom-call.54 = f32[1,128,128]{1,2,0:T(8,128)S(1)} custom-call(f32[1,128,128]{2,1,0:T(8,128)S(1)} %get-tuple-element.81), custom_call_target="InvertDiagBlocksLowerTriangular" | custom-call | tf_op jit(solution)/shard_map/cholesky | solution.py:101
  246.1 2.6 fusion.10
  248.8 11.7 %cholesky.584 = f32[128,128]{1,0:T(8,128)S(1)} custom-call(f32[128,128]{1,0:T(8,128)S(1)} %cholesky.682), custom_call_target="Cholesky" | custom-call | tf_op jit(solution)/shard_map/cholesky | solution.py:101
  261.8 10.2 %custom-call.55 = f32[1,128,128]{1,2,0:T(8,128)S(1)} custom-call(f32[1,128,128]{2,1,0:T(8,128)S(1)} %get-tuple-element.78), custom_call_target="InvertDiagBlocksLowerTriangular" | custom-call | tf_op jit(solution)/shard_map/cholesky | solution.py:101
  273.0 2.5 fusion.13
  275.6 11.7 %cholesky.604 = f32[128,128]{1,0:T(8,128)S(1)} custom-call(f32[128,128]{1,0:T(8,128)S(1)} %cholesky.687), custom_call_target="Cholesky" | custom-call | tf_op jit(solution)/shard_map/cholesky | solution.py:101
  288.6 9.8 %custom-call.56 = f32[1,128,128]{1,2,0:T(8,128)S(1)} custom-call(f32[1,128,128]{2,1,0:T(8,128)S(1)} %get-tuple-element.75), custom_call_target="InvertDiagBlocksLowerTriangular" | custom-call | tf_op jit(solution)/shard_map/cholesky | solution.py:101
  299.3 2.2 convolution_subtract_fusion.3
  301.6 11.9 %cholesky.624 = f32[128,128]{1,0:T(8,128)S(1)} custom-call(f32[128,128]{1,0:T(8,128)S(1)} %cholesky.692), custom_call_target="Cholesky" | custom-call | tf_op jit(solution)/shard_map/cholesky | solution.py:101
  314.7 9.8 %custom-call.57 = f32[1,128,128]{1,2,0:T(8,128)S(1)} custom-call(f32[1,128,128]{2,1,0:T(8,128)S(1)} %get-tuple-element.72), custom_call_target="InvertDiagBlocksLowerTriangular" | custom-call | tf_op jit(solution)/shard_map/cholesky | solution.py:101
  325.4 1.8 convolution_subtract_fusion.4
  327.2 11.7 %cholesky.641 = f32[128,128]{1,0:T(8,128)S(1)} custom-call(f32[128,128]{1,0:T(8,128)S(1)} %convolution_subtract_fusion.4), custom_call_target="Cholesky" | custom-call | tf_op jit(solution)/shard_map/cholesky | solution.py:101
  346.5 2.9 select_select_fusion
  355.8 16.1 %collective-permute-done.14 = f32[128,1024]{1,0:T(8,128)S(1)} collective-permute-done((f32[128,1024]{1,0:T(8,128)}, f32[128,1024]{1,0:T(8,128)S(1)}, u32[]{:S(2)}, u32[]{:S(2)}) %collective-permute-start.14) | collective-permute-done | bytes 524320 | tf_op jit(solution)/shard_map/ppermute | solution.py:117
  374.3 12.1 %collective-permute-done.8 = f32[128,1024]{1,0:T(8,128)S(1)} collective-permute-done((f32[128,1024]{1,0:T(8,128)}, f32[128,1024]{1,0:T(8,128)S(1)}, u32[]{:S(2)}, u32[]{:S(2)}) %collective-permute-start.8) | collective-permute-done | bytes 524320 | tf_op jit(solution)/shard_map/ppermute | solution.py:117
  387.7 9.0 %collective-permute-start.18 = (f32[128,1024]{1,0:T(8,128)S(1)}, f32[128,1024]{1,0:T(8,128)S(1)}, u32[]{:S(2)}, u32[]{:S(2)}) collective-permute-start(f32[128,1024]{1,0:T(8,128)S(1)} %get-tuple-element.26), channel_id=1, source_target_pairs={{0,96},{16,112},{32,0},{48,16},{64,32},{80,48},{96,64},{112,80},{1... | collective-permute-start | bytes 1572872 | tf_op jit(solution)/shard_map/ppermute | solution.py:122
  397.5 22.3 %collective-permute-done.18 = f32[128,1024]{1,0:T(8,128)S(1)} collective-permute-done((f32[128,1024]{1,0:T(8,128)S(1)}, f32[128,1024]{1,0:T(8,128)S(1)}, u32[]{:S(2)}, u32[]{:S(2)}) %collective-permute-start.18) | collective-permute-done | bytes 524320 | tf_op jit(solution)/shard_map/ppermute | solution.py:122
  419.8 3.4 collective-permute-done.16
  485.9 1.9 constant_dynamic-update-slice_fusion.3
  489.5 3.2 constant_dynamic-update-slice_fusion
  492.6 5.0 gather_fusion
  497.6 17.5 %bitcast_subtract_fusion = f32[8,4,256,256]{3,2,1,0:T(8,128)S(1)} fusion(f32[8,256,1024,1]{2,1,3,0:T(8,128)} %bitcast.191, f32[4,256,1024,1]{2,1,0,3:T(8,128)} %bitcast.198, f32[8,1,4,1,256,256]{5,4,3,2,1,0:T(8,128)} %param.4), kind=kOutput, calls=%fused_computation.1 | convolution fusion | flops 12886999040 | bytes 29360128 | tf_op jit(solution)/shard_map/dot_general | solution.py:132
  524.2 5.0 all-to-all-start.1
  545.2 78.6 %all-to-all-done.1 = f32[8,4,256,256]{3,2,1,0:T(8,128)} async-done(((f32[8,4,256,256]{3,2,1,0:T(8,128)}), f32[8,4,256,256]{3,2,1,0:T(8,128)}, u32[]{:S(2)}, u32[]{:S(2)}) %all-to-all-start.1) | async-done | bytes 8388640 | tf_op jit(solution)/shard_map/all_to_all | solution.py:150
  635.3 3.4 copy.53
  638.8 2.4 copy-done.4
  (145 shorter events, 69.4 us)
Async XLA Ops:
  7.2 30.7 %copy-start.6 = (s32[60]{0:T(128)S(1)}, s32[60]{0:T(128)}, u32[]{:S(2)}) copy-start(s32[60]{0:T(128)} %param.5) | copy-start | bytes 724
  7.2 97.6 %all-gather.5.cloned.1.call-start = ((), (), s32[]{:S(2)}) async-start(), calls=%async_computation.2 | async-start | bytes 4227072 | tf_op jit(solution)/shard_map/all_gather | solution.py:78
  8.1 8.7 %collective-permute-start.1 = (f32[32,256]{1,0:T(8,128)S(1)}, f32[32,256]{1,0:T(8,128)S(1)}, u32[]{:S(2)}, u32[]{:S(2)}) collective-permute-start(f32[32,256]{1,0:T(8,128)S(1)} %get-tuple-element.59), channel_id=1, source_target_pairs={{0,16},{1,17},{2,18},{3,19},{16,20},{17,21},{18,22},{19,23},{32,24... | collective-permute-start | bytes 98312 | tf_op jit(solution)/shard_map/ppermute | solution.py:76
  9.9 11.9 %collective-permute-start.7 = (f32[32,256]{1,0:T(8,128)S(1)}, f32[32,256]{1,0:T(8,128)S(1)}, u32[]{:S(2)}, u32[]{:S(2)}) collective-permute-start(f32[32,256]{1,0:T(8,128)S(1)} %get-tuple-element.60), channel_id=1, source_target_pairs={{0,112},{1,113},{2,114},{3,115},{16,116},{17,117},{18,118},{19,119... | collective-permute-start | bytes 98312 | tf_op jit(solution)/shard_map/ppermute | solution.py:76
  12.9 10.6 %collective-permute-start.6 = (f32[32,256]{1,0:T(8,128)S(1)}, f32[32,256]{1,0:T(8,128)S(1)}, u32[]{:S(2)}, u32[]{:S(2)}) collective-permute-start(f32[32,256]{1,0:T(8,128)S(1)} %get-tuple-element.61), channel_id=1, source_target_pairs={{0,96},{1,97},{2,98},{3,99},{16,100},{17,101},{18,102},{19,103},{3... | collective-permute-start | bytes 98312 | tf_op jit(solution)/shard_map/ppermute | solution.py:76
  14.2 10.0 %collective-permute-start.5 = (f32[32,256]{1,0:T(8,128)S(1)}, f32[32,256]{1,0:T(8,128)S(1)}, u32[]{:S(2)}, u32[]{:S(2)}) collective-permute-start(f32[32,256]{1,0:T(8,128)S(1)} %get-tuple-element.62), channel_id=1, source_target_pairs={{0,80},{1,81},{2,82},{3,83},{16,84},{17,85},{18,86},{19,87},{32,88... | collective-permute-start | bytes 98312 | tf_op jit(solution)/shard_map/ppermute | solution.py:76
  15.5 8.7 %collective-permute-start.4 = (f32[32,256]{1,0:T(8,128)S(1)}, f32[32,256]{1,0:T(8,128)S(1)}, u32[]{:S(2)}, u32[]{:S(2)}) collective-permute-start(f32[32,256]{1,0:T(8,128)S(1)} %get-tuple-element.63), channel_id=1, source_target_pairs={{0,64},{1,65},{2,66},{3,67},{16,68},{17,69},{18,70},{19,71},{32,72... | collective-permute-start | bytes 98312 | tf_op jit(solution)/shard_map/ppermute | solution.py:76
  16.8 7.4 %collective-permute-start.3 = (f32[32,256]{1,0:T(8,128)S(1)}, f32[32,256]{1,0:T(8,128)S(1)}, u32[]{:S(2)}, u32[]{:S(2)}) collective-permute-start(f32[32,256]{1,0:T(8,128)S(1)} %get-tuple-element.64), channel_id=1, source_target_pairs={{0,48},{1,49},{2,50},{3,51},{16,52},{17,53},{18,54},{19,55},{32,56... | collective-permute-start | bytes 98312 | tf_op jit(solution)/shard_map/ppermute | solution.py:76
  21.8 3.3 collective-permute-start.2
  23.5 1.6 collective-permute-start
  28.8 30.8 %all-to-all-start = ((f32[16,128,256]{2,1,0:T(8,128)}), f32[16,128,256]{2,1,0:T(8,128)S(1)}, u32[]{:S(2)}, u32[]{:S(2)}) async-start(f32[16,128,256]{2,1,0:T(8,128)} %bitcast.11), calls=%async_computation | async-start | bytes 4194304 | tf_op jit(solution)/shard_map/all_to_all | solution.py:84
  37.8 459.8 %all-gather.7.cloned.1.call-start = ((), (), s32[]{:S(2)}) async-start(), calls=%async_computation.3 | async-start | bytes 8912896 | tf_op jit(solution)/shard_map/all_gather | solution.py:107
  111.6 2.0 copy-start
  135.1 4.1 copy-start.1
  139.7 2.5 copy-start.2
  349.4 4.3 copy-start.7
  349.4 24.7 %copy-start.5 = (s32[60]{0:T(128)S(1)}, s32[60]{0:T(128)}, u32[]{:S(2)}) copy-start(s32[60]{0:T(128)} %param.6) | copy-start | bytes 724
  351.0 4.2 collective-permute-start.15
  351.7 20.2 %collective-permute-start.14 = (f32[128,1024]{1,0:T(8,128)}, f32[128,1024]{1,0:T(8,128)S(1)}, u32[]{:S(2)}, u32[]{:S(2)}) collective-permute-start(f32[128,1024]{1,0:T(8,128)} %slice_select_fusion), channel_id=1, source_target_pairs={{12,96},{28,113},{44,2},{60,19},{76,36},{92,53},{108,70},{124,87},... | collective-permute-start | bytes 1572872 | tf_op jit(solution)/shard_map/ppermute | solution.py:117
  353.0 19.6 %collective-permute-start.13 = (f32[128,1024]{1,0:T(8,128)}, f32[128,1024]{1,0:T(8,128)S(1)}, u32[]{:S(2)}, u32[]{:S(2)}) collective-permute-start(f32[128,1024]{1,0:T(8,128)} %slice_select_fusion), channel_id=1, source_target_pairs={{9,80},{25,97},{41,114},{57,3},{73,20},{89,37},{105,54},{121,71},{... | collective-permute-start | bytes 1572872 | tf_op jit(solution)/shard_map/ppermute | solution.py:117
  353.7 20.6 %collective-permute-start.12 = (f32[128,1024]{1,0:T(8,128)}, f32[128,1024]{1,0:T(8,128)S(1)}, u32[]{:S(2)}, u32[]{:S(2)}) collective-permute-start(f32[128,1024]{1,0:T(8,128)} %slice_select_fusion), channel_id=1, source_target_pairs={{8,64},{24,81},{40,98},{56,115},{72,4},{88,21},{104,38},{120,55},{... | collective-permute-start | bytes 1572872 | tf_op jit(solution)/shard_map/ppermute | solution.py:117
  354.4 19.9 %collective-permute-start.11 = (f32[128,1024]{1,0:T(8,128)}, f32[128,1024]{1,0:T(8,128)S(1)}, u32[]{:S(2)}, u32[]{:S(2)}) collective-permute-start(f32[128,1024]{1,0:T(8,128)} %slice_select_fusion), channel_id=1, source_target_pairs={{5,48},{21,65},{37,82},{53,99},{69,116},{85,5},{101,22},{117,39},{... | collective-permute-start | bytes 1572872 | tf_op jit(solution)/shard_map/ppermute | solution.py:117
  355.1 19.2 %collective-permute-start.10 = (f32[128,1024]{1,0:T(8,128)}, f32[128,1024]{1,0:T(8,128)S(1)}, u32[]{:S(2)}, u32[]{:S(2)}) collective-permute-start(f32[128,1024]{1,0:T(8,128)} %slice_select_fusion), channel_id=1, source_target_pairs={{4,32},{20,49},{36,66},{52,83},{68,100},{84,117},{100,6},{116,23},... | collective-permute-start | bytes 1572872 | tf_op jit(solution)/shard_map/ppermute | solution.py:117
  371.9 2.4 collective-permute-start.9
  372.6 13.9 %collective-permute-start.8 = (f32[128,1024]{1,0:T(8,128)}, f32[128,1024]{1,0:T(8,128)S(1)}, u32[]{:S(2)}, u32[]{:S(2)}) collective-permute-start(f32[128,1024]{1,0:T(8,128)} %slice_select_fusion), channel_id=1, source_target_pairs={{0,0},{16,17},{32,34},{48,51},{64,68},{80,85},{96,102},{112,119},{... | collective-permute-start | bytes 1572872 | tf_op jit(solution)/shard_map/ppermute | solution.py:117
  387.7 32.1 %collective-permute-start.18 = (f32[128,1024]{1,0:T(8,128)S(1)}, f32[128,1024]{1,0:T(8,128)S(1)}, u32[]{:S(2)}, u32[]{:S(2)}) collective-permute-start(f32[128,1024]{1,0:T(8,128)S(1)} %get-tuple-element.26), channel_id=1, source_target_pairs={{0,96},{16,112},{32,0},{48,16},{64,32},{80,48},{96,64},{112,80},{1... | collective-permute-start | bytes 1572872 | tf_op jit(solution)/shard_map/ppermute | solution.py:122
  396.6 23.2 %collective-permute-start.17 = (f32[128,1024]{1,0:T(8,128)S(1)}, f32[128,1024]{1,0:T(8,128)S(1)}, u32[]{:S(2)}, u32[]{:S(2)}) collective-permute-start(f32[128,1024]{1,0:T(8,128)S(1)} %get-tuple-element.26), channel_id=1, source_target_pairs={{0,64},{16,80},{32,96},{48,112},{64,0},{80,16},{96,32},{112,48},{1... | collective-permute-start | bytes 1572872 | tf_op jit(solution)/shard_map/ppermute | solution.py:122
  396.6 26.6 %collective-permute-start.16 = (f32[128,1024]{1,0:T(8,128)S(1)}, f32[128,1024]{1,0:T(8,128)S(1)}, u32[]{:S(2)}, u32[]{:S(2)}) collective-permute-start(f32[128,1024]{1,0:T(8,128)S(1)} %get-tuple-element.26), channel_id=1, source_target_pairs={{0,32},{16,48},{32,64},{48,80},{64,96},{80,112},{96,0},{112,16},{1... | collective-permute-start | bytes 1572872 | tf_op jit(solution)/shard_map/ppermute | solution.py:122
  423.2 0.8 copy-start.3
  423.5 66.0 %collective-permute-start.19 = (f32[4,128,1024]{2,1,0:T(8,128)S(1)}, f32[4,128,1024]{2,1,0:T(8,128)}, u32[]{:S(2)}, u32[]{:S(2)}) collective-permute-start(f32[4,128,1024]{2,1,0:T(8,128)S(1)} %pad_maximum_fusion), channel_id=1, source_target_pairs={{0,16},{16,0},{32,48},{48,32},{64,80},{80,64},{96,112},{112,96},{1... | collective-permute-start | bytes 6291464 | tf_op jit(solution)/shard_map/ppermute | solution.py:124
  524.2 99.6 %all-to-all-start.1 = ((f32[8,4,256,256]{3,2,1,0:T(8,128)}), f32[8,4,256,256]{3,2,1,0:T(8,128)}, u32[]{:S(2)}, u32[]{:S(2)}) async-start(f32[8,4,256,256]{3,2,1,0:T(8,128)} %fusion.23), calls=%async_computation.1 | async-start | bytes 16777216 | tf_op jit(solution)/shard_map/all_to_all | solution.py:150
  623.9 11.5 %slice-start = ((s8[8388608]{0:T(1024)(128)(4,1)}), s8[4194304]{0:T(1024)(128)(4,1)S(1)}, s32[]{:S(2)}) async-start(s8[8388608]{0:T(1024)(128)(4,1)} %bitcast.192), calls=%async_computation.4 | async-start | bytes 8388608
  629.6 5.7 slice-start.1
  635.3 5.9 copy-start.4
Sparse Core Ops, SparseCore 0:
  25.9 78.8 all-gather.4
  351.1 89.8 all-gather.6
